TPU v7x, 32 devices: a whole 2x2x4 slice. The times are simulated.
32 devices in a mesh: dp: 4 (over y, x), ctx: 8 (over z, core).
Axes of the slice: x: 2, y: 2, z: 4, core: 2. Of those that a mesh axis runs over, the one named last changes fastest.
Arguments:
- queries: bfloat16 [4, 1024, 4096], P('dp', 'ctx'), may hold values from -6 to 6
- keys: bfloat16 [4, 8192, 128], P('dp', 'ctx'), may hold values from -6 to 6
- head_weights: bfloat16 [4, 1024, 32], P('dp', 'ctx'), may hold values from -6 to 6
- block_ids: int32 [4, 16, 32], P('dp', 'ctx'), may hold values from -1 to 127, as said below
- target_mass: bfloat16 [4, 1024, 2048], P('dp', 'ctx'), may hold values from 0.0099487305 to 10
- key_gain: float32 [128], replicated, may hold values from 0.5 to 1.5
- key_bias: float32 [128], replicated, may hold values from -1.8 to 1.8
Outputs:
- seq_loss: float32 [4], P('dp')
- grad_queries: float32 [4, 1024, 4096], P('dp', 'ctx')
- grad_head_weights: float32 [4, 1024, 32], P('dp', 'ctx')
- grad_keys: float32 [4, 8192, 128], P('dp', 'ctx')
- grad_gain: float32 [128], replicated
- grad_bias: float32 [128], replicated
Inputs may be any that keep to these rules, and one draw needn't show every extreme that they name: `block_ids`: query block b of a sequence lies in the last 2 key blocks of the positions of index b // 2 of ctx. Its slots list distinct block ids, none after its own block; the first two are its own block and the block before it; filled slots come first and -1 marks the empty rest. The 2 query blocks of one index of ctx list at most 4 blocks that lie in the positions of any one index of ctx, and exactly 3 of their own index.
All inputs are finite; a program needn't handle non-finite values.
Results may differ from a plain program's by a relative error of at most 0.00115.
The roundings to bfloat16 on the way count: a program that leaves them out, or rounds other values in their place, can miss the bound.
Values may be sent and summed in bfloat16 or wider, within the bound.
No kernel may reach another device: no remote copies, remote signals or barrier semaphores. Data moves between devices by JAX's collectives and lax.ppermute only.
A program may use at most 64 MiB of HBM per device.

v0:
```python
import jax
import jax.numpy as jnp
from jax import lax
from jax.sharding import PartitionSpec as P

H = 32
DH = 128
BS = 64
NSEL = 32
QD = 128
KD = 1024


epsilon = 1e-06
soft_cap = 20.0


def key_norm(key_rows, key_gain, key_bias):
    key_float = key_rows.astype(jnp.float32)
    key_mean = jnp.mean(key_float, -1, keepdims=True)
    centered = key_float - key_mean
    key_var = jnp.mean(centered * centered, -1, keepdims=True)
    key_scale = lax.rsqrt(key_var + epsilon)
    key_hat = centered * key_scale
    normed_keys = (key_hat * key_gain + key_bias).astype(jnp.bfloat16)
    return (key_hat, key_scale, normed_keys)


def query_norm(query_rows):
    query_float = query_rows.astype(jnp.float32).reshape(query_rows.shape[0], H, DH)
    query_scale = lax.rsqrt(jnp.mean(query_float * query_float, -1, keepdims=True) + epsilon)
    query_hat = query_float * query_scale
    return (query_hat, query_scale, query_hat.astype(jnp.bfloat16))


def score_block(normed_queries, weight_rows, mass_rows, query_pos, slot_keys, slot_pos, slot_live):
    inv_root = DH ** (-0.5)
    scores = (
        jnp.einsum("thd,jd->thj", normed_queries, slot_keys, preferred_element_type=jnp.float32)
        * inv_root
    )
    activated = jax.nn.softplus(scores)
    mixture = jnp.sum(weight_rows[:, :, None] * activated, 1)
    squashed = jnp.tanh(mixture / soft_cap)
    logits = soft_cap * squashed
    is_valid = slot_live[None, :] & (slot_pos[None, :] <= query_pos[:, None])
    exp_terms = jnp.where(is_valid, jnp.exp(logits - soft_cap), 0.0)
    denominator = jnp.sum(exp_terms, 1, keepdims=True)
    log_prob = logits - soft_cap - jnp.log(denominator)
    kept_mass = jnp.where(is_valid, mass_rows, 0.0)
    target = kept_mass / jnp.sum(kept_mass, 1, keepdims=True)
    divergence = jnp.sum(
        jnp.where(is_valid, target * (jnp.log(jnp.where(is_valid, target, 1.0)) - log_prob), 0.0)
    )
    mix_grad = (exp_terms / denominator - target) * (1.0 - squashed * squashed)
    score_grad = (mix_grad[:, None, :] * weight_rows[:, :, None] * jax.nn.sigmoid(scores)).astype(
        jnp.bfloat16
    )
    weight_grad = jnp.sum(mix_grad[:, None, :] * activated, 2)
    query_grad = (
        jnp.einsum("thj,jd->thd", score_grad, slot_keys, preferred_element_type=jnp.float32)
        * inv_root
    )
    slot_grad = (
        jnp.einsum("thj,thd->jd", score_grad, normed_queries, preferred_element_type=jnp.float32)
        * inv_root
    )
    return (divergence, query_grad, weight_grad, slot_grad)


def per_device(queries, keys, head_weights, block_ids, target_mass, key_gain, key_bias):
    ctx_count = lax.axis_size("ctx")
    ctx_index = lax.axis_index("ctx")
    key_count = KD // BS
    query_count = QD // BS
    capacity = 2 * query_count
    request_count = query_count * NSEL
    slot_count = NSEL * BS
    key_hat, key_scale, normed_keys = key_norm(keys[0], key_gain, key_bias)
    listed_ids = block_ids[0].reshape(request_count)
    is_listed = listed_ids >= 0
    block_safe = jnp.maximum(listed_ids, 0)
    owner_index = block_safe // key_count
    local_block = block_safe % key_count
    owner_hits = (
        (owner_index[:, None] == jnp.arange(ctx_count, dtype=jnp.int32)[None, :])
        & is_listed[:, None]
    ).astype(jnp.int32)
    earlier = jnp.cumsum(owner_hits, 0) - owner_hits
    rank_slot = jnp.sum(earlier * owner_hits, 1)
    target_slot = jnp.where(is_listed, owner_index * capacity + rank_slot, 0)
    placement = (
        target_slot[:, None] == jnp.arange(ctx_count * capacity, dtype=jnp.int32)[None, :]
    ) & is_listed[:, None]
    request_table = jnp.sum(jnp.where(placement, local_block[:, None] + 1, 0), 0) - 1
    request_table = request_table.reshape(ctx_count, capacity)
    initial_slots = jnp.zeros((request_count, BS, DH), jnp.bfloat16)
    shard_rows = lax.all_gather(normed_keys, "ctx", axis=0, tiled=True)
    block_rows = shard_rows.shape[0] // BS
    relative = block_safe * BS
    inside = is_listed & (relative >= 0) & (relative < shard_rows.shape[0])
    picked = shard_rows.reshape(block_rows, BS, DH)[jnp.clip(relative // BS, 0, block_rows - 1)]
    slot_keys = jnp.where(inside[:, None, None], picked, initial_slots)
    slot_keys = slot_keys.reshape(query_count, slot_count, DH)
    slot_positions = (block_safe[:, None] * BS + jnp.arange(BS, dtype=jnp.int32)[None, :]).reshape(
        query_count, slot_count
    )
    slot_lives = jnp.repeat(is_listed, BS).reshape(query_count, slot_count)
    query_hat, query_scale, normed_queries = query_norm(queries[0])
    group_count = QD // 16
    first_pos = ctx_index * KD + KD - QD

    def group_step(carried, scanned):
        grad_slots, divergence_total = carried
        group, query_group, weight_group, mass_group = scanned
        block_index = group * 16 // BS
        group_keys = lax.dynamic_index_in_dim(slot_keys, block_index, 0, keepdims=False)
        group_pos = lax.dynamic_index_in_dim(slot_positions, block_index, 0, keepdims=False)
        group_live = lax.dynamic_index_in_dim(slot_lives, block_index, 0, keepdims=False)
        query_pos = first_pos + group * 16 + jnp.arange(16, dtype=jnp.int32)
        divergence, query_grad, weight_grad, slot_grad = score_block(
            query_group, weight_group, mass_group, query_pos, group_keys, group_pos, group_live
        )
        updated = lax.dynamic_index_in_dim(grad_slots, block_index, 0, keepdims=False) + slot_grad
        grad_slots = lax.dynamic_update_index_in_dim(grad_slots, updated, block_index, 0)
        return ((grad_slots, divergence_total + divergence), (query_grad, weight_grad))

    scanned = (
        jnp.arange(group_count, dtype=jnp.int32),
        normed_queries.reshape(group_count, 16, H, DH),
        head_weights[0].astype(jnp.float32).reshape(group_count, 16, H),
        target_mass[0].astype(jnp.float32).reshape(group_count, 16, slot_count),
    )
    initial = (jnp.zeros((query_count, slot_count, DH), jnp.float32), jnp.zeros((), jnp.float32))
    (grad_slots, divergence_total), (query_grads, weight_grads) = lax.scan(
        group_step, initial, scanned
    )
    query_grads = query_grads.reshape(QD, H, DH)
    grad_query_rows = (
        query_grads - query_hat * jnp.mean(query_grads * query_hat, -1, keepdims=True)
    ) * query_scale
    slot_flat = grad_slots.reshape(request_count, BS * DH)
    outbound = jnp.dot(placement.T.astype(jnp.float32), slot_flat, precision=lax.Precision.HIGHEST)
    returned, asked_back = (
        lax.all_to_all(
            outbound.reshape(ctx_count, capacity, BS * DH),
            "ctx",
            split_axis=0,
            concat_axis=0,
            tiled=True,
        ),
        lax.all_to_all(request_table, "ctx", split_axis=0, concat_axis=0, tiled=True),
    )
    own_rows = (
        asked_back.reshape(ctx_count * capacity)[None, :]
        == jnp.arange(key_count, dtype=jnp.int32)[:, None]
    ).astype(jnp.float32)
    key_grad = jnp.dot(
        own_rows, returned.reshape(ctx_count * capacity, BS * DH), precision=lax.Precision.HIGHEST
    ).reshape(KD, DH)
    gain_part = jnp.sum(key_grad * key_hat, 0)
    bias_part = jnp.sum(key_grad, 0)
    scaled_grad = key_grad * key_gain
    grad_key_rows = (
        scaled_grad
        - jnp.mean(scaled_grad, -1, keepdims=True)
        - key_hat * jnp.mean(scaled_grad * key_hat, -1, keepdims=True)
    ) * key_scale
    loss_total = lax.psum(divergence_total, "ctx")
    grad_gain, grad_bias = lax.psum((gain_part, bias_part), ("dp", "ctx"))
    seq_loss = jnp.reshape(loss_total / (QD * ctx_count), (1,))
    return (
        seq_loss,
        grad_query_rows.reshape(1, QD, H * DH),
        weight_grads.reshape(1, QD, H),
        grad_key_rows.reshape(1, KD, DH),
        grad_gain,
        grad_bias,
    )


def solution(mesh):
    in_specs = (
        P("dp", "ctx", None),
        P("dp", "ctx", None),
        P("dp", "ctx", None),
        P("dp", "ctx", None),
        P("dp", "ctx", None),
        P(),
        P(),
    )
    out_specs = (
        P("dp"),
        P("dp", "ctx", None),
        P("dp", "ctx", None),
        P("dp", "ctx", None),
        P(),
        P(),
    )
    return jax.shard_map(
        per_device, mesh=mesh, in_specs=in_specs, out_specs=out_specs, check_vma=False
    )
```

profile of v0, /device:TPU:0, one launch (start us, length us, event | category | flops | bytes accessed | tf_op | source)
XLA Modules:
  0.0 323.6 jit_solution(10738619323609780362)
XLA Ops:
  15.4 6.3 %all-to-all-start = ((s32[8,1,4]{2,1,0:T(1,128)}), s32[8,1,4]{2,1,0:T(1,128)S(1)}, u32[]{:S(2)}, u32[]{:S(2)}) async-start(s32[8,1,4]{2,1,0:T(1,128)} %bitcast.24), calls=%async_computation | async-start | bytes 8192 | tf_op jit(solution)/shard_map/all_to_all | solution.py:152
  31.1 12.7 %all-gather.2.cloned.1.call-done = bf16[8192,128]{1,0:T(8,128)(2,1)} async-done(((bf16[1024,128]{1,0:T(8,128)(2,1)}), bf16[8192,128]{1,0:T(8,128)(2,1)}) %all-gather.2.cloned.1.call-update) | async-done | bytes 2097168 | tf_op jit(solution)/shard_map/all_gather | solution.py:98
  48.8 168.0 %while.18 = (s32[]{:T(128)}, f32[2,2048,128]{2,1,0:T(8,128)}, f32[]{:T(128)}, f32[8,16,32,128]{3,2,1,0:T(8,128)}, f32[8,16,32]{2,1,0:T(8,128)S(1)}, /*index=5*/s...) while((s32[]{:T(128)}, f32[2,2048,128]{2,1,0:T(8,128)}, ...), condition=%wide.region_9.10_spmd, body=%wide.region_3.9_spmd.sunk | while | flops 844463616 | bytes 42798204 | solution.py:135
  51.9 3.2 multiply_reduce_fusion.6
  58.1 5.8 %multiply_reduce_fusion.7 = (f32[16,32]{1,0:T(8,128)S(1)}, bf16[16,32,2048]{2,1,0:T(8,128)(2,1)S(1)}) fusion(f32[16,2048]{1,0:T(8,128)S(1)} %get-tuple-element.335, f32[16,32,2048]{2,1,0:T(8,128)} %copy-done, u16[32,2048]{1,0:T(8,128)(2,1)S(1)} %get-tuple-element.332, f32[16,32]{1,0:T(8,128)S(1)} %dynamic-slice_bitcast_fusion.2), kind=kLoop, calls=%fused_computation.3.clone.1 | loop fusion | flops 18873856 | bytes 6557696 | tf_op jit(solution)/shard_map/while/body/eval_jaxpr/reduce_sum | solution.py:59
  65.1 2.6 fusion.70
  72.9 3.2 multiply_reduce_fusion.6
  79.1 5.8 %multiply_reduce_fusion.7 = (f32[16,32]{1,0:T(8,128)S(1)}, bf16[16,32,2048]{2,1,0:T(8,128)(2,1)S(1)}) fusion(f32[16,2048]{1,0:T(8,128)S(1)} %get-tuple-element.335, f32[16,32,2048]{2,1,0:T(8,128)} %copy-done, u16[32,2048]{1,0:T(8,128)(2,1)S(1)} %get-tuple-element.332, f32[16,32]{1,0:T(8,128)S(1)} %dynamic-slice_bitcast_fusion.2), kind=kLoop, calls=%fused_computation.3.clone.1 | loop fusion | flops 18873856 | bytes 6557696 | tf_op jit(solution)/shard_map/while/body/eval_jaxpr/reduce_sum | solution.py:59
  86.1 2.6 fusion.70
  93.9 3.2 multiply_reduce_fusion.6
  100.1 5.8 %multiply_reduce_fusion.7 = (f32[16,32]{1,0:T(8,128)S(1)}, bf16[16,32,2048]{2,1,0:T(8,128)(2,1)S(1)}) fusion(f32[16,2048]{1,0:T(8,128)S(1)} %get-tuple-element.335, f32[16,32,2048]{2,1,0:T(8,128)} %copy-done, u16[32,2048]{1,0:T(8,128)(2,1)S(1)} %get-tuple-element.332, f32[16,32]{1,0:T(8,128)S(1)} %dynamic-slice_bitcast_fusion.2), kind=kLoop, calls=%fused_computation.3.clone.1 | loop fusion | flops 18873856 | bytes 6557696 | tf_op jit(solution)/shard_map/while/body/eval_jaxpr/reduce_sum | solution.py:59
  107.1 2.6 fusion.70
  114.9 3.2 multiply_reduce_fusion.6
  121.1 5.8 %multiply_reduce_fusion.7 = (f32[16,32]{1,0:T(8,128)S(1)}, bf16[16,32,2048]{2,1,0:T(8,128)(2,1)S(1)}) fusion(f32[16,2048]{1,0:T(8,128)S(1)} %get-tuple-element.335, f32[16,32,2048]{2,1,0:T(8,128)} %copy-done, u16[32,2048]{1,0:T(8,128)(2,1)S(1)} %get-tuple-element.332, f32[16,32]{1,0:T(8,128)S(1)} %dynamic-slice_bitcast_fusion.2), kind=kLoop, calls=%fused_computation.3.clone.1 | loop fusion | flops 18873856 | bytes 6557696 | tf_op jit(solution)/shard_map/while/body/eval_jaxpr/reduce_sum | solution.py:59
  128.2 2.6 fusion.70
  135.9 3.2 multiply_reduce_fusion.6
  142.1 5.8 %multiply_reduce_fusion.7 = (f32[16,32]{1,0:T(8,128)S(1)}, bf16[16,32,2048]{2,1,0:T(8,128)(2,1)S(1)}) fusion(f32[16,2048]{1,0:T(8,128)S(1)} %get-tuple-element.335, f32[16,32,2048]{2,1,0:T(8,128)} %copy-done, u16[32,2048]{1,0:T(8,128)(2,1)S(1)} %get-tuple-element.332, f32[16,32]{1,0:T(8,128)S(1)} %dynamic-slice_bitcast_fusion.2), kind=kLoop, calls=%fused_computation.3.clone.1 | loop fusion | flops 18873856 | bytes 6557696 | tf_op jit(solution)/shard_map/while/body/eval_jaxpr/reduce_sum | solution.py:59
  149.2 2.6 fusion.70
  156.9 3.2 multiply_reduce_fusion.6
  163.1 5.8 %multiply_reduce_fusion.7 = (f32[16,32]{1,0:T(8,128)S(1)}, bf16[16,32,2048]{2,1,0:T(8,128)(2,1)S(1)}) fusion(f32[16,2048]{1,0:T(8,128)S(1)} %get-tuple-element.335, f32[16,32,2048]{2,1,0:T(8,128)} %copy-done, u16[32,2048]{1,0:T(8,128)(2,1)S(1)} %get-tuple-element.332, f32[16,32]{1,0:T(8,128)S(1)} %dynamic-slice_bitcast_fusion.2), kind=kLoop, calls=%fused_computation.3.clone.1 | loop fusion | flops 18873856 | bytes 6557696 | tf_op jit(solution)/shard_map/while/body/eval_jaxpr/reduce_sum | solution.py:59
  170.2 2.6 fusion.70
  177.9 3.2 multiply_reduce_fusion.6
  184.1 5.8 %multiply_reduce_fusion.7 = (f32[16,32]{1,0:T(8,128)S(1)}, bf16[16,32,2048]{2,1,0:T(8,128)(2,1)S(1)}) fusion(f32[16,2048]{1,0:T(8,128)S(1)} %get-tuple-element.335, f32[16,32,2048]{2,1,0:T(8,128)} %copy-done, u16[32,2048]{1,0:T(8,128)(2,1)S(1)} %get-tuple-element.332, f32[16,32]{1,0:T(8,128)S(1)} %dynamic-slice_bitcast_fusion.2), kind=kLoop, calls=%fused_computation.3.clone.1 | loop fusion | flops 18873856 | bytes 6557696 | tf_op jit(solution)/shard_map/while/body/eval_jaxpr/reduce_sum | solution.py:59
  191.1 2.6 fusion.70
  198.9 3.2 multiply_reduce_fusion.6
  205.1 5.8 %multiply_reduce_fusion.7 = (f32[16,32]{1,0:T(8,128)S(1)}, bf16[16,32,2048]{2,1,0:T(8,128)(2,1)S(1)}) fusion(f32[16,2048]{1,0:T(8,128)S(1)} %get-tuple-element.335, f32[16,32,2048]{2,1,0:T(8,128)} %copy-done, u16[32,2048]{1,0:T(8,128)(2,1)S(1)} %get-tuple-element.332, f32[16,32]{1,0:T(8,128)S(1)} %dynamic-slice_bitcast_fusion.2), kind=kLoop, calls=%fused_computation.3.clone.1 | loop fusion | flops 18873856 | bytes 6557696 | tf_op jit(solution)/shard_map/while/body/eval_jaxpr/reduce_sum | solution.py:59
  212.1 2.6 fusion.70
  220.9 4.2 %all-to-all-start.1 = ((f32[8,4,8192]{2,1,0:T(4,128)}), f32[8,4,8192]{2,1,0:T(4,128)}, u32[]{:S(2)}, u32[]{:S(2)}) async-start(f32[8,4,8192]{2,1,0:T(4,128)} %fusion.45), calls=%async_computation.1 | async-start | bytes 2097152 | tf_op jit(solution)/shard_map/all_to_all | solution.py:145
  228.6 26.5 %psum.21 = f32[]{:T(128)} all-reduce(f32[]{:T(128)} %get-tuple-element.172), channel_id=1, replica_groups=mesh['dp'=4,'ctx'=8] {'ctx'}, use_global_device_ids=true, to_apply=%region_10.11 | all-reduce | flops 1 | bytes 8 | tf_op jit(solution)/shard_map/psum | solution.py:169
  255.0 2.9 reshape.504
  264.0 4.8 %fusion.25 = f32[1,128,4096]{2,1,0:T(8,128)} fusion(f32[1,128,4096]{2,1,0:T(8,128)} %mul.289, f32[1,128,4096]{2,1,0:T(8,128)} %reshape.504, f32[1,128,4096]{2,1,0:T(8,128)} %mul.293, bf16[1,128,4096]{2,1,0:T(8,128)(2,1)S(1)} %copy-done.4), kind=kLoop, calls=%fused_computation.50 | loop fusion | flops 2621440 | bytes 9437184 | tf_op jit(solution)/shard_map/mul | solution.py:139
  271.9 42.3 %all-reduce = (f32[128]{0:T(128)}, f32[128]{0:T(128)}) all-reduce(f32[128]{0:T(128)S(1)} %get-tuple-element.196, f32[128]{0:T(128)S(1)} %get-tuple-element.199), channel_id=1, replica_groups=mesh['dp'=4,'ctx'=8] {'dp','ctx'}, use_global_device_ids=true, to_apply=%region_18.19 | all-reduce | flops 256 | bytes 2048 | tf_op jit(solution)/shard_map/psum | solution.py:170
  (198 shorter events, 103.7 us)
Async XLA Ops:
  7.2 15.8 %copy-start.3 = (bf16[1,128,4096]{2,1,0:T(8,128)(2,1)S(1)}, bf16[1,128,4096]{2,1,0:T(8,128)(2,1)}, u32[]{:S(2)}) copy-start(bf16[1,128,4096]{2,1,0:T(8,128)(2,1)} %param.9) | copy-start | bytes 3145732
  7.2 36.6 %all-gather.2.cloned.1.call-start = ((), (), s32[]{:S(2)}) async-start(), calls=%async_computation.2 | async-start | bytes 2359296 | tf_op jit(solution)/shard_map/all_gather | solution.py:98
  15.4 205.6 %all-to-all-start = ((s32[8,1,4]{2,1,0:T(1,128)}), s32[8,1,4]{2,1,0:T(1,128)S(1)}, u32[]{:S(2)}, u32[]{:S(2)}) async-start(s32[8,1,4]{2,1,0:T(1,128)} %bitcast.24), calls=%async_computation | async-start | bytes 8192 | tf_op jit(solution)/shard_map/all_to_all | solution.py:152
  25.1 1.0 copy-start.6
  25.5 5.7 %copy-start.1 = (f32[16,8,32,128]{3,2,1,0:T(8,128)}, f32[16,8,32,128]{3,2,1,0:T(8,128)S(1)}, u32[]{:S(2)}) copy-start(f32[16,8,32,128]{3,2,1,0:T(8,128)S(1)} %copy.28) | copy-start | bytes 6291460
  51.9 3.2 copy-start
  72.9 3.2 copy-start
  93.9 3.2 copy-start
  114.9 3.2 copy-start
  135.9 3.2 copy-start
  156.9 3.2 copy-start
  177.9 3.2 copy-start
  198.9 3.2 copy-start
  220.9 47.8 %all-to-all-start.1 = ((f32[8,4,8192]{2,1,0:T(4,128)}), f32[8,4,8192]{2,1,0:T(4,128)}, u32[]{:S(2)}, u32[]{:S(2)}) async-start(f32[8,4,8192]{2,1,0:T(4,128)} %fusion.45), calls=%async_computation.1 | async-start | bytes 2097152 | tf_op jit(solution)/shard_map/all_to_all | solution.py:145
  255.0 2.9 copy-start.2
  261.1 2.8 copy-start.4
  270.3 1.0 copy-start.5
  270.3 0.9 copy-start.7
Sparse Core Ops, SparseCore 0:
  11.9 31.8 all-gather.1
where the time goes:
time: 325 us; the launch traced here: 324 us
  other arithmetic  118 us (36%)
  blocking collectives  68.8 us (21%)
  matrix products  49.2 us (15%)
  local copies, waits for them, and re-layouts  36.8 us (11%)
  between operations  16.1 us (5%)
  waiting for transfers between devices  12.7 us (4%)
  loops' own time  11.2 us (3%)
  starting transfers between devices  10.6 us (3%)
    reduce_sum x8, other arithmetic, score_block(): weight_grad = jnp.sum(mix_grad[:, None, :] * activated, 2)  46.2 us
    psum x1, blocking collectives, per_device(): grad_gain, grad_bias = lax.psum((gain_part, bias_part), ('dp', 'ctx'))  42.3 us
    psum x1, blocking collectives, per_device(): loss_total = lax.psum(divergence_total, 'ctx')  26.5 us
    reduce_sum x8, other arithmetic, score_block(): mixture = jnp.sum(weight_rows[:, :, None] * activated, 1)  25.7 us
    dot_general x8, matrix products, score_block(): jnp.einsum('thj,thd->jd', score_grad, normed_queries, preferred_element_t...  21 us
    dot_general x8, matrix products, score_block(): jnp.einsum('thd,jd->thj', normed_queries, slot_keys, preferred_element_ty...  14.1 us
    reduce_sum x8, other arithmetic, score_block(): jnp.sum(jnp.where(is_valid, target * (jnp.log(jnp.where(is_valid, target,...  13.7 us
    all_gather x1, waiting for transfers between devices, per_device(): shard_rows = lax.all_gather(normed_keys, 'ctx', axis=0, tiled=True)  12.7 us
  transfers between devices with their start and end apart: 3, of which 1 were waited for; matrix products, arithmetic and copies ran while one was open for 60% of the time, Pallas kernels for 0%

commit v1 on v0

--- a/solution.py
+++ b/solution.py
@@ -1,6 +1,9 @@
+import functools
 import jax
 import jax.numpy as jnp
 from jax import lax
+from jax.experimental import pallas as pl
+from jax.experimental.pallas import tpu as pltpu
 from jax.sharding import PartitionSpec as P
 
 H = 32
@@ -10,9 +13,11 @@
 QD = 128
 KD = 1024
 
-
 epsilon = 1e-06
 soft_cap = 20.0
+
+HEAD_GROUP = 4
+CHUNK = 512
 
 
 def key_norm(key_rows, key_gain, key_bias):
@@ -33,44 +38,111 @@
     return (query_hat, query_scale, query_hat.astype(jnp.bfloat16))
 
 
-def score_block(normed_queries, weight_rows, mass_rows, query_pos, slot_keys, slot_pos, slot_live):
+def score_kernel(qr_ref, qt_ref, k_ref, kt_ref, w_ref, mass_ref, spos_ref, qpos_ref,
+                 qg_ref, wg_ref, sgt_ref, div_ref, mix_ref, mg_ref):
+    f32 = jnp.float32
     inv_root = DH ** (-0.5)
-    scores = (
-        jnp.einsum("thd,jd->thj", normed_queries, slot_keys, preferred_element_type=jnp.float32)
-        * inv_root
-    )
-    activated = jax.nn.softplus(scores)
-    mixture = jnp.sum(weight_rows[:, :, None] * activated, 1)
+    rows = HEAD_GROUP * BS
+    groups = H // HEAD_GROUP
+    slots = kt_ref.shape[1]
+    chunks = slots // CHUNK
+
+    mix_ref[...] = jnp.zeros_like(mix_ref)
+
+    def first_pass(g, carry):
+        r0 = pl.multiple_of(g * rows, rows)
+        q = qr_ref[pl.ds(r0, rows), :]
+        wcol = w_ref[pl.ds(r0, rows), :]
+        for c in range(chunks):
+            cs = slice(c * CHUNK, (c + 1) * CHUNK)
+            s = jnp.dot(q, kt_ref[:, cs], preferred_element_type=f32) * inv_root
+            sp = jnp.maximum(s, 0.0) + jnp.log1p(jnp.exp(-jnp.abs(s)))
+            ws = (wcol * sp).reshape(HEAD_GROUP, BS, CHUNK)
+            mix_ref[:, cs] += jnp.sum(ws, 0)
+        return carry
+
+    lax.fori_loop(0, groups, first_pass, 0)
+
+    mixture = mix_ref[...]
     squashed = jnp.tanh(mixture / soft_cap)
     logits = soft_cap * squashed
-    is_valid = slot_live[None, :] & (slot_pos[None, :] <= query_pos[:, None])
+    is_valid = spos_ref[...] <= qpos_ref[...]
     exp_terms = jnp.where(is_valid, jnp.exp(logits - soft_cap), 0.0)
     denominator = jnp.sum(exp_terms, 1, keepdims=True)
     log_prob = logits - soft_cap - jnp.log(denominator)
-    kept_mass = jnp.where(is_valid, mass_rows, 0.0)
+    kept_mass = jnp.where(is_valid, mass_ref[...].astype(f32), 0.0)
     target = kept_mass / jnp.sum(kept_mass, 1, keepdims=True)
-    divergence = jnp.sum(
-        jnp.where(is_valid, target * (jnp.log(jnp.where(is_valid, target, 1.0)) - log_prob), 0.0)
-    )
-    mix_grad = (exp_terms / denominator - target) * (1.0 - squashed * squashed)
-    score_grad = (mix_grad[:, None, :] * weight_rows[:, :, None] * jax.nn.sigmoid(scores)).astype(
-        jnp.bfloat16
-    )
-    weight_grad = jnp.sum(mix_grad[:, None, :] * activated, 2)
-    query_grad = (
-        jnp.einsum("thj,jd->thd", score_grad, slot_keys, preferred_element_type=jnp.float32)
-        * inv_root
-    )
-    slot_grad = (
-        jnp.einsum("thj,thd->jd", score_grad, normed_queries, preferred_element_type=jnp.float32)
-        * inv_root
-    )
-    return (divergence, query_grad, weight_grad, slot_grad)
+    div_ref[...] = jnp.sum(
+        jnp.where(is_valid, target * (jnp.log(jnp.where(is_valid, target, 1.0)) - log_prob), 0.0),
+        1, keepdims=True)
+    mg_ref[...] = (exp_terms / denominator - target) * (1.0 - squashed * squashed)
+
+    sgt_ref[...] = jnp.zeros_like(sgt_ref)
+
+    def second_pass(g, carry):
+        r0 = pl.multiple_of(g * rows, rows)
+        q = qr_ref[pl.ds(r0, rows), :]
+        qt = qt_ref[:, pl.ds(r0, rows)]
+        wcol = w_ref[pl.ds(r0, rows), :]
+        qg_acc = jnp.zeros((rows, DH), f32)
+        wg_acc = jnp.zeros((rows, 1), f32)
+        for c in range(chunks):
+            cs = slice(c * CHUNK, (c + 1) * CHUNK)
+            s = jnp.dot(q, kt_ref[:, cs], preferred_element_type=f32) * inv_root
+            e = jnp.exp(-jnp.abs(s))
+            sp = jnp.maximum(s, 0.0) + jnp.log1p(e)
+            r = 1.0 / (1.0 + e)
+            sig = jnp.where(s >= 0.0, r, e * r)
+            mgc = mg_ref[:, cs]
+            mg4 = jnp.broadcast_to(mgc[None], (HEAD_GROUP, BS, CHUNK)).reshape(rows, CHUNK)
+            sg = (mg4 * wcol * sig).astype(jnp.bfloat16)
+            wg_acc = wg_acc + jnp.sum(mg4 * sp, 1, keepdims=True)
+            qg_acc = qg_acc + jnp.dot(sg, k_ref[cs, :], preferred_element_type=f32)
+            sgt_ref[:, cs] += jnp.dot(qt, sg, preferred_element_type=f32)
+        qg_ref[pl.ds(r0, rows), :] = qg_acc * inv_root
+        wg_ref[pl.ds(r0, rows), :] = wg_acc
+        return carry
+
+    lax.fori_loop(0, groups, second_pass, 0)
+    sgt_ref[...] = sgt_ref[...] * inv_root
+
+
+def score_blocks(qr, qt, k, kt, wcol, mass, spos, qpos):
+    nblk, nrows, _ = qr.shape
+    slots = k.shape[1]
+    f32 = jnp.float32
+
+    def blk(*shape):
+        return pl.BlockSpec((None,) + shape, lambda b: (b,) + (0,) * len(shape))
+
+    flops = nblk * (4 * 2 * nrows * slots * DH)
+    return pl.pallas_call(
+        score_kernel,
+        grid=(nblk,),
+        in_specs=[
+            blk(nrows, DH), blk(DH, nrows), blk(slots, DH), blk(DH, slots),
+            blk(nrows, 1), blk(BS, slots), blk(1, slots), blk(BS, 1),
+        ],
+        out_specs=[blk(nrows, DH), blk(nrows, 1), blk(DH, slots), blk(BS, 1)],
+        out_shape=[
+            jax.ShapeDtypeStruct((nblk, nrows, DH), f32),
+            jax.ShapeDtypeStruct((nblk, nrows, 1), f32),
+            jax.ShapeDtypeStruct((nblk, DH, slots), f32),
+            jax.ShapeDtypeStruct((nblk, BS, 1), f32),
+        ],
+        scratch_shapes=[pltpu.VMEM((BS, slots), f32), pltpu.VMEM((BS, slots), f32)],
+        compiler_params=pltpu.CompilerParams(dimension_semantics=("arbitrary",)),
+        cost_estimate=pl.CostEstimate(
+            flops=flops, transcendentals=nblk * nrows * slots * 5,
+            bytes_accessed=nblk * (nrows * DH * 4 + slots * DH * 4 + nrows * DH * 4 + DH * slots * 4)),
+    )(qr, qt, k, kt, wcol, mass, spos, qpos)
 
 
 def per_device(queries, keys, head_weights, block_ids, target_mass, key_gain, key_bias):
     ctx_count = lax.axis_size("ctx")
     ctx_index = lax.axis_index("ctx")
+    dp_count = lax.axis_size("dp")
+    dp_index = lax.axis_index("dp")
     key_count = KD // BS
     query_count = QD // BS
     capacity = 2 * query_count
@@ -106,36 +178,30 @@
         query_count, slot_count
     )
     slot_lives = jnp.repeat(is_listed, BS).reshape(query_count, slot_count)
+    never = jnp.iinfo(jnp.int32).max
+    slot_limit = jnp.where(slot_lives, slot_positions, never).reshape(query_count, 1, slot_count)
     query_hat, query_scale, normed_queries = query_norm(queries[0])
-    group_count = QD // 16
     first_pos = ctx_index * KD + KD - QD
-
-    def group_step(carried, scanned):
-        grad_slots, divergence_total = carried
-        group, query_group, weight_group, mass_group = scanned
-        block_index = group * 16 // BS
-        group_keys = lax.dynamic_index_in_dim(slot_keys, block_index, 0, keepdims=False)
-        group_pos = lax.dynamic_index_in_dim(slot_positions, block_index, 0, keepdims=False)
-        group_live = lax.dynamic_index_in_dim(slot_lives, block_index, 0, keepdims=False)
-        query_pos = first_pos + group * 16 + jnp.arange(16, dtype=jnp.int32)
-        divergence, query_grad, weight_grad, slot_grad = score_block(
-            query_group, weight_group, mass_group, query_pos, group_keys, group_pos, group_live
-        )
-        updated = lax.dynamic_index_in_dim(grad_slots, block_index, 0, keepdims=False) + slot_grad
-        grad_slots = lax.dynamic_update_index_in_dim(grad_slots, updated, block_index, 0)
-        return ((grad_slots, divergence_total + divergence), (query_grad, weight_grad))
-
-    scanned = (
-        jnp.arange(group_count, dtype=jnp.int32),
-        normed_queries.reshape(group_count, 16, H, DH),
-        head_weights[0].astype(jnp.float32).reshape(group_count, 16, H),
-        target_mass[0].astype(jnp.float32).reshape(group_count, 16, slot_count),
-    )
-    initial = (jnp.zeros((query_count, slot_count, DH), jnp.float32), jnp.zeros((), jnp.float32))
-    (grad_slots, divergence_total), (query_grads, weight_grads) = lax.scan(
-        group_step, initial, scanned
-    )
-    query_grads = query_grads.reshape(QD, H, DH)
+    query_pos = (first_pos + jnp.arange(QD, dtype=jnp.int32)).reshape(query_count, BS, 1)
+
+    head_rows = (
+        normed_queries.reshape(query_count, BS, H, DH).transpose(0, 2, 1, 3).reshape(query_count, H * BS, DH)
+    )
+    head_cols = head_rows.transpose(0, 2, 1)
+    key_cols = slot_keys.transpose(0, 2, 1)
+    weight_col = (
+        head_weights[0].astype(jnp.float32).reshape(query_count, BS, H).transpose(0, 2, 1)
+        .reshape(query_count, H * BS, 1)
+    )
+    mass_rows = target_mass[0].reshape(query_count, BS, slot_count)
+    qg_rows, wg_rows, slot_grad_t, div_rows = score_blocks(
+        head_rows, head_cols, slot_keys, key_cols, weight_col, mass_rows, slot_limit, query_pos
+    )
+    divergence_total = jnp.sum(div_rows)
+    query_grads = qg_rows.reshape(query_count, H, BS, DH).transpose(0, 2, 1, 3).reshape(QD, H, DH)
+    weight_grads = wg_rows.reshape(query_count, H, BS).transpose(0, 2, 1).reshape(QD, H)
+    grad_slots = slot_grad_t.transpose(0, 2, 1)
+
     grad_query_rows = (
         query_grads - query_hat * jnp.mean(query_grads * query_hat, -1, keepdims=True)
     ) * query_scale
@@ -166,8 +232,11 @@
         - jnp.mean(scaled_grad, -1, keepdims=True)
         - key_hat * jnp.mean(scaled_grad * key_hat, -1, keepdims=True)
     ) * key_scale
-    loss_total = lax.psum(divergence_total, "ctx")
-    grad_gain, grad_bias = lax.psum((gain_part, bias_part), ("dp", "ctx"))
+    loss_slots = jnp.where(jnp.arange(dp_count) == dp_index, divergence_total, 0.0)
+    packed = lax.psum(jnp.concatenate([gain_part, bias_part, loss_slots]), ("dp", "ctx"))
+    grad_gain = packed[:DH]
+    grad_bias = packed[DH:2 * DH]
+    loss_total = lax.dynamic_index_in_dim(packed, 2 * DH + dp_index, 0, keepdims=False)
     seq_loss = jnp.reshape(loss_total / (QD * ctx_count), (1,))
     return (
         seq_loss,

time: 325 us -> 225 us (0.69)
  other arithmetic: 118 us -> 27.6 us
  Pallas kernels: 0 us -> 73.1 us
  matrix products: 49.2 us -> 4.28 us
  blocking collectives: 68.8 us -> 40.5 us
  loops' own time: 11.2 us -> 0 us
  local copies, waits for them, and re-layouts: 36.8 us -> 41.5 us
    reduce_sum x33 -> x2, other arithmetic: 95.2 us -> 1.26 us  [the longest x1 0.64 us: per_device(): jnp.mean(scaled_grad * key_hat, -1, keepdims=True)]
    pallas_call x0 -> x1, Pallas kernels: none -> 73.1 us  [score_blocks(): pl.pallas_call(score_kernel, grid=(nblk,), in_specs=[blk(nrows, DH), blk(...]
    dot_general x24 -> x0, matrix products: 46.5 us -> none  [the longest x8 21 us: score_block(): jnp.einsum('thj,thd->jd', score_grad, normed_queries, preferred_element_t...]
    psum x2 -> x1, blocking collectives: 68.8 us -> 40.5 us  [per_device(): lax.psum(jnp.concatenate([gain_part, bias_part, loss_slots]), ('dp', 'ctx'))]
    dynamic_slice x32 -> x1, local copies, waits for them, and re-layouts: 15.5 us -> 0.58 us  [per_device(): lax.dynamic_index_in_dim(packed, 2 * DH + dp_index, 0, keepdims=False)]
    another operation x1 -> x0, loops' own time: 11.2 us -> none  [per_device(): lax.scan(group_step, initial, scanned)]
    reshape x1 -> x7, local copies, waits for them, and re-layouts: 2.92 us -> 12.8 us  [the longest x2 6.89 us: per_device(): qg_rows.reshape(query_count, H, BS, DH).transpose(0, 2, 1, 3)]
    transpose x0 -> x3, local copies, waits for them, and re-layouts: none -> 4.32 us  [the longest x1 2.88 us: per_device(): grad_slots = slot_grad_t.transpose(0, 2, 1)]
  transfers between devices with their start and end apart: 3 -> 3, of which waited for: 1 -> 1; matrix products, arithmetic and copies ran while one was open for 60% -> 28% of each run, Pallas kernels for 0% -> 33%
where the time goes in v1:
time: 225 us; the launch traced here: 224 us
  Pallas kernels  73.1 us (32%)
  local copies, waits for them, and re-layouts  41.5 us (18%)
  blocking collectives  40.5 us (18%)
  other arithmetic  27.6 us (12%)
  between operations  16.1 us (7%)
  starting transfers between devices  10.8 us (5%)
  waiting for transfers between devices  10.2 us (5%)
  matrix products  4.28 us (2%)
    pallas_call x1, Pallas kernels, score_blocks(): pl.pallas_call(score_kernel, grid=(nblk,), in_specs=[blk(nrows, DH), blk(...  73.1 us
    psum x1, blocking collectives, per_device(): lax.psum(jnp.concatenate([gain_part, bias_part, loss_slots]), ('dp', 'ctx'))  40.5 us
    all_gather x1, waiting for transfers between devices, per_device(): shard_rows = lax.all_gather(normed_keys, 'ctx', axis=0, tiled=True)  10.1 us
    reshape x2, local copies, waits for them, and re-layouts, per_device(): qg_rows.reshape(query_count, H, BS, DH).transpose(0, 2, 1, 3)  6.89 us
    all_to_all x1, starting transfers between devices, per_device(): lax.all_to_all(request_table, 'ctx', split_axis=0, concat_axis=0, tiled=T...  6.33 us
    gather x2, local copies, waits for them, and re-layouts, per_device(): shard_rows.reshape(block_rows, BS, DH)  5.54 us
    mul x2, local copies, waits for them, and re-layouts, query_norm(): query_hat = query_float * query_scale  4.71 us
  transfers between devices with their start and end apart: 3, of which 1 were waited for; matrix products, arithmetic and copies ran while one was open for 28% of the time, Pallas kernels for 33%

profile of v1, /device:TPU:0, one launch (start us, length us, event | category | flops | bytes accessed | tf_op | source)
XLA Modules:
  0.0 224.1 jit_solution(1491783544073201192)
XLA Ops:
  7.2 1.2 convert_reduce_fusion
  8.4 1.3 fusion.16
  9.7 2.0 fusion.13
  12.5 0.7 compare_and_fusion.1
  15.4 6.3 %all-to-all-start = ((s32[8,1,4]{2,1,0:T(1,128)}), s32[8,1,4]{2,1,0:T(1,128)S(1)}, u32[]{:S(2)}, u32[]{:S(2)}) async-start(s32[8,1,4]{2,1,0:T(1,128)} %bitcast), calls=%async_computation | async-start | bytes 8192 | tf_op jit(solution)/shard_map/all_to_all | solution.py:218
  23.7 0.7 fusion.5
  24.4 1.4 copy.74
  25.8 2.3 %copy.75 = bf16[2,2048,128]{1,2,0:T(8,128)(2,1)} copy(bf16[2,2048,128]{2,1,0:T(8,128)(2,1)} %bitcast.87) | data formatting | bytes 2097152 | tf_op jit(solution)/shard_map/reshape | solution.py:188
  28.5 3.4 %reshape.501.w_ref = f32[2,2048,1]{2,1,0:T(8,128)} reshape(f32[2,32,64]{2,1,0:T(8,128)S(1)} %bitcast.95) | data formatting | bytes 32768 | tf_op jit(solution)/shard_map/reshape | solution.py:194
  33.7 10.1 %all-gather.2.cloned.1.call-done = bf16[8192,128]{1,0:T(8,128)(2,1)} async-done(((bf16[1024,128]{1,0:T(8,128)(2,1)}), bf16[8192,128]{1,0:T(8,128)(2,1)}) %all-gather.2.cloned.1.call-update) | async-done | bytes 2097168 | tf_op jit(solution)/shard_map/all_gather | solution.py:170
  43.9 3.3 %gather_fusion = bf16[64,64,128]{2,1,0:T(8,128)(2,1)} fusion(bf16[128,64,128]{2,1,0:T(8,128)(2,1)} %bitcast.93, s32[1024]{0:T(1024)S(1)} %pad_clamp_fusion), kind=kCustom, calls=%fused_computation | custom fusion | bytes 2097408 | tf_op jit(solution)/shard_map/gather | solution.py:174
  47.1 2.3 %copy.76 = bf16[2,2048,128]{1,2,0:T(8,128)(2,1)} copy(bf16[2,2048,128]{2,1,0:T(8,128)(2,1)} %bitcast.86) | data formatting | bytes 2097152 | tf_op jit(solution)/shard_map/gather | solution.py:174
  49.4 2.4 %broadcast_select_fusion = bf16[2,2048,128]{1,2,0:T(8,128)(2,1)} fusion(bf16[2,2048,128]{1,2,0:T(8,128)(2,1)} %copy.76, pred[2,2048]{1,0:T(4,128)(4,1)S(1)} %broadcast_in_dim.70), kind=kLoop, calls=%fused_computation.13 | loop fusion | flops 524288 | bytes 2101248 | tf_op jit(solution)/shard_map/jit(_where)/select_n | solution.py:175
  51.8 1.1 fusion.34.kt_ref
  52.8 2.3 %copy.79.k_ref = bf16[2,2048,128]{2,1,0:T(8,128)(2,1)} copy(bf16[2,2048,128]{1,2,0:T(8,128)(2,1)} %broadcast_select_fusion) | data formatting | bytes 2097152 | tf_op jit(solution)/shard_map/jit(_where)/select_n | solution.py:175
  55.2 73.1 %shard_map.118 = (f32[2,2048,128]{2,1,0:T(8,128)}, f32[2,2048,1]{2,1,0:T(8,128)}, f32[2,128,2048]{2,1,0:T(8,128)}, f32[2,64,1]{2,1,0:T(8,128)}) custom-call(bf16[2,2048,128]{2,1,0:T(8,128)(2,1)} %bitcast.88, bf16[2,128,2048]{2,1,0:T(8,128)(2,1)} %bitcast.92, bf16[2,2048,128]{2,1,0:T(8,128)(2,1)} %copy.79.k_ref, bf16[2,128,2048]{2,1,0:T(8,128)(2,1)} %fusion.34.kt_ref, ...), custom_call_target="tpu_custom_call" | custom-call | flops 8589934592 | bytes 8388608 | tf_op jit(solution)/shard_map/pallas_call | solution.py:119
  128.3 2.9 %copy.81 = f32[2,2048,128]{2,1,0:T(8,128)} copy(f32[2,2048,128]{1,2,0:T(8,128)} %bitcast.89) | data formatting | bytes 4194304 | tf_op jit(solution)/shard_map/transpose | solution.py:203
  131.2 2.7 %reshape.500 = f32[64,8192,1]{1,0,2:T(8,128)} reshape(f32[2,2048,128]{2,1,0:T(8,128)} %copy.81) | data formatting | bytes 4194304 | tf_op jit(solution)/shard_map/reshape | solution.py:208
  134.0 3.8 %fusion.24 = f32[8,4,8192]{2,1,0:T(4,128)} fusion(f32[64,8192,1]{1,0,2:T(8,128)} %reshape.500, pred[8,4,64]{2,0,1:T(8,128)(4,1)S(1)} %compare_and_fusion), kind=kOutput, calls=%fused_computation.45 | convolution fusion | flops 201326592 | bytes 3147776 | tf_op jit(solution)/shard_map/dot_general | solution.py:209
  137.8 4.4 %all-to-all-start.1 = ((f32[8,4,8192]{2,1,0:T(4,128)}), f32[8,4,8192]{2,1,0:T(4,128)}, u32[]{:S(2)}, u32[]{:S(2)}) async-start(f32[8,4,8192]{2,1,0:T(4,128)} %fusion.24), calls=%async_computation.1 | async-start | bytes 2097152 | tf_op jit(solution)/shard_map/all_to_all | solution.py:211
  142.2 1.9 mul.172
  144.1 2.8 %mul.173 = f32[1,128,4096]{2,1,0:T(8,128)} reshape(f32[128,32,128]{2,1,0:T(8,128)} %mul.172) | data formatting | bytes 4194304 | tf_op jit(solution)/shard_map/mul | solution.py:37
  148.8 4.1 %copy.97 = f32[2,32,64,128]{3,1,2,0:T(8,128)} copy(f32[2,32,64,128]{3,2,1,0:T(8,128)} %bitcast.82) | data formatting | bytes 4194304 | tf_op jit(solution)/shard_map/reshape | solution.py:201
  152.9 2.8 %reshape.483 = f32[1,128,4096]{2,1,0:T(8,128)} reshape(f32[2,64,32,128]{3,2,1,0:T(8,128)} %bitcast.85) | data formatting | bytes 4194304 | tf_op jit(solution)/shard_map/reshape | solution.py:201
  155.7 3.5 %multiply_reduce_fusion = f32[2,64,32]{2,1,0:T(8,128)S(1)} fusion(f32[2,64,32]{2,1,0:T(8,128)S(1)} %bitcast.91, f32[2,32,64,128]{3,2,1,0:T(8,128)} %bitcast.83, f32[2,64,32,128]{3,2,1,0:T(8,128)S(1)} %bitcast.81), kind=kLoop, calls=%fused_computation.10 | loop fusion | flops 1568768 | bytes 4227072 | tf_op jit(solution)/shard_map/reduce_sum | solution.py:206
  159.8 1.5 mul.177
  161.3 2.4 %reduce.3 = f32[2,2048]{1,0:T(2,128)S(1)} reduce(f32[2,2048,1]{2,1,0:T(8,128)} %get-tuple-element.13, f32[]{:T(128)} %constant.115), dimensions={2}, to_apply=%get-tuple-element.13.reduce_sub_computation | reduce | bytes 32772 | tf_op jit(solution)/shard_map/pallas_call | solution.py:119
  163.8 0.7 reshape_reshape.4
  165.2 4.1 %fusion.3 = f32[1,128,4096]{2,1,0:T(8,128)} fusion(f32[1,128,4096]{2,1,0:T(8,128)S(1)} %copy-done.2, f32[1,128,4096]{2,1,0:T(8,128)} %reshape.483, f32[1,128,4096]{2,1,0:T(8,128)} %mul.177, bf16[1,128,4096]{2,1,0:T(8,128)(2,1)S(1)} %copy-done), kind=kLoop, calls=%fused_computation.7 | loop fusion | flops 2621440 | bytes 9437184 | tf_op jit(solution)/shard_map/mul | solution.py:205
  169.2 1.6 reshape.480
  172.4 40.5 %psum.7 = f32[260]{0:T(512)S(1)} all-reduce(f32[260]{0:T(512)S(1)} %pad_maximum_fusion), channel_id=1, replica_groups=mesh['dp'=4,'ctx'=8] {'dp','ctx'}, use_global_device_ids=true, to_apply=%region_9.10 | all-reduce | flops 260 | bytes 2080 | tf_op jit(solution)/shard_map/psum | solution.py:236
  214.7 1.4 fusion.20
  (76 shorter events, 12.9 us)
Async XLA Ops:
  7.2 14.5 %copy-start = (bf16[1,128,4096]{2,1,0:T(8,128)(2,1)S(1)}, bf16[1,128,4096]{2,1,0:T(8,128)(2,1)}, u32[]{:S(2)}) copy-start(bf16[1,128,4096]{2,1,0:T(8,128)(2,1)} %param.7) | copy-start | bytes 3145732
  7.2 36.7 %all-gather.2.cloned.1.call-start = ((), (), s32[]{:S(2)}) async-start(), calls=%async_computation.2 | async-start | bytes 2359296 | tf_op jit(solution)/shard_map/all_gather | solution.py:170
  15.4 122.4 %all-to-all-start = ((s32[8,1,4]{2,1,0:T(1,128)}), s32[8,1,4]{2,1,0:T(1,128)S(1)}, u32[]{:S(2)}, u32[]{:S(2)}) async-start(s32[8,1,4]{2,1,0:T(1,128)} %bitcast), calls=%async_computation | async-start | bytes 8192 | tf_op jit(solution)/shard_map/all_to_all | solution.py:218
  24.4 4.0 %copy-start.5 = (bf16[1,128,32]{1,2,0:T(8,128)(2,1)S(1)}, bf16[1,128,32]{1,2,0:T(8,128)(2,1)}, u32[]{:S(2)}) copy-start(bf16[1,128,32]{1,2,0:T(8,128)(2,1)} %param.9) | copy-start | bytes 24580
  49.4 2.4 %copy-start.1 = (bf16[2,2048,128]{1,2,0:T(8,128)(2,1)S(1)}, bf16[2,2048,128]{1,2,0:T(8,128)(2,1)}, u32[]{:S(2)}) copy-start(bf16[2,2048,128]{1,2,0:T(8,128)(2,1)} %copy.76) | copy-start | bytes 3145732
  137.8 31.5 %all-to-all-start.1 = ((f32[8,4,8192]{2,1,0:T(4,128)}), f32[8,4,8192]{2,1,0:T(4,128)}, u32[]{:S(2)}, u32[]{:S(2)}) async-start(f32[8,4,8192]{2,1,0:T(4,128)} %fusion.24), calls=%async_computation.1 | async-start | bytes 2097152 | tf_op jit(solution)/shard_map/all_to_all | solution.py:211
  144.1 4.0 %copy-start.4 = (f32[2,64,1]{2,1,0:T(8,128)S(1)}, f32[2,64,1]{2,1,0:T(8,128)}, u32[]{:S(2)}) copy-start(f32[2,64,1]{2,1,0:T(8,128)} %get-tuple-element.11) | copy-start | bytes 1540
  161.3 3.8 %copy-start.2 = (f32[1,128,4096]{2,1,0:T(8,128)S(1)}, f32[1,128,4096]{2,1,0:T(8,128)}, u32[]{:S(2)}) copy-start(f32[1,128,4096]{2,1,0:T(8,128)} %mul.173) | copy-start | bytes 6291460
  170.8 1.0 copy-start.3
  170.8 0.9 copy-start.6
Sparse Core Ops, SparseCore 0:
  11.9 31.9 all-gather.1

commit v2 on v1

--- a/solution.py
+++ b/solution.py
@@ -233,7 +233,8 @@
         - key_hat * jnp.mean(scaled_grad * key_hat, -1, keepdims=True)
     ) * key_scale
     loss_slots = jnp.where(jnp.arange(dp_count) == dp_index, divergence_total, 0.0)
-    packed = lax.psum(jnp.concatenate([gain_part, bias_part, loss_slots]), ("dp", "ctx"))
+    packed = jnp.concatenate([gain_part, bias_part, loss_slots])
+    packed = lax.psum(jnp.pad(packed, (0, max(16384, packed.shape[0]) - packed.shape[0])), ("dp", "ctx"))
     grad_gain = packed[:DH]
     grad_bias = packed[DH:2 * DH]
     loss_total = lax.dynamic_index_in_dim(packed, 2 * DH + dp_index, 0, keepdims=False)

time: 225 us -> 305 us (1.36)
  waiting for transfers between devices: 10.2 us -> 128 us
  blocking collectives: 40.5 us -> 0 us
    psum x0 -> x1, waiting for transfers between devices: none -> 117 us  [per_device(): lax.psum(jnp.pad(packed, (0, max(16384, packed.shape[0]) - packed.shape[0...]
    psum x1 -> x0, blocking collectives: 40.5 us -> none  [per_device(): lax.psum(jnp.concatenate([gain_part, bias_part, loss_slots]), ('dp', 'ctx'))]
  transfers between devices with their start and end apart: 3 -> 4, of which waited for: 1 -> 2; matrix products, arithmetic and copies ran while one was open for 28% -> 21% of each run, Pallas kernels for 33% -> 24%
where the time goes in v2:
time: 305 us; the launch traced here: 303 us
  waiting for transfers between devices  128 us (42%)
  Pallas kernels  73.1 us (24%)
  local copies, waits for them, and re-layouts  43 us (14%)
  other arithmetic  28.2 us (9%)
  between operations  16.1 us (5%)
  starting transfers between devices  10.8 us (4%)
  matrix products  4.28 us (1%)
    psum x1, waiting for transfers between devices, per_device(): lax.psum(jnp.pad(packed, (0, max(16384, packed.shape[0]) - packed.shape[0...  117 us
    pallas_call x1, Pallas kernels, score_blocks(): pl.pallas_call(score_kernel, grid=(nblk,), in_specs=[blk(nrows, DH), blk(...  73.1 us
    all_gather x1, waiting for transfers between devices, per_device(): shard_rows = lax.all_gather(normed_keys, 'ctx', axis=0, tiled=True)  10.1 us
    reshape x2, local copies, waits for them, and re-layouts, per_device(): qg_rows.reshape(query_count, H, BS, DH).transpose(0, 2, 1, 3)  6.89 us
    all_to_all x1, starting transfers between devices, per_device(): lax.all_to_all(request_table, 'ctx', split_axis=0, concat_axis=0, tiled=T...  6.33 us
  transfers between devices with their start and end apart: 4, of which 2 were waited for; matrix products, arithmetic and copies ran while one was open for 21% of the time, Pallas kernels for 24%

profile of v2, /device:TPU:0, one launch (start us, length us, event | category | flops | bytes accessed | tf_op | source)
XLA Modules:
  0.0 303.0 jit_solution(14654959901846769686)
XLA Ops:
  7.2 1.2 convert_reduce_fusion
  8.4 1.3 fusion.16
  9.7 2.0 fusion.13
  15.4 6.3 %all-to-all-start = ((s32[8,1,4]{2,1,0:T(1,128)}), s32[8,1,4]{2,1,0:T(1,128)S(1)}, u32[]{:S(2)}, u32[]{:S(2)}) async-start(s32[8,1,4]{2,1,0:T(1,128)} %bitcast), calls=%async_computation | async-start | bytes 8192 | tf_op jit(solution)/shard_map/all_to_all | solution.py:218
  23.7 0.7 fusion.5
  24.4 1.4 copy.74
  25.8 2.3 copy.75
  28.5 3.4 %reshape.501.w_ref = f32[2,2048,1]{2,1,0:T(8,128)} reshape(f32[2,32,64]{2,1,0:T(8,128)S(1)} %bitcast.95) | data formatting | bytes 32768 | tf_op jit(solution)/shard_map/reshape | solution.py:194
  33.7 10.1 %all-gather.2.cloned.1.call-done = bf16[8192,128]{1,0:T(8,128)(2,1)} async-done(((bf16[1024,128]{1,0:T(8,128)(2,1)}), bf16[8192,128]{1,0:T(8,128)(2,1)}) %all-gather.2.cloned.1.call-update) | async-done | bytes 2097168 | tf_op jit(solution)/shard_map/all_gather | solution.py:170
  43.9 3.3 %gather_fusion = bf16[64,64,128]{2,1,0:T(8,128)(2,1)} fusion(bf16[128,64,128]{2,1,0:T(8,128)(2,1)} %bitcast.93, s32[1024]{0:T(1024)S(1)} %pad_clamp_fusion), kind=kCustom, calls=%fused_computation | custom fusion | bytes 2097408 | tf_op jit(solution)/shard_map/gather | solution.py:174
  47.1 2.3 copy.76
  49.4 2.4 broadcast_select_fusion
  51.8 1.1 fusion.34.kt_ref
  52.8 2.3 copy.79.k_ref
  55.2 73.1 %shard_map.118 = (f32[2,2048,128]{2,1,0:T(8,128)}, f32[2,2048,1]{2,1,0:T(8,128)}, f32[2,128,2048]{2,1,0:T(8,128)}, f32[2,64,1]{2,1,0:T(8,128)}) custom-call(bf16[2,2048,128]{2,1,0:T(8,128)(2,1)} %bitcast.88, bf16[2,128,2048]{2,1,0:T(8,128)(2,1)} %bitcast.92, bf16[2,2048,128]{2,1,0:T(8,128)(2,1)} %copy.79.k_ref, bf16[2,128,2048]{2,1,0:T(8,128)(2,1)} %fusion.34.kt_ref, ...), custom_call_target="tpu_custom_call" | custom-call | flops 8589934592 | bytes 8388608 | tf_op jit(solution)/shard_map/pallas_call | solution.py:119
  128.3 2.9 copy.81
  131.2 2.7 reshape.500
  133.9 3.8 %fusion.24 = f32[8,4,8192]{2,1,0:T(4,128)} fusion(f32[64,8192,1]{1,0,2:T(8,128)} %reshape.500, pred[8,4,64]{2,0,1:T(8,128)(4,1)S(1)} %compare_and_fusion), kind=kOutput, calls=%fused_computation.48 | convolution fusion | flops 201326592 | bytes 3147776 | tf_op jit(solution)/shard_map/dot_general | solution.py:209
  137.8 4.2 %all-to-all-start.1 = ((f32[8,4,8192]{2,1,0:T(4,128)}), f32[8,4,8192]{2,1,0:T(4,128)}, u32[]{:S(2)}, u32[]{:S(2)}) async-start(f32[8,4,8192]{2,1,0:T(4,128)} %fusion.24), calls=%async_computation.1 | async-start | bytes 2097152 | tf_op jit(solution)/shard_map/all_to_all | solution.py:211
  142.2 1.9 mul.172
  144.2 2.8 mul.173
  148.8 4.1 %copy.97 = f32[2,32,64,128]{3,1,2,0:T(8,128)} copy(f32[2,32,64,128]{3,2,1,0:T(8,128)} %bitcast.82) | data formatting | bytes 4194304 | tf_op jit(solution)/shard_map/reshape | solution.py:201
  153.0 2.8 reshape.483
  155.7 3.5 %multiply_reduce_fusion = f32[2,64,32]{2,1,0:T(8,128)S(1)} fusion(f32[2,64,32]{2,1,0:T(8,128)S(1)} %bitcast.91, f32[2,32,64,128]{3,2,1,0:T(8,128)} %bitcast.83, f32[2,64,32,128]{3,2,1,0:T(8,128)S(1)} %bitcast.81), kind=kLoop, calls=%fused_computation.10 | loop fusion | flops 1568768 | bytes 4227072 | tf_op jit(solution)/shard_map/reduce_sum | solution.py:206
  159.8 1.5 mul.177
  161.4 2.4 reduce.3
  165.2 4.1 %fusion.3 = f32[1,128,4096]{2,1,0:T(8,128)} fusion(f32[1,128,4096]{2,1,0:T(8,128)S(1)} %copy-done.2, f32[1,128,4096]{2,1,0:T(8,128)} %reshape.483, f32[1,128,4096]{2,1,0:T(8,128)} %mul.177, bf16[1,128,4096]{2,1,0:T(8,128)(2,1)S(1)} %copy-done), kind=kLoop, calls=%fused_computation.7 | loop fusion | flops 2621440 | bytes 9437184 | tf_op jit(solution)/shard_map/mul | solution.py:205
  169.3 1.6 reshape.480
  173.1 1.4 fusion.20
  174.5 117.3 %all-reduce.3.cloned.1.call-done = f32[16384]{0:T(1024)} async-done(((f32[16384]{0:T(1024)}), f32[16384]{0:T(1024)}) %all-reduce.3.cloned.1.call-update) | async-done | bytes 65552 | tf_op jit(solution)/shard_map/psum | solution.py:237
  291.9 1.3 dynamic_slice.4
  293.8 1.3 fusion.31
  (78 shorter events, 14.1 us)
Async XLA Ops:
  7.2 14.5 %copy-start = (bf16[1,128,4096]{2,1,0:T(8,128)(2,1)S(1)}, bf16[1,128,4096]{2,1,0:T(8,128)(2,1)}, u32[]{:S(2)}) copy-start(bf16[1,128,4096]{2,1,0:T(8,128)(2,1)} %param.7) | copy-start | bytes 3145732
  7.2 36.7 %all-gather.2.cloned.1.call-start = ((), (), s32[]{:S(2)}) async-start(), calls=%async_computation.2 | async-start | bytes 2359296 | tf_op jit(solution)/shard_map/all_gather | solution.py:170
  15.4 122.4 %all-to-all-start = ((s32[8,1,4]{2,1,0:T(1,128)}), s32[8,1,4]{2,1,0:T(1,128)S(1)}, u32[]{:S(2)}, u32[]{:S(2)}) async-start(s32[8,1,4]{2,1,0:T(1,128)} %bitcast), calls=%async_computation | async-start | bytes 8192 | tf_op jit(solution)/shard_map/all_to_all | solution.py:218
  24.4 4.0 %copy-start.5 = (bf16[1,128,32]{1,2,0:T(8,128)(2,1)S(1)}, bf16[1,128,32]{1,2,0:T(8,128)(2,1)}, u32[]{:S(2)}) copy-start(bf16[1,128,32]{1,2,0:T(8,128)(2,1)} %param.9) | copy-start | bytes 24580
  49.4 2.4 copy-start.1
  137.8 31.5 %all-to-all-start.1 = ((f32[8,4,8192]{2,1,0:T(4,128)}), f32[8,4,8192]{2,1,0:T(4,128)}, u32[]{:S(2)}, u32[]{:S(2)}) async-start(f32[8,4,8192]{2,1,0:T(4,128)} %fusion.24), calls=%async_computation.1 | async-start | bytes 2097152 | tf_op jit(solution)/shard_map/all_to_all | solution.py:211
  142.0 149.9 %all-reduce.3.cloned.1.call-start = ((), (), s32[]{:S(2)}) async-start(), calls=%async_computation.3 | async-start | bytes 131072 | tf_op jit(solution)/shard_map/psum | solution.py:237
  144.2 4.0 %copy-start.4 = (f32[2,64,1]{2,1,0:T(8,128)S(1)}, f32[2,64,1]{2,1,0:T(8,128)}, u32[]{:S(2)}) copy-start(f32[2,64,1]{2,1,0:T(8,128)} %get-tuple-element.11) | copy-start | bytes 1540
  161.4 3.8 %copy-start.2 = (f32[1,128,4096]{2,1,0:T(8,128)S(1)}, f32[1,128,4096]{2,1,0:T(8,128)}, u32[]{:S(2)}) copy-start(f32[1,128,4096]{2,1,0:T(8,128)} %mul.173) | copy-start | bytes 6291460
  170.9 1.0 copy-start.3
  170.9 0.9 copy-start.6
Sparse Core Ops, SparseCore 0:
  11.9 31.9 all-gather.1
  173.2 118.5 all-reduce.2

commit v3 on v1

--- a/solution.py
+++ b/solution.py
@@ -136,6 +136,20 @@
             flops=flops, transcendentals=nblk * nrows * slots * 5,
             bytes_accessed=nblk * (nrows * DH * 4 + slots * DH * 4 + nrows * DH * 4 + DH * slots * 4)),
     )(qr, qt, k, kt, wcol, mass, spos, qpos)
+
+
+def butterfly_sum(value, axes):
+    count = 1
+    for axis in axes:
+        count *= lax.axis_size(axis)
+    if count & (count - 1):
+        return lax.psum(value, axes)
+    stride = 1
+    while stride < count:
+        pairs = [(i, i ^ stride) for i in range(count)]
+        value = value + lax.ppermute(value, axes, pairs)
+        stride *= 2
+    return value
 
 
 def per_device(queries, keys, head_weights, block_ids, target_mass, key_gain, key_bias):
@@ -233,7 +247,7 @@
         - key_hat * jnp.mean(scaled_grad * key_hat, -1, keepdims=True)
     ) * key_scale
     loss_slots = jnp.where(jnp.arange(dp_count) == dp_index, divergence_total, 0.0)
-    packed = lax.psum(jnp.concatenate([gain_part, bias_part, loss_slots]), ("dp", "ctx"))
+    packed = butterfly_sum(jnp.concatenate([gain_part, bias_part, loss_slots]), ("dp", "ctx"))
     grad_gain = packed[:DH]
     grad_bias = packed[DH:2 * DH]
     loss_total = lax.dynamic_index_in_dim(packed, 2 * DH + dp_index, 0, keepdims=False)

time: 225 us -> 212 us (0.942)
  blocking collectives: 40.5 us -> 0 us
  waiting for transfers between devices: 10.2 us -> 32.1 us
  starting transfers between devices: 10.8 us -> 15.7 us
    psum x1 -> x0, blocking collectives: 40.5 us -> none  [per_device(): lax.psum(jnp.concatenate([gain_part, bias_part, loss_slots]), ('dp', 'ctx'))]
    all_to_all x1, waiting for transfers between devices: 0.01 us -> 19.1 us  [per_device(): lax.all_to_all(outbound.reshape(ctx_count, capacity, BS * DH), 'ctx', spl...]
    ppermute x0 -> x5, starting transfers between devices: none -> 4.95 us  [butterfly_sum(): value = value + lax.ppermute(value, axes, pairs)]
    reshape x2, local copies, waits for them, and re-layouts: 6.89 us -> 2.74 us  [per_device(): qg_rows.reshape(query_count, H, BS, DH).transpose(0, 2, 1, 3)]
    ppermute x0 -> x5, waiting for transfers between devices: none -> 2.76 us  [butterfly_sum(): value = value + lax.ppermute(value, axes, pairs)]
  transfers between devices with their start and end apart: 3 -> 8, of which waited for: 1 -> 4; matrix products, arithmetic and copies ran while one was open for 28% -> 28% of each run, Pallas kernels for 33% -> 35%
where the time goes in v3:
time: 212 us; the launch traced here: 211 us
  Pallas kernels  73.1 us (34%)
  local copies, waits for them, and re-layouts  39.9 us (19%)
  waiting for transfers between devices  32.1 us (15%)
  other arithmetic  27.7 us (13%)
  between operations  16.2 us (8%)
  starting transfers between devices  15.7 us (7%)
  matrix products  6.23 us (3%)
    pallas_call x1, Pallas kernels, score_blocks(): pl.pallas_call(score_kernel, grid=(nblk,), in_specs=[blk(nrows, DH), blk(...  73.1 us
    all_to_all x1, waiting for transfers between devices, per_device(): lax.all_to_all(outbound.reshape(ctx_count, capacity, BS * DH), 'ctx', spl...  19.1 us
    all_gather x1, waiting for transfers between devices, per_device(): shard_rows = lax.all_gather(normed_keys, 'ctx', axis=0, tiled=True)  10.1 us
    all_to_all x1, starting transfers between devices, per_device(): lax.all_to_all(request_table, 'ctx', split_axis=0, concat_axis=0, tiled=T...  6.33 us
    gather x2, local copies, waits for them, and re-layouts, per_device(): shard_rows.reshape(block_rows, BS, DH)  5.54 us
    ppermute x5, starting transfers between devices, butterfly_sum(): value = value + lax.ppermute(value, axes, pairs)  4.95 us
    mul x1, other arithmetic, per_device(): (query_grads - query_hat * jnp.mean(query_grads * query_hat, -1, keepdims...  4.75 us
    mul x2, local copies, waits for them, and re-layouts, query_norm(): query_hat = query_float * query_scale  4.71 us
  transfers between devices with their start and end apart: 8, of which 4 were waited for; matrix products, arithmetic and copies ran while one was open for 28% of the time, Pallas kernels for 35%

profile of v3, /device:TPU:0, one launch (start us, length us, event | category | flops | bytes accessed | tf_op | source)
XLA Modules:
  0.0 211.0 jit_solution(4652228438321916230)
XLA Ops:
  8.4 1.3 fusion.16
  9.7 2.0 fusion.13
  15.4 6.3 %all-to-all-start = ((s32[8,1,4]{2,1,0:T(1,128)}), s32[8,1,4]{2,1,0:T(1,128)S(1)}, u32[]{:S(2)}, u32[]{:S(2)}) async-start(s32[8,1,4]{2,1,0:T(1,128)} %bitcast), calls=%async_computation | async-start | bytes 8192 | tf_op jit(solution)/shard_map/all_to_all | solution.py:232
  24.4 1.4 copy.74
  25.8 2.3 %copy.75 = bf16[2,2048,128]{1,2,0:T(8,128)(2,1)} copy(bf16[2,2048,128]{2,1,0:T(8,128)(2,1)} %bitcast.87) | data formatting | bytes 2097152 | tf_op jit(solution)/shard_map/reshape | solution.py:202
  28.5 3.4 %reshape.501.w_ref = f32[2,2048,1]{2,1,0:T(8,128)} reshape(f32[2,32,64]{2,1,0:T(8,128)S(1)} %bitcast.95) | data formatting | bytes 32768 | tf_op jit(solution)/shard_map/reshape | solution.py:208
  33.7 10.1 %all-gather.2.cloned.1.call-done = bf16[8192,128]{1,0:T(8,128)(2,1)} async-done(((bf16[1024,128]{1,0:T(8,128)(2,1)}), bf16[8192,128]{1,0:T(8,128)(2,1)}) %all-gather.2.cloned.1.call-update) | async-done | bytes 2097168 | tf_op jit(solution)/shard_map/all_gather | solution.py:184
  43.8 3.3 %gather_fusion = bf16[64,64,128]{2,1,0:T(8,128)(2,1)} fusion(bf16[128,64,128]{2,1,0:T(8,128)(2,1)} %bitcast.93, s32[1024]{0:T(1024)S(1)} %pad_clamp_fusion), kind=kCustom, calls=%fused_computation | custom fusion | bytes 2097408 | tf_op jit(solution)/shard_map/gather | solution.py:188
  47.1 2.3 %copy.76 = bf16[2,2048,128]{1,2,0:T(8,128)(2,1)} copy(bf16[2,2048,128]{2,1,0:T(8,128)(2,1)} %bitcast.86) | data formatting | bytes 2097152 | tf_op jit(solution)/shard_map/gather | solution.py:188
  49.4 2.4 %broadcast_select_fusion = bf16[2,2048,128]{1,2,0:T(8,128)(2,1)} fusion(bf16[2,2048,128]{1,2,0:T(8,128)(2,1)} %copy.76, pred[2,2048]{1,0:T(4,128)(4,1)S(1)} %broadcast_in_dim.70), kind=kLoop, calls=%fused_computation.13 | loop fusion | flops 524288 | bytes 2101248 | tf_op jit(solution)/shard_map/jit(_where)/select_n | solution.py:189
  52.8 2.3 %copy.79.k_ref = bf16[2,2048,128]{2,1,0:T(8,128)(2,1)} copy(bf16[2,2048,128]{1,2,0:T(8,128)(2,1)} %broadcast_select_fusion) | data formatting | bytes 2097152 | tf_op jit(solution)/shard_map/jit(_where)/select_n | solution.py:189
  55.2 73.1 %shard_map.118 = (f32[2,2048,128]{2,1,0:T(8,128)}, f32[2,2048,1]{2,1,0:T(8,128)}, f32[2,128,2048]{2,1,0:T(8,128)}, f32[2,64,1]{2,1,0:T(8,128)}) custom-call(bf16[2,2048,128]{2,1,0:T(8,128)(2,1)} %bitcast.88, bf16[2,128,2048]{2,1,0:T(8,128)(2,1)} %bitcast.92, bf16[2,2048,128]{2,1,0:T(8,128)(2,1)} %copy.79.k_ref, bf16[2,128,2048]{2,1,0:T(8,128)(2,1)} %fusion.35.kt_ref, ...), custom_call_target="tpu_custom_call" | custom-call | flops 8589934592 | bytes 8388608 | tf_op jit(solution)/shard_map/pallas_call | solution.py:119
  128.3 2.9 %copy.81 = f32[2,2048,128]{2,1,0:T(8,128)} copy(f32[2,2048,128]{1,2,0:T(8,128)} %bitcast.89) | data formatting | bytes 4194304 | tf_op jit(solution)/shard_map/transpose | solution.py:217
  131.2 2.7 %reshape.500 = f32[64,8192,1]{1,0,2:T(8,128)} reshape(f32[2,2048,128]{2,1,0:T(8,128)} %copy.81) | data formatting | bytes 4194304 | tf_op jit(solution)/shard_map/reshape | solution.py:222
  133.9 3.7 %fusion.24 = f32[8,4,8192]{2,1,0:T(4,128)} fusion(f32[64,8192,1]{1,0,2:T(8,128)} %reshape.500, pred[8,4,64]{2,0,1:T(8,128)(4,1)S(1)} %compare_and_fusion), kind=kOutput, calls=%fused_computation.45 | convolution fusion | flops 201326592 | bytes 3147776 | tf_op jit(solution)/shard_map/dot_general | solution.py:223
  137.7 4.4 %all-to-all-start.1 = ((f32[8,4,8192]{2,1,0:T(4,128)}), f32[8,4,8192]{2,1,0:T(4,128)}, u32[]{:S(2)}, u32[]{:S(2)}) async-start(f32[8,4,8192]{2,1,0:T(4,128)} %fusion.24), calls=%async_computation.1 | async-start | bytes 2097152 | tf_op jit(solution)/shard_map/all_to_all | solution.py:225
  142.1 1.9 mul.172
  144.0 2.8 %mul.173 = f32[1,128,4096]{2,1,0:T(8,128)} reshape(f32[128,32,128]{2,1,0:T(8,128)} %mul.172) | data formatting | bytes 4194304 | tf_op jit(solution)/shard_map/mul | solution.py:37
  149.4 19.1 %all-to-all-done.1 = f32[8,4,8192]{2,1,0:T(4,128)} async-done(((f32[8,4,8192]{2,1,0:T(4,128)}), f32[8,4,8192]{2,1,0:T(4,128)}, u32[]{:S(2)}, u32[]{:S(2)}) %all-to-all-start.1) | async-done | bytes 1048608 | tf_op jit(solution)/shard_map/all_to_all | solution.py:225
  168.5 2.6 %reshape.480 = f32[32,8192]{1,0:T(8,128)} reshape(f32[8,4,8192]{2,1,0:T(4,128)} %all-to-all-done.1) | data formatting | bytes 2097152 | tf_op jit(solution)/shard_map/reshape | solution.py:239
  171.1 2.5 %fusion.26 = f32[16,8192]{1,0:T(8,128)} fusion(f32[32,8192]{1,0:T(8,128)} %reshape.480, s32[32]{0:T(128)S(1)} %eq.77), kind=kOutput, calls=%fused_computation.49 | convolution fusion | flops 50332160 | bytes 1572992 | tf_op jit(solution)/shard_map/dot_general | solution.py:238
  173.6 1.9 reshape.481
  175.5 1.7 fusion.15
  177.3 3.7 %multiply_reduce_fusion = f32[2,64,32]{2,1,0:T(8,128)S(1)} fusion(f32[2,64,32]{2,1,0:T(8,128)S(1)} %bitcast.91, f32[2,32,64,128]{3,2,1,0:T(8,128)} %bitcast.82, f32[2,64,32,128]{3,2,1,0:T(8,128)S(1)} %bitcast.81), kind=kLoop, calls=%fused_computation.10 | loop fusion | flops 1568768 | bytes 4227072 | tf_op jit(solution)/shard_map/reduce_sum | solution.py:220
  182.3 1.5 reshape.483
  184.4 1.5 mul.177
  186.0 1.9 collective-permute-start.2
  187.8 4.7 %fusion.3 = f32[1,128,4096]{2,1,0:T(8,128)} fusion(f32[1,128,4096]{2,1,0:T(8,128)} %mul.173, f32[1,128,4096]{2,1,0:T(8,128)} %reshape.483, f32[1,128,4096]{2,1,0:T(8,128)} %mul.177, bf16[1,128,4096]{2,1,0:T(8,128)(2,1)S(1)} %copy-done), kind=kLoop, calls=%fused_computation.7 | loop fusion | flops 2621440 | bytes 9437184 | tf_op jit(solution)/shard_map/mul | solution.py:219
  194.1 1.5 collective-permute-start.3
  195.6 2.0 collective-permute-done.3
  197.6 1.5 collective-permute-start.4
  199.1 1.4 fusion.20
  (94 shorter events, 18.5 us)
Async XLA Ops:
  7.2 14.5 %copy-start = (bf16[1,128,4096]{2,1,0:T(8,128)(2,1)S(1)}, bf16[1,128,4096]{2,1,0:T(8,128)(2,1)}, u32[]{:S(2)}) copy-start(bf16[1,128,4096]{2,1,0:T(8,128)(2,1)} %param.7) | copy-start | bytes 3145732
  7.2 36.7 %all-gather.2.cloned.1.call-start = ((), (), s32[]{:S(2)}) async-start(), calls=%async_computation.2 | async-start | bytes 2359296 | tf_op jit(solution)/shard_map/all_gather | solution.py:184
  15.4 122.3 %all-to-all-start = ((s32[8,1,4]{2,1,0:T(1,128)}), s32[8,1,4]{2,1,0:T(1,128)S(1)}, u32[]{:S(2)}, u32[]{:S(2)}) async-start(s32[8,1,4]{2,1,0:T(1,128)} %bitcast), calls=%async_computation | async-start | bytes 8192 | tf_op jit(solution)/shard_map/all_to_all | solution.py:232
  24.4 4.0 %copy-start.7 = (bf16[1,128,32]{1,2,0:T(8,128)(2,1)S(1)}, bf16[1,128,32]{1,2,0:T(8,128)(2,1)}, u32[]{:S(2)}) copy-start(bf16[1,128,32]{1,2,0:T(8,128)(2,1)} %param.9) | copy-start | bytes 24580
  49.4 2.4 %copy-start.1 = (bf16[2,2048,128]{1,2,0:T(8,128)(2,1)S(1)}, bf16[2,2048,128]{1,2,0:T(8,128)(2,1)}, u32[]{:S(2)}) copy-start(bf16[2,2048,128]{1,2,0:T(8,128)(2,1)} %copy.76) | copy-start | bytes 3145732
  137.7 30.8 %all-to-all-start.1 = ((f32[8,4,8192]{2,1,0:T(4,128)}), f32[8,4,8192]{2,1,0:T(4,128)}, u32[]{:S(2)}, u32[]{:S(2)}) async-start(f32[8,4,8192]{2,1,0:T(4,128)} %fusion.24), calls=%async_computation.1 | async-start | bytes 2097152 | tf_op jit(solution)/shard_map/all_to_all | solution.py:225
  144.0 4.0 %copy-start.6 = (f32[2,64,1]{2,1,0:T(8,128)S(1)}, f32[2,64,1]{2,1,0:T(8,128)}, u32[]{:S(2)}) copy-start(f32[2,64,1]{2,1,0:T(8,128)} %get-tuple-element.11) | copy-start | bytes 1540
  149.4 26.1 %copy-start.3 = (bf16[1,1024,128]{2,1,0:T(8,128)(2,1)S(1)}, bf16[1,1024,128]{2,1,0:T(8,128)(2,1)}, u32[]{:S(2)}) copy-start(bf16[1,1024,128]{2,1,0:T(8,128)(2,1)} %param.8) | copy-start | bytes 786436
  149.4 26.1 %copy-start.8 = (f32[128]{0:T(128)S(1)}, f32[128]{0:T(128)}, u32[]{:S(2)}) copy-start(f32[128]{0:T(128)} %param.12) | copy-start | bytes 1540
  177.2 3.8 %collective-permute-start = (f32[260]{0:T(512)S(1)}, f32[260]{0:T(512)S(1)}, u32[]{:S(2)}, u32[]{:S(2)}) collective-permute-start(f32[260]{0:T(512)S(1)} %pad_maximum_fusion), channel_id=1, source_target_pairs={{0,1},{1,0},{2,3},{3,2},{4,5},{5,4},{6,7},{7,6},{8,9},{9,8},{10,11... | collective-permute-start | bytes 3128 | tf_op jit(solution)/shard_map/ppermute | solution.py:150
  177.3 3.8 %copy-start.2 = (f32[2,2048,128]{2,1,0:T(8,128)S(1)}, f32[2,2048,128]{2,1,0:T(8,128)}, u32[]{:S(2)}) copy-start(f32[2,2048,128]{2,1,0:T(8,128)} %get-tuple-element.12) | copy-start | bytes 6291460
  181.0 5.0 %collective-permute-start.1 = (f32[260]{0:T(512)S(1)}, f32[260]{0:T(512)S(1)}, u32[]{:S(2)}, u32[]{:S(2)}) collective-permute-start(f32[260]{0:T(512)S(1)} %fusion.30), channel_id=1, source_target_pairs={{0,2},{1,3},{2,0},{3,1},{4,6},{5,7},{6,4},{7,5},{8,10},{9,11},{10,... | collective-permute-start | bytes 3128 | tf_op jit(solution)/shard_map/ppermute | solution.py:150
  186.0 6.6 %copy-start.5 = (f32[2,2048,1]{2,1,0:T(8,128)S(1)}, f32[2,2048,1]{2,1,0:T(8,128)}, u32[]{:S(2)}) copy-start(f32[2,2048,1]{2,1,0:T(8,128)} %get-tuple-element.13) | copy-start | bytes 49156
  186.0 8.1 %collective-permute-start.2 = (f32[260]{0:T(512)S(1)}, f32[260]{0:T(512)S(1)}, u32[]{:S(2)}, u32[]{:S(2)}) collective-permute-start(f32[260]{0:T(512)S(1)} %add.193), channel_id=1, source_target_pairs={{0,4},{1,5},{2,6},{3,7},{4,0},{5,1},{6,2},{7,3},{8,12},{9,13},{10,... | collective-permute-start | bytes 3128 | tf_op jit(solution)/shard_map/ppermute | solution.py:150
  192.6 2.9 %copy-start.4 = (f32[16,8192]{1,0:T(8,128)S(1)}, f32[16,8192]{1,0:T(8,128)}, u32[]{:S(2)}) copy-start(f32[16,8192]{1,0:T(8,128)} %fusion.26) | copy-start | bytes 1572868
  194.1 3.6 %collective-permute-start.3 = (f32[260]{0:T(512)S(1)}, f32[260]{0:T(512)S(1)}, u32[]{:S(2)}, u32[]{:S(2)}) collective-permute-start(f32[260]{0:T(512)S(1)} %add.194), channel_id=1, source_target_pairs={{0,8},{1,9},{2,10},{3,11},{4,12},{5,13},{6,14},{7,15},{8,0},{9,1},... | collective-permute-start | bytes 3128 | tf_op jit(solution)/shard_map/ppermute | solution.py:150
  197.6 3.6 %collective-permute-start.4 = (f32[260]{0:T(512)S(1)}, f32[260]{0:T(512)S(1)}, u32[]{:S(2)}, u32[]{:S(2)}) collective-permute-start(f32[260]{0:T(512)S(1)} %add.195), channel_id=1, source_target_pairs={{0,16},{1,17},{2,18},{3,19},{4,20},{5,21},{6,22},{7,23},{8,24},{9,... | collective-permute-start | bytes 3128 | tf_op jit(solution)/shard_map/ppermute | solution.py:150
Sparse Core Ops, SparseCore 0:
  11.9 31.9 all-gather.1

commit v4 on v3

--- a/solution.py
+++ b/solution.py
@@ -39,7 +39,7 @@
 
 
 def score_kernel(qr_ref, qt_ref, k_ref, kt_ref, w_ref, mass_ref, spos_ref, qpos_ref,
-                 qg_ref, wg_ref, sgt_ref, div_ref, mix_ref, mg_ref):
+                 qg_ref, wg_ref, sgt_ref, div_ref, mix_ref, mg_ref, sp_ref):
     f32 = jnp.float32
     inv_root = DH ** (-0.5)
     rows = HEAD_GROUP * BS
@@ -57,6 +57,7 @@
             cs = slice(c * CHUNK, (c + 1) * CHUNK)
             s = jnp.dot(q, kt_ref[:, cs], preferred_element_type=f32) * inv_root
             sp = jnp.maximum(s, 0.0) + jnp.log1p(jnp.exp(-jnp.abs(s)))
+            sp_ref[pl.ds(r0, rows), cs] = sp
             ws = (wcol * sp).reshape(HEAD_GROUP, BS, CHUNK)
             mix_ref[:, cs] += jnp.sum(ws, 0)
         return carry
@@ -89,10 +90,8 @@
         for c in range(chunks):
             cs = slice(c * CHUNK, (c + 1) * CHUNK)
             s = jnp.dot(q, kt_ref[:, cs], preferred_element_type=f32) * inv_root
-            e = jnp.exp(-jnp.abs(s))
-            sp = jnp.maximum(s, 0.0) + jnp.log1p(e)
-            r = 1.0 / (1.0 + e)
-            sig = jnp.where(s >= 0.0, r, e * r)
+            sp = sp_ref[pl.ds(r0, rows), cs]
+            sig = jnp.exp(s - sp)
             mgc = mg_ref[:, cs]
             mg4 = jnp.broadcast_to(mgc[None], (HEAD_GROUP, BS, CHUNK)).reshape(rows, CHUNK)
             sg = (mg4 * wcol * sig).astype(jnp.bfloat16)
@@ -130,10 +129,14 @@
             jax.ShapeDtypeStruct((nblk, DH, slots), f32),
             jax.ShapeDtypeStruct((nblk, BS, 1), f32),
         ],
-        scratch_shapes=[pltpu.VMEM((BS, slots), f32), pltpu.VMEM((BS, slots), f32)],
-        compiler_params=pltpu.CompilerParams(dimension_semantics=("arbitrary",)),
+        scratch_shapes=[
+            pltpu.VMEM((BS, slots), f32), pltpu.VMEM((BS, slots), f32), pltpu.VMEM((nrows, slots), f32)
+        ],
+        compiler_params=pltpu.CompilerParams(
+            dimension_semantics=("arbitrary",), vmem_limit_bytes=60 * 1024 * 1024
+        ),
         cost_estimate=pl.CostEstimate(
-            flops=flops, transcendentals=nblk * nrows * slots * 5,
+            flops=flops, transcendentals=nblk * nrows * slots * 3,
             bytes_accessed=nblk * (nrows * DH * 4 + slots * DH * 4 + nrows * DH * 4 + DH * slots * 4)),
     )(qr, qt, k, kt, wcol, mass, spos, qpos)
 

time: 212 us -> 190 us (0.90)
  Pallas kernels: 73.1 us -> 51.9 us
    pallas_call x1, Pallas kernels: 73.1 us -> 51.9 us  [score_blocks(): pl.pallas_call(score_kernel, grid=(nblk,), in_specs=[blk(nrows, DH), blk(...]
  transfers between devices with their start and end apart: 8 -> 8, of which waited for: 4 -> 4; matrix products, arithmetic and copies ran while one was open for 28% -> 31% of each run, Pallas kernels for 35% -> 27%
where the time goes in v4:
time: 190 us
  Pallas kernels  51.9 us (27%)
  local copies, waits for them, and re-layouts  39.9 us (21%)
  waiting for transfers between devices  32 us (17%)
  other arithmetic  27.7 us (15%)
  between operations  16.2 us (9%)
  starting transfers between devices  15.8 us (8%)
  matrix products  6.23 us (3%)
    pallas_call x1, Pallas kernels, score_blocks(): pl.pallas_call(score_kernel, grid=(nblk,), in_specs=[blk(nrows, DH), blk(...  51.9 us
    all_to_all x1, waiting for transfers between devices, per_device(): lax.all_to_all(outbound.reshape(ctx_count, capacity, BS * DH), 'ctx', spl...  19.1 us
    all_gather x1, waiting for transfers between devices, per_device(): shard_rows = lax.all_gather(normed_keys, 'ctx', axis=0, tiled=True)  10.1 us
    all_to_all x1, starting transfers between devices, per_device(): lax.all_to_all(request_table, 'ctx', split_axis=0, concat_axis=0, tiled=T...  6.33 us
    gather x2, local copies, waits for them, and re-layouts, per_device(): shard_rows.reshape(block_rows, BS, DH)  5.54 us
    ppermute x5, starting transfers between devices, butterfly_sum(): value = value + lax.ppermute(value, axes, pairs)  4.99 us
    mul x1, other arithmetic, per_device(): (query_grads - query_hat * jnp.mean(query_grads * query_hat, -1, keepdims...  4.75 us
    mul x2, local copies, waits for them, and re-layouts, query_norm(): query_hat = query_float * query_scale  4.71 us
  transfers between devices with their start and end apart: 8, of which 4 were waited for; matrix products, arithmetic and copies ran while one was open for 31% of the time, Pallas kernels for 27%

profile of v4, /device:TPU:0, one launch (start us, length us, event | category | flops | bytes accessed | tf_op | source)
XLA Modules:
  0.0 189.7 jit_solution(14921074027555722536)
XLA Ops:
  8.4 1.3 fusion.16
  9.7 2.0 %fusion.13 = bf16[1024,128]{1,0:T(8,128)(2,1)} fusion(bf16[1,1024,128]{2,1,0:T(8,128)(2,1)} %param.8, f32[128]{0:T(128)} %param.13, f32[128]{0:T(128)} %param.12, f32[1024]{0:T(1024)S(1)} %add_rsqrt_fusion.1, f32[1024]{0:T(1024)S(1)} %broadcast_multiply_fusion.3), kind=kLoop, calls=%fused_computation.24 | loop fusion | flops 786432 | bytes 533504 | tf_op jit(solution)/shard_map/convert_element_type | solution.py:30
  15.4 6.3 %all-to-all-start = ((s32[8,1,4]{2,1,0:T(1,128)}), s32[8,1,4]{2,1,0:T(1,128)S(1)}, u32[]{:S(2)}, u32[]{:S(2)}) async-start(s32[8,1,4]{2,1,0:T(1,128)} %bitcast), calls=%async_computation | async-start | bytes 8192 | tf_op jit(solution)/shard_map/all_to_all | solution.py:235
  24.4 1.4 copy.74
  25.8 2.3 %copy.75 = bf16[2,2048,128]{1,2,0:T(8,128)(2,1)} copy(bf16[2,2048,128]{2,1,0:T(8,128)(2,1)} %bitcast.87) | data formatting | bytes 2097152 | tf_op jit(solution)/shard_map/reshape | solution.py:205
  28.5 3.4 %reshape.501.w_ref = f32[2,2048,1]{2,1,0:T(8,128)} reshape(f32[2,32,64]{2,1,0:T(8,128)S(1)} %bitcast.95) | data formatting | bytes 32768 | tf_op jit(solution)/shard_map/reshape | solution.py:211
  33.7 10.1 %all-gather.2.cloned.1.call-done = bf16[8192,128]{1,0:T(8,128)(2,1)} async-done(((bf16[1024,128]{1,0:T(8,128)(2,1)}), bf16[8192,128]{1,0:T(8,128)(2,1)}) %all-gather.2.cloned.1.call-update) | async-done | bytes 2097168 | tf_op jit(solution)/shard_map/all_gather | solution.py:187
  43.8 3.3 %gather_fusion = bf16[64,64,128]{2,1,0:T(8,128)(2,1)} fusion(bf16[128,64,128]{2,1,0:T(8,128)(2,1)} %bitcast.93, s32[1024]{0:T(1024)S(1)} %pad_clamp_fusion), kind=kCustom, calls=%fused_computation | custom fusion | bytes 2097408 | tf_op jit(solution)/shard_map/gather | solution.py:191
  47.1 2.3 %copy.76 = bf16[2,2048,128]{1,2,0:T(8,128)(2,1)} copy(bf16[2,2048,128]{2,1,0:T(8,128)(2,1)} %bitcast.86) | data formatting | bytes 2097152 | tf_op jit(solution)/shard_map/gather | solution.py:191
  49.4 2.4 %broadcast_select_fusion = bf16[2,2048,128]{1,2,0:T(8,128)(2,1)} fusion(bf16[2,2048,128]{1,2,0:T(8,128)(2,1)} %copy.76, pred[2,2048]{1,0:T(4,128)(4,1)S(1)} %broadcast_in_dim.70), kind=kLoop, calls=%fused_computation.13 | loop fusion | flops 524288 | bytes 2101248 | tf_op jit(solution)/shard_map/jit(_where)/select_n | solution.py:192
  52.8 2.3 %copy.79.k_ref = bf16[2,2048,128]{2,1,0:T(8,128)(2,1)} copy(bf16[2,2048,128]{1,2,0:T(8,128)(2,1)} %broadcast_select_fusion) | data formatting | bytes 2097152 | tf_op jit(solution)/shard_map/jit(_where)/select_n | solution.py:192
  55.2 51.9 %shard_map.118 = (f32[2,2048,128]{2,1,0:T(8,128)}, f32[2,2048,1]{2,1,0:T(8,128)}, f32[2,128,2048]{2,1,0:T(8,128)}, f32[2,64,1]{2,1,0:T(8,128)}) custom-call(bf16[2,2048,128]{2,1,0:T(8,128)(2,1)} %bitcast.88, bf16[2,128,2048]{2,1,0:T(8,128)(2,1)} %bitcast.92, bf16[2,2048,128]{2,1,0:T(8,128)(2,1)} %copy.79.k_ref, bf16[2,128,2048]{2,1,0:T(8,128)(2,1)} %fusion.35.kt_ref, ...), custom_call_target="tpu_custom_call" | custom-call | flops 8589934592 | bytes 8388608 | tf_op jit(solution)/shard_map/pallas_call | solution.py:118
  107.0 2.9 %copy.81 = f32[2,2048,128]{2,1,0:T(8,128)} copy(f32[2,2048,128]{1,2,0:T(8,128)} %bitcast.89) | data formatting | bytes 4194304 | tf_op jit(solution)/shard_map/transpose | solution.py:220
  109.9 2.7 %reshape.500 = f32[64,8192,1]{1,0,2:T(8,128)} reshape(f32[2,2048,128]{2,1,0:T(8,128)} %copy.81) | data formatting | bytes 4194304 | tf_op jit(solution)/shard_map/reshape | solution.py:225
  112.7 3.7 %fusion.24 = f32[8,4,8192]{2,1,0:T(4,128)} fusion(f32[64,8192,1]{1,0,2:T(8,128)} %reshape.500, pred[8,4,64]{2,0,1:T(8,128)(4,1)S(1)} %compare_and_fusion), kind=kOutput, calls=%fused_computation.45 | convolution fusion | flops 201326592 | bytes 3147776 | tf_op jit(solution)/shard_map/dot_general | solution.py:226
  116.4 4.4 %all-to-all-start.1 = ((f32[8,4,8192]{2,1,0:T(4,128)}), f32[8,4,8192]{2,1,0:T(4,128)}, u32[]{:S(2)}, u32[]{:S(2)}) async-start(f32[8,4,8192]{2,1,0:T(4,128)} %fusion.24), calls=%async_computation.1 | async-start | bytes 2097152 | tf_op jit(solution)/shard_map/all_to_all | solution.py:228
  120.8 1.9 %mul.172 = f32[128,32,128]{2,1,0:T(8,128)} broadcast(f32[128,32]{1,0:T(8,128)S(1)} %copy.88), dimensions={0,1} | broadcast | bytes 2113536 | tf_op jit(solution)/shard_map/mul | solution.py:37
  122.8 2.8 %mul.173 = f32[1,128,4096]{2,1,0:T(8,128)} reshape(f32[128,32,128]{2,1,0:T(8,128)} %mul.172) | data formatting | bytes 4194304 | tf_op jit(solution)/shard_map/mul | solution.py:37
  128.1 19.1 %all-to-all-done.1 = f32[8,4,8192]{2,1,0:T(4,128)} async-done(((f32[8,4,8192]{2,1,0:T(4,128)}), f32[8,4,8192]{2,1,0:T(4,128)}, u32[]{:S(2)}, u32[]{:S(2)}) %all-to-all-start.1) | async-done | bytes 1048608 | tf_op jit(solution)/shard_map/all_to_all | solution.py:228
  147.3 2.6 %reshape.480 = f32[32,8192]{1,0:T(8,128)} reshape(f32[8,4,8192]{2,1,0:T(4,128)} %all-to-all-done.1) | data formatting | bytes 2097152 | tf_op jit(solution)/shard_map/reshape | solution.py:242
  149.8 2.5 %fusion.26 = f32[16,8192]{1,0:T(8,128)} fusion(f32[32,8192]{1,0:T(8,128)} %reshape.480, s32[32]{0:T(128)S(1)} %eq.77), kind=kOutput, calls=%fused_computation.49 | convolution fusion | flops 50332160 | bytes 1572992 | tf_op jit(solution)/shard_map/dot_general | solution.py:241
  152.3 1.9 %reshape.481 = f32[1024,128]{1,0:T(8,128)} reshape(f32[16,8192]{1,0:T(8,128)} %fusion.26) | data formatting | bytes 1048576 | tf_op jit(solution)/shard_map/reshape | solution.py:243
  154.2 1.7 fusion.15
  156.0 3.7 %multiply_reduce_fusion = f32[2,64,32]{2,1,0:T(8,128)S(1)} fusion(f32[2,64,32]{2,1,0:T(8,128)S(1)} %bitcast.91, f32[2,32,64,128]{3,2,1,0:T(8,128)} %bitcast.82, f32[2,64,32,128]{3,2,1,0:T(8,128)S(1)} %bitcast.81), kind=kLoop, calls=%fused_computation.10 | loop fusion | flops 1568768 | bytes 4227072 | tf_op jit(solution)/shard_map/reduce_sum | solution.py:223
  161.0 1.5 reshape.483
  163.2 1.5 mul.177
  164.7 1.9 collective-permute-start.2
  166.6 4.7 %fusion.3 = f32[1,128,4096]{2,1,0:T(8,128)} fusion(f32[1,128,4096]{2,1,0:T(8,128)} %mul.173, f32[1,128,4096]{2,1,0:T(8,128)} %reshape.483, f32[1,128,4096]{2,1,0:T(8,128)} %mul.177, bf16[1,128,4096]{2,1,0:T(8,128)(2,1)S(1)} %copy-done), kind=kLoop, calls=%fused_computation.7 | loop fusion | flops 2621440 | bytes 9437184 | tf_op jit(solution)/shard_map/mul | solution.py:222
  172.8 1.5 collective-permute-start.3
  174.4 2.0 %collective-permute-done.3 = f32[260]{0:T(512)S(1)} collective-permute-done((f32[260]{0:T(512)S(1)}, f32[260]{0:T(512)S(1)}, u32[]{:S(2)}, u32[]{:S(2)}) %collective-permute-start.3) | collective-permute-done | bytes 1072 | tf_op jit(solution)/shard_map/ppermute | solution.py:153
  176.4 1.5 collective-permute-start.4
  177.9 1.4 fusion.20
  (94 shorter events, 18.5 us)
Async XLA Ops:
  7.2 14.5 %copy-start = (bf16[1,128,4096]{2,1,0:T(8,128)(2,1)S(1)}, bf16[1,128,4096]{2,1,0:T(8,128)(2,1)}, u32[]{:S(2)}) copy-start(bf16[1,128,4096]{2,1,0:T(8,128)(2,1)} %param.7) | copy-start | bytes 3145732
  7.2 36.7 %all-gather.2.cloned.1.call-start = ((), (), s32[]{:S(2)}) async-start(), calls=%async_computation.2 | async-start | bytes 2359296 | tf_op jit(solution)/shard_map/all_gather | solution.py:187
  15.4 101.0 %all-to-all-start = ((s32[8,1,4]{2,1,0:T(1,128)}), s32[8,1,4]{2,1,0:T(1,128)S(1)}, u32[]{:S(2)}, u32[]{:S(2)}) async-start(s32[8,1,4]{2,1,0:T(1,128)} %bitcast), calls=%async_computation | async-start | bytes 8192 | tf_op jit(solution)/shard_map/all_to_all | solution.py:235
  24.4 4.0 %copy-start.7 = (bf16[1,128,32]{1,2,0:T(8,128)(2,1)S(1)}, bf16[1,128,32]{1,2,0:T(8,128)(2,1)}, u32[]{:S(2)}) copy-start(bf16[1,128,32]{1,2,0:T(8,128)(2,1)} %param.9) | copy-start | bytes 24580
  49.4 2.4 %copy-start.1 = (bf16[2,2048,128]{1,2,0:T(8,128)(2,1)S(1)}, bf16[2,2048,128]{1,2,0:T(8,128)(2,1)}, u32[]{:S(2)}) copy-start(bf16[2,2048,128]{1,2,0:T(8,128)(2,1)} %copy.76) | copy-start | bytes 3145732
  116.4 30.8 %all-to-all-start.1 = ((f32[8,4,8192]{2,1,0:T(4,128)}), f32[8,4,8192]{2,1,0:T(4,128)}, u32[]{:S(2)}, u32[]{:S(2)}) async-start(f32[8,4,8192]{2,1,0:T(4,128)} %fusion.24), calls=%async_computation.1 | async-start | bytes 2097152 | tf_op jit(solution)/shard_map/all_to_all | solution.py:228
  122.8 4.0 %copy-start.6 = (f32[2,64,1]{2,1,0:T(8,128)S(1)}, f32[2,64,1]{2,1,0:T(8,128)}, u32[]{:S(2)}) copy-start(f32[2,64,1]{2,1,0:T(8,128)} %get-tuple-element.11) | copy-start | bytes 1540
  128.1 26.1 %copy-start.3 = (bf16[1,1024,128]{2,1,0:T(8,128)(2,1)S(1)}, bf16[1,1024,128]{2,1,0:T(8,128)(2,1)}, u32[]{:S(2)}) copy-start(bf16[1,1024,128]{2,1,0:T(8,128)(2,1)} %param.8) | copy-start | bytes 786436
  128.1 26.1 %copy-start.8 = (f32[128]{0:T(128)S(1)}, f32[128]{0:T(128)}, u32[]{:S(2)}) copy-start(f32[128]{0:T(128)} %param.12) | copy-start | bytes 1540
  155.9 3.8 %collective-permute-start = (f32[260]{0:T(512)S(1)}, f32[260]{0:T(512)S(1)}, u32[]{:S(2)}, u32[]{:S(2)}) collective-permute-start(f32[260]{0:T(512)S(1)} %pad_maximum_fusion), channel_id=1, source_target_pairs={{0,1},{1,0},{2,3},{3,2},{4,5},{5,4},{6,7},{7,6},{8,9},{9,8},{10,11... | collective-permute-start | bytes 3128 | tf_op jit(solution)/shard_map/ppermute | solution.py:153
  156.0 3.8 %copy-start.2 = (f32[2,2048,128]{2,1,0:T(8,128)S(1)}, f32[2,2048,128]{2,1,0:T(8,128)}, u32[]{:S(2)}) copy-start(f32[2,2048,128]{2,1,0:T(8,128)} %get-tuple-element.12) | copy-start | bytes 6291460
  159.7 5.0 %collective-permute-start.1 = (f32[260]{0:T(512)S(1)}, f32[260]{0:T(512)S(1)}, u32[]{:S(2)}, u32[]{:S(2)}) collective-permute-start(f32[260]{0:T(512)S(1)} %fusion.30), channel_id=1, source_target_pairs={{0,2},{1,3},{2,0},{3,1},{4,6},{5,7},{6,4},{7,5},{8,10},{9,11},{10,... | collective-permute-start | bytes 3128 | tf_op jit(solution)/shard_map/ppermute | solution.py:153
  164.7 6.6 %copy-start.5 = (f32[2,2048,1]{2,1,0:T(8,128)S(1)}, f32[2,2048,1]{2,1,0:T(8,128)}, u32[]{:S(2)}) copy-start(f32[2,2048,1]{2,1,0:T(8,128)} %get-tuple-element.13) | copy-start | bytes 49156
  164.7 8.1 %collective-permute-start.2 = (f32[260]{0:T(512)S(1)}, f32[260]{0:T(512)S(1)}, u32[]{:S(2)}, u32[]{:S(2)}) collective-permute-start(f32[260]{0:T(512)S(1)} %add.193), channel_id=1, source_target_pairs={{0,4},{1,5},{2,6},{3,7},{4,0},{5,1},{6,2},{7,3},{8,12},{9,13},{10,... | collective-permute-start | bytes 3128 | tf_op jit(solution)/shard_map/ppermute | solution.py:153
  171.3 2.9 %copy-start.4 = (f32[16,8192]{1,0:T(8,128)S(1)}, f32[16,8192]{1,0:T(8,128)}, u32[]{:S(2)}) copy-start(f32[16,8192]{1,0:T(8,128)} %fusion.26) | copy-start | bytes 1572868
  172.8 3.6 %collective-permute-start.3 = (f32[260]{0:T(512)S(1)}, f32[260]{0:T(512)S(1)}, u32[]{:S(2)}, u32[]{:S(2)}) collective-permute-start(f32[260]{0:T(512)S(1)} %add.194), channel_id=1, source_target_pairs={{0,8},{1,9},{2,10},{3,11},{4,12},{5,13},{6,14},{7,15},{8,0},{9,1},... | collective-permute-start | bytes 3128 | tf_op jit(solution)/shard_map/ppermute | solution.py:153
  176.4 3.6 %collective-permute-start.4 = (f32[260]{0:T(512)S(1)}, f32[260]{0:T(512)S(1)}, u32[]{:S(2)}, u32[]{:S(2)}) collective-permute-start(f32[260]{0:T(512)S(1)} %add.195), channel_id=1, source_target_pairs={{0,16},{1,17},{2,18},{3,19},{4,20},{5,21},{6,22},{7,23},{8,24},{9,... | collective-permute-start | bytes 3128 | tf_op jit(solution)/shard_map/ppermute | solution.py:153
Sparse Core Ops, SparseCore 0:
  11.9 31.9 all-gather.1

commit v5 on v4

--- a/solution.py
+++ b/solution.py
@@ -183,14 +183,10 @@
     ) & is_listed[:, None]
     request_table = jnp.sum(jnp.where(placement, local_block[:, None] + 1, 0), 0) - 1
     request_table = request_table.reshape(ctx_count, capacity)
-    initial_slots = jnp.zeros((request_count, BS, DH), jnp.bfloat16)
     shard_rows = lax.all_gather(normed_keys, "ctx", axis=0, tiled=True)
     block_rows = shard_rows.shape[0] // BS
-    relative = block_safe * BS
-    inside = is_listed & (relative >= 0) & (relative < shard_rows.shape[0])
-    picked = shard_rows.reshape(block_rows, BS, DH)[jnp.clip(relative // BS, 0, block_rows - 1)]
-    slot_keys = jnp.where(inside[:, None, None], picked, initial_slots)
-    slot_keys = slot_keys.reshape(query_count, slot_count, DH)
+    picked = shard_rows.reshape(block_rows, BS, DH)[jnp.clip(block_safe, 0, block_rows - 1)]
+    slot_keys = picked.reshape(query_count, slot_count, DH)
     slot_positions = (block_safe[:, None] * BS + jnp.arange(BS, dtype=jnp.int32)[None, :]).reshape(
         query_count, slot_count
     )
@@ -224,16 +220,16 @@
     ) * query_scale
     slot_flat = grad_slots.reshape(request_count, BS * DH)
     outbound = jnp.dot(placement.T.astype(jnp.float32), slot_flat, precision=lax.Precision.HIGHEST)
-    returned, asked_back = (
-        lax.all_to_all(
-            outbound.reshape(ctx_count, capacity, BS * DH),
-            "ctx",
-            split_axis=0,
-            concat_axis=0,
-            tiled=True,
-        ),
-        lax.all_to_all(request_table, "ctx", split_axis=0, concat_axis=0, tiled=True),
-    )
+    id_lanes = jnp.broadcast_to(request_table.astype(jnp.float32)[:, :, None], (ctx_count, capacity, 128))
+    combined = lax.all_to_all(
+        jnp.concatenate([outbound.reshape(ctx_count, capacity, BS * DH), id_lanes], -1),
+        "ctx",
+        split_axis=0,
+        concat_axis=0,
+        tiled=True,
+    )
+    returned = combined[:, :, : BS * DH]
+    asked_back = combined[:, :, BS * DH].astype(jnp.int32)
     own_rows = (
         asked_back.reshape(ctx_count * capacity)[None, :]
         == jnp.arange(key_count, dtype=jnp.int32)[:, None]

time: 190 us -> 191 us (level)
  waiting for transfers between devices: 32 us -> 41.4 us
  starting transfers between devices: 15.8 us -> 9.38 us
  other arithmetic: 27.7 us -> 23.8 us
  local copies, waits for them, and re-layouts: 39.9 us -> 42.6 us
    all_gather x1, waiting for transfers between devices: 10.1 us -> 17.8 us  [per_device(): shard_rows = lax.all_gather(normed_keys, 'ctx', axis=0, tiled=True)]
    all_to_all x2 -> x1, starting transfers between devices: 10.7 us -> 4.42 us  [per_device(): lax.all_to_all(jnp.concatenate([outbound.reshape(ctx_count, capacity, BS...]
    mul x2, local copies, waits for them, and re-layouts: 2.1 us -> 4.64 us  [per_device(): query_hat * jnp.mean(query_grads * query_hat, -1, keepdims=True)]
    select_n x1, other arithmetic: 2.38 us -> 0.01 us  [per_device(): owner_index = block_safe // key_count]
    select_n x1 -> x0, local copies, waits for them, and re-layouts: 2.33 us -> none  [per_device(): slot_keys = jnp.where(inside[:, None, None], picked, initial_slots)]
    slice x0 -> x1, local copies, waits for them, and re-layouts: none -> 2.27 us  [per_device(): returned = combined[:, :, :BS * DH]]
    reshape x0 -> x1, local copies, waits for them, and re-layouts: none -> 2.26 us  [per_device(): slot_keys = picked.reshape(query_count, slot_count, DH)]
    gather x2 -> x1, local copies, waits for them, and re-layouts: 5.54 us -> 3.34 us  [per_device(): shard_rows.reshape(block_rows, BS, DH)]
  transfers between devices with their start and end apart: 8 -> 7, of which waited for: 4 -> 4; matrix products, arithmetic and copies ran while one was open for 31% -> 20% of each run, Pallas kernels for 27% -> 0%
where the time goes in v5:
time: 191 us; the launch traced here: 190 us
  Pallas kernels  51.9 us (27%)
  local copies, waits for them, and re-layouts  42.6 us (22%)
  waiting for transfers between devices  41.4 us (22%)
  other arithmetic  23.8 us (12%)
  between operations  16.1 us (8%)
  starting transfers between devices  9.38 us (5%)
  matrix products  4.92 us (3%)
    pallas_call x1, Pallas kernels, score_blocks(): pl.pallas_call(score_kernel, grid=(nblk,), in_specs=[blk(nrows, DH), blk(...  51.9 us
    all_to_all x1, waiting for transfers between devices, per_device(): lax.all_to_all(jnp.concatenate([outbound.reshape(ctx_count, capacity, BS...  20.8 us
    all_gather x1, waiting for transfers between devices, per_device(): shard_rows = lax.all_gather(normed_keys, 'ctx', axis=0, tiled=True)  17.8 us
    ppermute x5, starting transfers between devices, butterfly_sum(): value = value + lax.ppermute(value, axes, pairs)  4.92 us
    mul x1, other arithmetic, per_device(): (query_grads - query_hat * jnp.mean(query_grads * query_hat, -1, keepdims...  4.75 us
    mul x2, local copies, waits for them, and re-layouts, query_norm(): query_hat = query_float * query_scale  4.71 us
    mul x2, local copies, waits for them, and re-layouts, per_device(): query_hat * jnp.mean(query_grads * query_hat, -1, keepdims=True)  4.64 us
    all_to_all x1, starting transfers between devices, per_device(): lax.all_to_all(jnp.concatenate([outbound.reshape(ctx_count, capacity, BS...  4.42 us
  transfers between devices with their start and end apart: 7, of which 4 were waited for; matrix products, arithmetic and copies ran while one was open for 20% of the time, Pallas kernels for 0%

profile of v5, /device:TPU:0, one launch (start us, length us, event | category | flops | bytes accessed | tf_op | source)
XLA Modules:
  0.0 190.2 jit_solution(1940620474815784398)
XLA Ops:
  8.4 1.3 fusion.16
  9.7 2.0 %fusion.13 = bf16[1024,128]{1,0:T(8,128)(2,1)} fusion(bf16[1,1024,128]{2,1,0:T(8,128)(2,1)} %param.8, f32[128]{0:T(128)} %param.13, f32[128]{0:T(128)} %param.12, f32[1024]{0:T(1024)S(1)} %add_rsqrt_fusion.1, f32[1024]{0:T(1024)S(1)} %broadcast_multiply_fusion.3), kind=kLoop, calls=%fused_computation.24 | loop fusion | flops 786432 | bytes 533504 | tf_op jit(solution)/shard_map/convert_element_type | solution.py:30
  16.7 1.4 copy.75
  18.1 2.3 %copy.76 = bf16[2,2048,128]{1,2,0:T(8,128)(2,1)} copy(bf16[2,2048,128]{2,1,0:T(8,128)(2,1)} %bitcast.84) | data formatting | bytes 2097152 | tf_op jit(solution)/shard_map/reshape | solution.py:201
  20.5 3.4 %reshape.435.w_ref = f32[2,2048,1]{2,1,0:T(8,128)} reshape(f32[2,32,64]{2,1,0:T(8,128)S(1)} %bitcast.93) | data formatting | bytes 32768 | tf_op jit(solution)/shard_map/reshape | solution.py:207
  25.9 17.8 %all-gather.2.cloned.1.call-done = bf16[8192,128]{1,0:T(8,128)(2,1)} async-done(((bf16[1024,128]{1,0:T(8,128)(2,1)}), bf16[8192,128]{1,0:T(8,128)(2,1)}) %all-gather.2.cloned.1.call-update) | async-done | bytes 2097168 | tf_op jit(solution)/shard_map/all_gather | solution.py:186
  43.7 3.3 %gather_fusion = bf16[64,64,128]{2,1,0:T(8,128)(2,1)} fusion(bf16[128,64,128]{2,1,0:T(8,128)(2,1)} %bitcast.91, s32[1024]{0:T(1024)S(1)} %pad_clamp_fusion), kind=kCustom, calls=%fused_computation | custom fusion | bytes 2097408 | tf_op jit(solution)/shard_map/gather | solution.py:188
  47.1 2.3 %copy.77 = bf16[2,2048,128]{1,2,0:T(8,128)(2,1)} copy(bf16[2,2048,128]{2,1,0:T(8,128)(2,1)} %bitcast.82) | data formatting | bytes 2097152 | tf_op jit(solution)/shard_map/reshape | solution.py:189
  49.3 51.9 %shard_map.118 = (f32[2,2048,128]{2,1,0:T(8,128)}, f32[2,2048,1]{2,1,0:T(8,128)}, f32[2,128,2048]{2,1,0:T(8,128)}, f32[2,64,1]{2,1,0:T(8,128)}) custom-call(bf16[2,2048,128]{2,1,0:T(8,128)(2,1)} %bitcast.85, bf16[2,128,2048]{2,1,0:T(8,128)(2,1)} %bitcast.89, bf16[2,2048,128]{2,1,0:T(8,128)(2,1)} %bitcast.83, bf16[2,128,2048]{2,1,0:T(8,128)(2,1)} %bitcast.90, ...), custom_call_target="tpu_custom_call" | custom-call | flops 8589934592 | bytes 8388608 | tf_op jit(solution)/shard_map/pallas_call | solution.py:118
  101.2 2.9 %copy.81 = f32[2,2048,128]{2,1,0:T(8,128)} copy(f32[2,2048,128]{1,2,0:T(8,128)} %bitcast.86) | data formatting | bytes 4194304 | tf_op jit(solution)/shard_map/transpose | solution.py:216
  104.1 2.7 %reshape.434 = f32[64,8192,1]{1,0,2:T(8,128)} reshape(f32[2,2048,128]{2,1,0:T(8,128)} %copy.81) | data formatting | bytes 4194304 | tf_op jit(solution)/shard_map/reshape | solution.py:221
  106.9 2.4 %fusion.25 = f32[8,4,8192]{2,0,1:T(8,128)S(1)} fusion(f32[64,8192,1]{1,0,2:T(8,128)} %reshape.434, s32[8,4]{0,1:T(4,128)S(1)} %multiply_add_fusion, s32[64]{0:T(128)S(1)} %add_select_fusion.1, pred[64]{0:T(512)(128)(4,1)S(1)} %ge.18), kind=kOutput, calls=%fused_computation.47 | convolution fusion | flops 201330688 | bytes 3146176 | tf_op jit(solution)/shard_map/dot_general | solution.py:222
  109.4 1.3 copy.83
  110.7 4.4 %all-to-all-start = ((f32[8,4,8320]{2,1,0:T(4,128)}), f32[8,4,8320]{2,1,0:T(4,128)}, u32[]{:S(2)}, u32[]{:S(2)}) async-start(f32[8,4,8320]{2,1,0:T(4,128)} %copy.83), calls=%async_computation | async-start | bytes 2129920 | tf_op jit(solution)/shard_map/all_to_all | solution.py:224
  115.1 1.9 %mul.156 = f32[128,32,128]{2,1,0:T(8,128)} broadcast(f32[128,32]{1,0:T(8,128)S(1)} %copy.87), dimensions={0,1} | broadcast | bytes 2113536 | tf_op jit(solution)/shard_map/mul | solution.py:37
  117.0 2.8 %mul.157 = f32[1,128,4096]{2,1,0:T(8,128)} reshape(f32[128,32,128]{2,1,0:T(8,128)} %mul.156) | data formatting | bytes 4194304 | tf_op jit(solution)/shard_map/mul | solution.py:37
  121.1 20.8 %all-to-all-done = f32[8,4,8320]{2,1,0:T(4,128)} async-done(((f32[8,4,8320]{2,1,0:T(4,128)}), f32[8,4,8320]{2,1,0:T(4,128)}, u32[]{:S(2)}, u32[]{:S(2)}) %all-to-all-start) | async-done | bytes 1064992 | tf_op jit(solution)/shard_map/all_to_all | solution.py:224
  141.9 2.3 %slice.19 = f32[8,4,8192]{2,1,0:T(4,128)} slice(f32[8,4,8320]{2,1,0:T(4,128)} %all-to-all-done), slice={[0:8], [0:4], [0:8192]} | slice | bytes 2097152 | tf_op jit(solution)/shard_map/slice | solution.py:231
  144.2 2.6 %reshape.414 = f32[32,8192]{1,0:T(8,128)} reshape(f32[8,4,8192]{2,1,0:T(4,128)} %slice.19) | data formatting | bytes 2097152 | tf_op jit(solution)/shard_map/reshape | solution.py:238
  147.8 2.5 %fusion.30 = f32[16,8192]{1,0:T(8,128)} fusion(f32[32,8192]{1,0:T(8,128)} %reshape.414, s32[32]{0:T(128)S(1)} %convert_element_type.73), kind=kOutput, calls=%fused_computation.53 | convolution fusion | flops 50332160 | bytes 1572992 | tf_op jit(solution)/shard_map/dot_general | solution.py:237
  150.3 1.9 %reshape.415 = f32[1024,128]{1,0:T(8,128)} reshape(f32[16,8192]{1,0:T(8,128)} %fusion.30) | data formatting | bytes 1048576 | tf_op jit(solution)/shard_map/reshape | solution.py:239
  152.2 1.7 fusion.15
  154.0 3.7 %multiply_reduce_fusion = f32[2,64,32]{2,1,0:T(8,128)S(1)} fusion(f32[2,64,32]{2,1,0:T(8,128)S(1)} %bitcast.88, f32[2,32,64,128]{3,2,1,0:T(8,128)} %bitcast.78, f32[2,64,32,128]{3,2,1,0:T(8,128)S(1)} %bitcast.77), kind=kLoop, calls=%fused_computation.10 | loop fusion | flops 1568768 | bytes 4227072 | tf_op jit(solution)/shard_map/reduce_sum | solution.py:219
  159.0 1.9 %mul.160 = f32[128,32,128]{2,1,0:T(8,128)} broadcast(f32[128,32]{1,0:T(8,128)S(1)} %bitcast.92), dimensions={0,1} | broadcast | bytes 2113536 | tf_op jit(solution)/shard_map/mul | solution.py:219
  161.0 2.7 %mul.161 = f32[1,128,4096]{2,1,0:T(8,128)} reshape(f32[128,32,128]{2,1,0:T(8,128)} %mul.160) | data formatting | bytes 4194304 | tf_op jit(solution)/shard_map/mul | solution.py:219
  163.7 1.5 reshape.417
  165.2 1.9 collective-permute-start.2
  167.1 4.7 %fusion.3 = f32[1,128,4096]{2,1,0:T(8,128)} fusion(f32[1,128,4096]{2,1,0:T(8,128)} %mul.157, f32[1,128,4096]{2,1,0:T(8,128)} %reshape.417, f32[1,128,4096]{2,1,0:T(8,128)} %mul.161, bf16[1,128,4096]{2,1,0:T(8,128)(2,1)S(1)} %copy-done), kind=kLoop, calls=%fused_computation.7 | loop fusion | flops 2621440 | bytes 9437184 | tf_op jit(solution)/shard_map/mul | solution.py:218
  173.3 1.4 collective-permute-start.3
  174.8 2.0 %collective-permute-done.3 = f32[260]{0:T(512)S(1)} collective-permute-done((f32[260]{0:T(512)S(1)}, f32[260]{0:T(512)S(1)}, u32[]{:S(2)}, u32[]{:S(2)}) %collective-permute-start.3) | collective-permute-done | bytes 1072 | tf_op jit(solution)/shard_map/ppermute | solution.py:153
  176.9 1.5 collective-permute-start.4
  178.3 1.4 fusion.20
  (87 shorter events, 15.3 us)
Async XLA Ops:
  7.2 6.8 %copy-start = (bf16[1,128,4096]{2,1,0:T(8,128)(2,1)S(1)}, bf16[1,128,4096]{2,1,0:T(8,128)(2,1)}, u32[]{:S(2)}) copy-start(bf16[1,128,4096]{2,1,0:T(8,128)(2,1)} %param.7) | copy-start | bytes 3145732
  7.2 36.6 %all-gather.2.cloned.1.call-start = ((), (), s32[]{:S(2)}) async-start(), calls=%async_computation.1 | async-start | bytes 2359296 | tf_op jit(solution)/shard_map/all_gather | solution.py:186
  16.7 3.7 %copy-start.6 = (bf16[1,128,32]{1,2,0:T(8,128)(2,1)S(1)}, bf16[1,128,32]{1,2,0:T(8,128)(2,1)}, u32[]{:S(2)}) copy-start(bf16[1,128,32]{1,2,0:T(8,128)(2,1)} %param.9) | copy-start | bytes 24580
  110.7 31.2 %all-to-all-start = ((f32[8,4,8320]{2,1,0:T(4,128)}), f32[8,4,8320]{2,1,0:T(4,128)}, u32[]{:S(2)}, u32[]{:S(2)}) async-start(f32[8,4,8320]{2,1,0:T(4,128)} %copy.83), calls=%async_computation | async-start | bytes 2129920 | tf_op jit(solution)/shard_map/all_to_all | solution.py:224
  117.0 2.8 %copy-start.5 = (f32[2,64,1]{2,1,0:T(8,128)S(1)}, f32[2,64,1]{2,1,0:T(8,128)}, u32[]{:S(2)}) copy-start(f32[2,64,1]{2,1,0:T(8,128)} %get-tuple-element.11) | copy-start | bytes 1540
  144.2 8.1 %copy-start.2 = (bf16[1,1024,128]{2,1,0:T(8,128)(2,1)S(1)}, bf16[1,1024,128]{2,1,0:T(8,128)(2,1)}, u32[]{:S(2)}) copy-start(bf16[1,1024,128]{2,1,0:T(8,128)(2,1)} %param.8) | copy-start | bytes 786436
  144.2 8.1 %copy-start.7 = (f32[128]{0:T(128)S(1)}, f32[128]{0:T(128)}, u32[]{:S(2)}) copy-start(f32[128]{0:T(128)} %param.12) | copy-start | bytes 1540
  153.9 3.8 %collective-permute-start = (f32[260]{0:T(512)S(1)}, f32[260]{0:T(512)S(1)}, u32[]{:S(2)}, u32[]{:S(2)}) collective-permute-start(f32[260]{0:T(512)S(1)} %pad_maximum_fusion.1), channel_id=1, source_target_pairs={{0,1},{1,0},{2,3},{3,2},{4,5},{5,4},{6,7},{7,6},{8,9},{9,8},{10,11... | collective-permute-start | bytes 3128 | tf_op jit(solution)/shard_map/ppermute | solution.py:153
  154.0 3.8 %copy-start.1 = (f32[2,2048,128]{2,1,0:T(8,128)S(1)}, f32[2,2048,128]{2,1,0:T(8,128)}, u32[]{:S(2)}) copy-start(f32[2,2048,128]{2,1,0:T(8,128)} %get-tuple-element.12) | copy-start | bytes 6291460
  157.7 7.5 %collective-permute-start.1 = (f32[260]{0:T(512)S(1)}, f32[260]{0:T(512)S(1)}, u32[]{:S(2)}, u32[]{:S(2)}) collective-permute-start(f32[260]{0:T(512)S(1)} %fusion.35), channel_id=1, source_target_pairs={{0,2},{1,3},{2,0},{3,1},{4,6},{5,7},{6,4},{7,5},{8,10},{9,11},{10,... | collective-permute-start | bytes 3128 | tf_op jit(solution)/shard_map/ppermute | solution.py:153
  165.2 6.6 %copy-start.4 = (f32[2,2048,1]{2,1,0:T(8,128)S(1)}, f32[2,2048,1]{2,1,0:T(8,128)}, u32[]{:S(2)}) copy-start(f32[2,2048,1]{2,1,0:T(8,128)} %get-tuple-element.13) | copy-start | bytes 49156
  165.2 8.1 %collective-permute-start.2 = (f32[260]{0:T(512)S(1)}, f32[260]{0:T(512)S(1)}, u32[]{:S(2)}, u32[]{:S(2)}) collective-permute-start(f32[260]{0:T(512)S(1)} %add.182), channel_id=1, source_target_pairs={{0,4},{1,5},{2,6},{3,7},{4,0},{5,1},{6,2},{7,3},{8,12},{9,13},{10,... | collective-permute-start | bytes 3128 | tf_op jit(solution)/shard_map/ppermute | solution.py:153
  171.8 2.9 %copy-start.3 = (f32[16,8192]{1,0:T(8,128)S(1)}, f32[16,8192]{1,0:T(8,128)}, u32[]{:S(2)}) copy-start(f32[16,8192]{1,0:T(8,128)} %fusion.30) | copy-start | bytes 1572868
  173.3 3.6 %collective-permute-start.3 = (f32[260]{0:T(512)S(1)}, f32[260]{0:T(512)S(1)}, u32[]{:S(2)}, u32[]{:S(2)}) collective-permute-start(f32[260]{0:T(512)S(1)} %add.183), channel_id=1, source_target_pairs={{0,8},{1,9},{2,10},{3,11},{4,12},{5,13},{6,14},{7,15},{8,0},{9,1},... | collective-permute-start | bytes 3128 | tf_op jit(solution)/shard_map/ppermute | solution.py:153
  176.9 3.6 %collective-permute-start.4 = (f32[260]{0:T(512)S(1)}, f32[260]{0:T(512)S(1)}, u32[]{:S(2)}, u32[]{:S(2)}) collective-permute-start(f32[260]{0:T(512)S(1)} %add.184), channel_id=1, source_target_pairs={{0,16},{1,17},{2,18},{3,19},{4,20},{5,21},{6,22},{7,23},{8,24},{9,... | collective-permute-start | bytes 3128 | tf_op jit(solution)/shard_map/ppermute | solution.py:153
Sparse Core Ops, SparseCore 0:
  11.9 31.7 all-gather.1

commit v6 on v5

--- a/solution.py
+++ b/solution.py
@@ -183,9 +183,10 @@
     ) & is_listed[:, None]
     request_table = jnp.sum(jnp.where(placement, local_block[:, None] + 1, 0), 0) - 1
     request_table = request_table.reshape(ctx_count, capacity)
-    shard_rows = lax.all_gather(normed_keys, "ctx", axis=0, tiled=True)
-    block_rows = shard_rows.shape[0] // BS
-    picked = shard_rows.reshape(block_rows, BS, DH)[jnp.clip(block_safe, 0, block_rows - 1)]
+    asked_back = lax.all_to_all(request_table, "ctx", split_axis=0, concat_axis=0, tiled=True)
+    sent_keys = normed_keys.reshape(key_count, BS, DH)[jnp.clip(asked_back, 0, key_count - 1)]
+    arrived_keys = lax.all_to_all(sent_keys, "ctx", split_axis=0, concat_axis=0, tiled=True)
+    picked = arrived_keys.reshape(ctx_count * capacity, BS, DH)[target_slot]
     slot_keys = picked.reshape(query_count, slot_count, DH)
     slot_positions = (block_safe[:, None] * BS + jnp.arange(BS, dtype=jnp.int32)[None, :]).reshape(
         query_count, slot_count
@@ -220,16 +221,9 @@
     ) * query_scale
     slot_flat = grad_slots.reshape(request_count, BS * DH)
     outbound = jnp.dot(placement.T.astype(jnp.float32), slot_flat, precision=lax.Precision.HIGHEST)
-    id_lanes = jnp.broadcast_to(request_table.astype(jnp.float32)[:, :, None], (ctx_count, capacity, 128))
-    combined = lax.all_to_all(
-        jnp.concatenate([outbound.reshape(ctx_count, capacity, BS * DH), id_lanes], -1),
-        "ctx",
-        split_axis=0,
-        concat_axis=0,
-        tiled=True,
-    )
-    returned = combined[:, :, : BS * DH]
-    asked_back = combined[:, :, BS * DH].astype(jnp.int32)
+    returned = lax.all_to_all(
+        outbound.reshape(ctx_count, capacity, BS * DH), "ctx", split_axis=0, concat_axis=0, tiled=True
+    )
     own_rows = (
         asked_back.reshape(ctx_count * capacity)[None, :]
         == jnp.arange(key_count, dtype=jnp.int32)[:, None]

time: 191 us -> 185 us (0.969)
  waiting for transfers between devices: 41.4 us -> 22.8 us
  between operations: 16.1 us -> 2.7 us
  starting transfers between devices: 9.38 us -> 20.9 us
  other arithmetic: 23.8 us -> 30.7 us
  local copies, waits for them, and re-layouts: 42.6 us -> 48.3 us
    all_gather x1 -> x0, waiting for transfers between devices: 17.8 us -> none  [per_device(): shard_rows = lax.all_gather(normed_keys, 'ctx', axis=0, tiled=True)]
    all_to_all x1 -> x3, starting transfers between devices: 4.42 us -> 15.8 us  [the longest x1 6.33 us: per_device(): lax.all_to_all(request_table, 'ctx', split_axis=0, concat_axis=0, tiled=T...]
    unnamed x18 -> x24, local copies, waits for them, and re-layouts: 0.77 us -> 3.71 us
    unnamed x2, other arithmetic: 0.41 us -> 3.01 us
    slice x1 -> x0, local copies, waits for them, and re-layouts: 2.27 us -> none  [per_device(): returned = combined[:, :, :BS * DH]]
    gather x1 -> x2, local copies, waits for them, and re-layouts: 3.34 us -> 5.15 us  [the longest x1 2.79 us: per_device(): picked = arrived_keys.reshape(ctx_count * capacity, BS, DH)[target_slot]]
    all_to_all x1 -> x3, waiting for transfers between devices: 20.8 us -> 20.1 us  [the longest x1 19.3 us: per_device(): lax.all_to_all(outbound.reshape(ctx_count, capacity, BS * DH), 'ctx', spl...]
  transfers between devices with their start and end apart: 7 -> 8, of which waited for: 4 -> 4; matrix products, arithmetic and copies ran while one was open for 20% -> 30% of each run, Pallas kernels for 0% -> 0%
where the time goes in v6:
time: 185 us; the launch traced here: 184 us
  Pallas kernels  51.9 us (28%)
  local copies, waits for them, and re-layouts  48.3 us (26%)
  other arithmetic  30.7 us (17%)
  waiting for transfers between devices  22.8 us (12%)
  starting transfers between devices  20.9 us (11%)
  matrix products  6.23 us (3%)
  between operations  2.7 us (1%)
    pallas_call x1, Pallas kernels, score_blocks(): pl.pallas_call(score_kernel, grid=(nblk,), in_specs=[blk(nrows, DH), blk(...  51.9 us
    all_to_all x1, waiting for transfers between devices, per_device(): lax.all_to_all(outbound.reshape(ctx_count, capacity, BS * DH), 'ctx', spl...  19.3 us
    all_to_all x1, starting transfers between devices, per_device(): lax.all_to_all(request_table, 'ctx', split_axis=0, concat_axis=0, tiled=T...  6.33 us
    all_to_all x1, starting transfers between devices, per_device(): lax.all_to_all(sent_keys, 'ctx', split_axis=0, concat_axis=0, tiled=True)  5.1 us
    ppermute x5, starting transfers between devices, butterfly_sum(): value = value + lax.ppermute(value, axes, pairs)  5.05 us
    mul x1, other arithmetic, per_device(): (query_grads - query_hat * jnp.mean(query_grads * query_hat, -1, keepdims...  4.75 us
    mul x2, local copies, waits for them, and re-layouts, query_norm(): query_hat = query_float * query_scale  4.71 us
    mul x2, local copies, waits for them, and re-layouts, per_device(): query_hat * jnp.mean(query_grads * query_hat, -1, keepdims=True)  4.64 us
  transfers between devices with their start and end apart: 8, of which 4 were waited for; matrix products, arithmetic and copies ran while one was open for 30% of the time, Pallas kernels for 0%

profile of v6, /device:TPU:0, one launch (start us, length us, event | category | flops | bytes accessed | tf_op | source)
XLA Modules:
  0.0 183.6 jit_solution(3890076535499941386)
XLA Ops:
  3.6 6.3 %all-to-all-start = ((s32[8,1,4]{2,1,0:T(1,128)}), s32[8,1,4]{2,1,0:T(1,128)S(1)}, u32[]{:S(2)}, u32[]{:S(2)}) async-start(s32[8,1,4]{2,1,0:T(1,128)} %bitcast), calls=%async_computation | async-start | bytes 8192 | tf_op jit(solution)/shard_map/all_to_all | solution.py:186
  14.1 1.6 convert_bitcast_fusion
  15.8 1.7 copy.97
  17.5 2.2 %reduce_sum.103 = f32[128,32]{1,0:T(8,128)S(1)} reduce(f32[128,32,128]{2,1,0:T(8,128)} %bitcast.79, f32[]{:T(128)} %constant.83.clone.1), dimensions={2}, to_apply=%region_3.4 | reduce | flops 520192 | bytes 2113540 | tf_op jit(solution)/shard_map/reduce_sum | solution.py:36
  19.9 2.0 %copy.96 = f32[16,8,32,128]{3,2,1,0:T(8,128)S(1)} copy(f32[16,8,32,128]{3,1,2,0:T(8,128)} %convert_bitcast_fusion) | data formatting | bytes 4194304
  25.2 2.4 %gather_fusion = bf16[32,64,128]{2,1,0:T(8,128)(2,1)} fusion(bf16[16,64,128]{2,1,0:T(8,128)(2,1)} %add_convert_fusion, s32[1024]{0:T(1024)S(1)} %pad_clamp_fusion.1), kind=kCustom, calls=%fused_computation | custom fusion | bytes 1048704 | tf_op jit(solution)/shard_map/gather | solution.py:187
  27.6 5.1 %all-to-all-start.1 = ((bf16[8,4,64,128]{3,2,1,0:T(8,128)(2,1)}), bf16[8,4,64,128]{3,2,1,0:T(8,128)(2,1)}, u32[]{:S(2)}, u32[]{:S(2)}) async-start(bf16[8,4,64,128]{3,2,1,0:T(8,128)(2,1)} %bitcast.86), calls=%async_computation.1 | async-start | bytes 1048576 | tf_op jit(solution)/shard_map/all_to_all | solution.py:188
  35.5 2.6 %copy.80 = bf16[2,32,64,128]{3,2,1,0:T(8,128)(2,1)} copy(bf16[2,32,64,128]{3,1,2,0:T(8,128)(2,1)} %fusion.5) | data formatting | bytes 2097152 | tf_op jit(solution)/shard_map/transpose | solution.py:202
  38.1 2.3 %copy.81 = bf16[2,2048,128]{1,2,0:T(8,128)(2,1)} copy(bf16[2,2048,128]{2,1,0:T(8,128)(2,1)} %bitcast.83) | data formatting | bytes 2097152 | tf_op jit(solution)/shard_map/reshape | solution.py:202
  40.5 3.4 %reshape.543.w_ref = f32[2,2048,1]{2,1,0:T(8,128)} reshape(f32[2,32,64]{2,1,0:T(8,128)S(1)} %bitcast.92) | data formatting | bytes 32768 | tf_op jit(solution)/shard_map/reshape | solution.py:208
  48.2 2.8 %gather_fusion.1 = bf16[64,64,128]{2,1,0:T(8,128)(2,1)} fusion(bf16[32,64,128]{2,1,0:T(8,128)(2,1)} %bitcast.9, s32[1024]{0:T(1024)S(1)} %pad_clamp_fusion), kind=kCustom, calls=%fused_computation.1 | custom fusion | bytes 2097408 | tf_op jit(solution)/shard_map/gather | solution.py:189
  50.9 2.3 %copy.84 = bf16[2,2048,128]{1,2,0:T(8,128)(2,1)} copy(bf16[2,2048,128]{2,1,0:T(8,128)(2,1)} %bitcast.81) | data formatting | bytes 2097152 | tf_op jit(solution)/shard_map/reshape | solution.py:190
  53.2 51.9 %shard_map.118 = (f32[2,2048,128]{2,1,0:T(8,128)}, f32[2,2048,1]{2,1,0:T(8,128)}, f32[2,128,2048]{2,1,0:T(8,128)}, f32[2,64,1]{2,1,0:T(8,128)}) custom-call(bf16[2,2048,128]{2,1,0:T(8,128)(2,1)} %bitcast.84, bf16[2,128,2048]{2,1,0:T(8,128)(2,1)} %bitcast.89, bf16[2,2048,128]{2,1,0:T(8,128)(2,1)} %bitcast.82, bf16[2,128,2048]{2,1,0:T(8,128)(2,1)} %bitcast.90, ...), custom_call_target="tpu_custom_call" | custom-call | flops 8589934592 | bytes 8388608 | tf_op jit(solution)/shard_map/pallas_call | solution.py:118
  105.1 2.9 %copy.88 = f32[2,2048,128]{2,1,0:T(8,128)} copy(f32[2,2048,128]{1,2,0:T(8,128)} %bitcast.85) | data formatting | bytes 4194304 | tf_op jit(solution)/shard_map/transpose | solution.py:217
  108.0 2.7 %reshape.542 = f32[64,8192,1]{1,0,2:T(8,128)} reshape(f32[2,2048,128]{2,1,0:T(8,128)} %copy.88) | data formatting | bytes 4194304 | tf_op jit(solution)/shard_map/reshape | solution.py:222
  110.7 3.7 %fusion.10 = f32[8,4,8192]{2,1,0:T(4,128)} fusion(f32[64,8192,1]{1,0,2:T(8,128)} %reshape.542, pred[8,4,64]{2,0,1:T(8,128)(4,1)S(1)} %compare_and_fusion), kind=kOutput, calls=%fused_computation.35 | convolution fusion | flops 201326592 | bytes 3147776 | tf_op jit(solution)/shard_map/dot_general | solution.py:223
  114.4 4.4 %all-to-all-start.2 = ((f32[8,4,8192]{2,1,0:T(4,128)}), f32[8,4,8192]{2,1,0:T(4,128)}, u32[]{:S(2)}, u32[]{:S(2)}) async-start(f32[8,4,8192]{2,1,0:T(4,128)} %fusion.10), calls=%async_computation.2 | async-start | bytes 2097152 | tf_op jit(solution)/shard_map/all_to_all | solution.py:224
  118.9 1.9 %mul.175 = f32[128,32,128]{2,1,0:T(8,128)} broadcast(f32[128,32]{1,0:T(8,128)S(1)} %copy.95), dimensions={0,1} | broadcast | bytes 2113536 | tf_op jit(solution)/shard_map/mul | solution.py:37
  120.8 2.8 %mul.176 = f32[1,128,4096]{2,1,0:T(8,128)} reshape(f32[128,32,128]{2,1,0:T(8,128)} %mul.175) | data formatting | bytes 4194304 | tf_op jit(solution)/shard_map/mul | solution.py:37
  126.1 19.3 %all-to-all-done.2 = f32[8,4,8192]{2,1,0:T(4,128)} async-done(((f32[8,4,8192]{2,1,0:T(4,128)}), f32[8,4,8192]{2,1,0:T(4,128)}, u32[]{:S(2)}, u32[]{:S(2)}) %all-to-all-start.2) | async-done | bytes 1048608 | tf_op jit(solution)/shard_map/all_to_all | solution.py:224
  145.4 2.6 %reshape.512 = f32[32,8192]{1,0:T(8,128)} reshape(f32[8,4,8192]{2,1,0:T(4,128)} %all-to-all-done.2) | data formatting | bytes 2097152 | tf_op jit(solution)/shard_map/reshape | solution.py:232
  148.0 2.5 %fusion.12 = f32[16,8192]{1,0:T(8,128)} fusion(f32[32,8192]{1,0:T(8,128)} %reshape.512, s32[32]{0:T(128)S(1)} %eq.77), kind=kOutput, calls=%fused_computation.39 | convolution fusion | flops 50332160 | bytes 1572992 | tf_op jit(solution)/shard_map/dot_general | solution.py:231
  150.5 1.9 %reshape.513 = f32[1024,128]{1,0:T(8,128)} reshape(f32[16,8192]{1,0:T(8,128)} %fusion.12) | data formatting | bytes 1048576 | tf_op jit(solution)/shard_map/reshape | solution.py:233
  152.4 1.7 multiply_reduce_fusion.1
  154.2 3.7 %multiply_reduce_fusion = f32[2,64,32]{2,1,0:T(8,128)S(1)} fusion(f32[2,64,32]{2,1,0:T(8,128)S(1)} %bitcast.88, f32[2,32,64,128]{3,2,1,0:T(8,128)} %bitcast.76, f32[2,64,32,128]{3,2,1,0:T(8,128)S(1)} %bitcast.75), kind=kLoop, calls=%fused_computation.11 | loop fusion | flops 1568768 | bytes 4227072 | tf_op jit(solution)/shard_map/reduce_sum | solution.py:220
  159.2 1.9 %mul.179 = f32[128,32,128]{2,1,0:T(8,128)} broadcast(f32[128,32]{1,0:T(8,128)S(1)} %bitcast.91), dimensions={0,1} | broadcast | bytes 2113536 | tf_op jit(solution)/shard_map/mul | solution.py:220
  161.1 2.7 %mul.180 = f32[1,128,4096]{2,1,0:T(8,128)} reshape(f32[128,32,128]{2,1,0:T(8,128)} %mul.179) | data formatting | bytes 4194304 | tf_op jit(solution)/shard_map/mul | solution.py:220
  163.9 1.5 reshape.515
  165.4 1.9 %collective-permute-start.2 = (f32[260]{0:T(512)S(1)}, f32[260]{0:T(512)S(1)}, u32[]{:S(2)}, u32[]{:S(2)}) collective-permute-start(f32[260]{0:T(512)S(1)} %add.218), channel_id=1, source_target_pairs={{0,4},{1,5},{2,6},{3,7},{4,0},{5,1},{6,2},{7,3},{8,12},{9,13},{10,... | collective-permute-start | bytes 3128 | tf_op jit(solution)/shard_map/ppermute | solution.py:153
  167.3 4.7 %fusion.3 = f32[1,128,4096]{2,1,0:T(8,128)} fusion(f32[1,128,4096]{2,1,0:T(8,128)} %mul.176, f32[1,128,4096]{2,1,0:T(8,128)} %reshape.515, f32[1,128,4096]{2,1,0:T(8,128)} %mul.180, bf16[1,128,4096]{2,1,0:T(8,128)(2,1)S(1)} %copy-done), kind=kLoop, calls=%fused_computation.8 | loop fusion | flops 2621440 | bytes 9437184 | tf_op jit(solution)/shard_map/mul | solution.py:219
  175.1 2.0 %collective-permute-done.3 = f32[260]{0:T(512)S(1)} collective-permute-done((f32[260]{0:T(512)S(1)}, f32[260]{0:T(512)S(1)}, u32[]{:S(2)}, u32[]{:S(2)}) %collective-permute-start.3) | collective-permute-done | bytes 1072 | tf_op jit(solution)/shard_map/ppermute | solution.py:153
  177.1 1.5 collective-permute-start.4
  (101 shorter events, 28.0 us)
Async XLA Ops:
  0.6 13.4 %copy-start = (bf16[1,128,4096]{2,1,0:T(8,128)(2,1)S(1)}, bf16[1,128,4096]{2,1,0:T(8,128)(2,1)}, u32[]{:S(2)}) copy-start(bf16[1,128,4096]{2,1,0:T(8,128)(2,1)} %param.7) | copy-start | bytes 3145732
  2.8 12.8 %copy-start.9 = (s32[64]{0:T(128)}, s32[64]{0:T(128)S(1)}, u32[]{:S(2)}) copy-start(s32[64]{0:T(128)S(1)} %add_select_fusion.2) | copy-start | bytes 772
  3.6 21.3 %all-to-all-start = ((s32[8,1,4]{2,1,0:T(1,128)}), s32[8,1,4]{2,1,0:T(1,128)S(1)}, u32[]{:S(2)}, u32[]{:S(2)}) async-start(s32[8,1,4]{2,1,0:T(1,128)} %bitcast), calls=%async_computation | async-start | bytes 8192 | tf_op jit(solution)/shard_map/all_to_all | solution.py:186
  21.9 1.5 copy-start.2
  21.9 1.5 copy-start.7
  21.9 1.5 copy-start.10
  27.6 20.6 %all-to-all-start.1 = ((bf16[8,4,64,128]{3,2,1,0:T(8,128)(2,1)}), bf16[8,4,64,128]{3,2,1,0:T(8,128)(2,1)}, u32[]{:S(2)}, u32[]{:S(2)}) async-start(bf16[8,4,64,128]{3,2,1,0:T(8,128)(2,1)} %bitcast.86), calls=%async_computation.1 | async-start | bytes 1048576 | tf_op jit(solution)/shard_map/all_to_all | solution.py:188
  35.5 4.9 %copy-start.6 = (bf16[1,128,32]{1,2,0:T(8,128)(2,1)S(1)}, bf16[1,128,32]{1,2,0:T(8,128)(2,1)}, u32[]{:S(2)}) copy-start(bf16[1,128,32]{1,2,0:T(8,128)(2,1)} %param.9) | copy-start | bytes 24580
  114.4 31.0 %all-to-all-start.2 = ((f32[8,4,8192]{2,1,0:T(4,128)}), f32[8,4,8192]{2,1,0:T(4,128)}, u32[]{:S(2)}, u32[]{:S(2)}) async-start(f32[8,4,8192]{2,1,0:T(4,128)} %fusion.10), calls=%async_computation.2 | async-start | bytes 2097152 | tf_op jit(solution)/shard_map/all_to_all | solution.py:224
  120.8 4.0 %copy-start.5 = (f32[2,64,1]{2,1,0:T(8,128)S(1)}, f32[2,64,1]{2,1,0:T(8,128)}, u32[]{:S(2)}) copy-start(f32[2,64,1]{2,1,0:T(8,128)} %get-tuple-element.11) | copy-start | bytes 1540
  126.1 26.3 %copy-start.8 = (f32[128]{0:T(128)S(1)}, f32[128]{0:T(128)}, u32[]{:S(2)}) copy-start(f32[128]{0:T(128)} %param.12) | copy-start | bytes 1540
  154.1 3.8 %collective-permute-start = (f32[260]{0:T(512)S(1)}, f32[260]{0:T(512)S(1)}, u32[]{:S(2)}, u32[]{:S(2)}) collective-permute-start(f32[260]{0:T(512)S(1)} %pad_maximum_fusion), channel_id=1, source_target_pairs={{0,1},{1,0},{2,3},{3,2},{4,5},{5,4},{6,7},{7,6},{8,9},{9,8},{10,11... | collective-permute-start | bytes 3128 | tf_op jit(solution)/shard_map/ppermute | solution.py:153
  154.2 3.8 %copy-start.1 = (f32[2,2048,128]{2,1,0:T(8,128)S(1)}, f32[2,2048,128]{2,1,0:T(8,128)}, u32[]{:S(2)}) copy-start(f32[2,2048,128]{2,1,0:T(8,128)} %get-tuple-element.12) | copy-start | bytes 6291460
  157.9 7.5 %collective-permute-start.1 = (f32[260]{0:T(512)S(1)}, f32[260]{0:T(512)S(1)}, u32[]{:S(2)}, u32[]{:S(2)}) collective-permute-start(f32[260]{0:T(512)S(1)} %fusion.18), channel_id=1, source_target_pairs={{0,2},{1,3},{2,0},{3,1},{4,6},{5,7},{6,4},{7,5},{8,10},{9,11},{10,... | collective-permute-start | bytes 3128 | tf_op jit(solution)/shard_map/ppermute | solution.py:153
  165.4 6.7 %copy-start.4 = (f32[2,2048,1]{2,1,0:T(8,128)S(1)}, f32[2,2048,1]{2,1,0:T(8,128)}, u32[]{:S(2)}) copy-start(f32[2,2048,1]{2,1,0:T(8,128)} %get-tuple-element.13) | copy-start | bytes 49156
  165.4 8.1 %collective-permute-start.2 = (f32[260]{0:T(512)S(1)}, f32[260]{0:T(512)S(1)}, u32[]{:S(2)}, u32[]{:S(2)}) collective-permute-start(f32[260]{0:T(512)S(1)} %add.218), channel_id=1, source_target_pairs={{0,4},{1,5},{2,6},{3,7},{4,0},{5,1},{6,2},{7,3},{8,12},{9,13},{10,... | collective-permute-start | bytes 3128 | tf_op jit(solution)/shard_map/ppermute | solution.py:153
  172.0 3.0 %copy-start.3 = (f32[16,8192]{1,0:T(8,128)S(1)}, f32[16,8192]{1,0:T(8,128)}, u32[]{:S(2)}) copy-start(f32[16,8192]{1,0:T(8,128)} %fusion.12) | copy-start | bytes 1572868
  173.5 3.6 %collective-permute-start.3 = (f32[260]{0:T(512)S(1)}, f32[260]{0:T(512)S(1)}, u32[]{:S(2)}, u32[]{:S(2)}) collective-permute-start(f32[260]{0:T(512)S(1)} %add.219), channel_id=1, source_target_pairs={{0,8},{1,9},{2,10},{3,11},{4,12},{5,13},{6,14},{7,15},{8,0},{9,1},... | collective-permute-start | bytes 3128 | tf_op jit(solution)/shard_map/ppermute | solution.py:153
  177.1 3.6 %collective-permute-start.4 = (f32[260]{0:T(512)S(1)}, f32[260]{0:T(512)S(1)}, u32[]{:S(2)}, u32[]{:S(2)}) collective-permute-start(f32[260]{0:T(512)S(1)} %add.220), channel_id=1, source_target_pairs={{0,16},{1,17},{2,18},{3,19},{4,20},{5,21},{6,22},{7,23},{8,24},{9,... | collective-permute-start | bytes 3128 | tf_op jit(solution)/shard_map/ppermute | solution.py:153

commit v7 on v6

--- a/solution.py
+++ b/solution.py
@@ -38,8 +38,8 @@
     return (query_hat, query_scale, query_hat.astype(jnp.bfloat16))
 
 
-def score_kernel(qr_ref, qt_ref, k_ref, kt_ref, w_ref, mass_ref, spos_ref, qpos_ref,
-                 qg_ref, wg_ref, sgt_ref, div_ref, mix_ref, mg_ref, sp_ref):
+def score_kernel(q_ref, k_ref, kt_ref, w_ref, mass_ref, spos_ref, qpos_ref,
+                 gq_ref, wg_ref, sgt_ref, div_ref, qr_ref, qt_ref, mix_ref, mg_ref, sp_ref):
     f32 = jnp.float32
     inv_root = DH ** (-0.5)
     rows = HEAD_GROUP * BS
@@ -47,12 +47,28 @@
     slots = kt_ref.shape[1]
     chunks = slots // CHUNK
 
+    for h in range(H):
+        x = q_ref[:, h * DH:(h + 1) * DH].astype(f32)
+        scale = lax.rsqrt(jnp.mean(x * x, -1, keepdims=True) + epsilon)
+        nq = (x * scale).astype(jnp.bfloat16)
+        qr_ref[h * BS:(h + 1) * BS, :] = nq
+        qt_ref[:, h * BS:(h + 1) * BS] = nq.astype(f32).T.astype(jnp.bfloat16)
+
+    head_ids = lax.broadcasted_iota(jnp.int32, (H, HEAD_GROUP), 0)
+    pick_ids = lax.broadcasted_iota(jnp.int32, (H, HEAD_GROUP), 1)
+    lane_heads = lax.broadcasted_iota(jnp.int32, (1, H), 1)
+
+    def group_weights(g):
+        onehot = (head_ids == g * HEAD_GROUP + pick_ids).astype(jnp.bfloat16)
+        w4 = jnp.dot(w_ref[...], onehot, preferred_element_type=f32)
+        return jnp.concatenate([w4[:, hh:hh + 1] for hh in range(HEAD_GROUP)], 0)
+
     mix_ref[...] = jnp.zeros_like(mix_ref)
 
     def first_pass(g, carry):
         r0 = pl.multiple_of(g * rows, rows)
         q = qr_ref[pl.ds(r0, rows), :]
-        wcol = w_ref[pl.ds(r0, rows), :]
+        wcol = group_weights(g)
         for c in range(chunks):
             cs = slice(c * CHUNK, (c + 1) * CHUNK)
             s = jnp.dot(q, kt_ref[:, cs], preferred_element_type=f32) * inv_root
@@ -79,12 +95,13 @@
     mg_ref[...] = (exp_terms / denominator - target) * (1.0 - squashed * squashed)
 
     sgt_ref[...] = jnp.zeros_like(sgt_ref)
+    wg_ref[...] = jnp.zeros_like(wg_ref)
 
     def second_pass(g, carry):
         r0 = pl.multiple_of(g * rows, rows)
         q = qr_ref[pl.ds(r0, rows), :]
         qt = qt_ref[:, pl.ds(r0, rows)]
-        wcol = w_ref[pl.ds(r0, rows), :]
+        wcol = group_weights(g)
         qg_acc = jnp.zeros((rows, DH), f32)
         wg_acc = jnp.zeros((rows, 1), f32)
         for c in range(chunks):
@@ -98,17 +115,28 @@
             wg_acc = wg_acc + jnp.sum(mg4 * sp, 1, keepdims=True)
             qg_acc = qg_acc + jnp.dot(sg, k_ref[cs, :], preferred_element_type=f32)
             sgt_ref[:, cs] += jnp.dot(qt, sg, preferred_element_type=f32)
-        qg_ref[pl.ds(r0, rows), :] = qg_acc * inv_root
-        wg_ref[pl.ds(r0, rows), :] = wg_acc
+        qg_acc = qg_acc * inv_root
+        wg_sum = wg_ref[...]
+        for hh in range(HEAD_GROUP):
+            h = g * HEAD_GROUP + hh
+            wg_sum = wg_sum + jnp.where(lane_heads == h, wg_acc[hh * BS:(hh + 1) * BS], 0.0)
+            lanes = pl.ds(pl.multiple_of(h * DH, DH), DH)
+            x = q_ref[:, lanes].astype(f32)
+            scale = lax.rsqrt(jnp.mean(x * x, -1, keepdims=True) + epsilon)
+            query_hat = x * scale
+            qg = qg_acc[hh * BS:(hh + 1) * BS]
+            gq_ref[:, lanes] = (qg - query_hat * jnp.mean(qg * query_hat, -1, keepdims=True)) * scale
+        wg_ref[...] = wg_sum
         return carry
 
     lax.fori_loop(0, groups, second_pass, 0)
     sgt_ref[...] = sgt_ref[...] * inv_root
 
 
-def score_blocks(qr, qt, k, kt, wcol, mass, spos, qpos):
-    nblk, nrows, _ = qr.shape
+def score_blocks(q, k, kt, w, mass, spos, qpos):
+    nblk = q.shape[0]
     slots = k.shape[1]
+    nrows = H * BS
     f32 = jnp.float32
 
     def blk(*shape):
@@ -119,17 +147,18 @@
         score_kernel,
         grid=(nblk,),
         in_specs=[
-            blk(nrows, DH), blk(DH, nrows), blk(slots, DH), blk(DH, slots),
-            blk(nrows, 1), blk(BS, slots), blk(1, slots), blk(BS, 1),
+            blk(BS, H * DH), blk(slots, DH), blk(DH, slots),
+            blk(BS, H), blk(BS, slots), blk(1, slots), blk(BS, 1),
         ],
-        out_specs=[blk(nrows, DH), blk(nrows, 1), blk(DH, slots), blk(BS, 1)],
+        out_specs=[blk(BS, H * DH), blk(BS, H), blk(DH, slots), blk(BS, 1)],
         out_shape=[
-            jax.ShapeDtypeStruct((nblk, nrows, DH), f32),
-            jax.ShapeDtypeStruct((nblk, nrows, 1), f32),
+            jax.ShapeDtypeStruct((nblk, BS, H * DH), f32),
+            jax.ShapeDtypeStruct((nblk, BS, H), f32),
             jax.ShapeDtypeStruct((nblk, DH, slots), f32),
             jax.ShapeDtypeStruct((nblk, BS, 1), f32),
         ],
         scratch_shapes=[
+            pltpu.VMEM((nrows, DH), jnp.bfloat16), pltpu.VMEM((DH, nrows), jnp.bfloat16),
             pltpu.VMEM((BS, slots), f32), pltpu.VMEM((BS, slots), f32), pltpu.VMEM((nrows, slots), f32)
         ],
         compiler_params=pltpu.CompilerParams(
@@ -137,8 +166,8 @@
         ),
         cost_estimate=pl.CostEstimate(
             flops=flops, transcendentals=nblk * nrows * slots * 3,
-            bytes_accessed=nblk * (nrows * DH * 4 + slots * DH * 4 + nrows * DH * 4 + DH * slots * 4)),
-    )(qr, qt, k, kt, wcol, mass, spos, qpos)
+            bytes_accessed=nblk * (BS * H * DH * 6 + slots * DH * 4 + DH * slots * 4)),
+    )(q, k, kt, w, mass, spos, qpos)
 
 
 def butterfly_sum(value, axes):
@@ -194,31 +223,17 @@
     slot_lives = jnp.repeat(is_listed, BS).reshape(query_count, slot_count)
     never = jnp.iinfo(jnp.int32).max
     slot_limit = jnp.where(slot_lives, slot_positions, never).reshape(query_count, 1, slot_count)
-    query_hat, query_scale, normed_queries = query_norm(queries[0])
     first_pos = ctx_index * KD + KD - QD
     query_pos = (first_pos + jnp.arange(QD, dtype=jnp.int32)).reshape(query_count, BS, 1)
 
-    head_rows = (
-        normed_queries.reshape(query_count, BS, H, DH).transpose(0, 2, 1, 3).reshape(query_count, H * BS, DH)
-    )
-    head_cols = head_rows.transpose(0, 2, 1)
     key_cols = slot_keys.transpose(0, 2, 1)
-    weight_col = (
-        head_weights[0].astype(jnp.float32).reshape(query_count, BS, H).transpose(0, 2, 1)
-        .reshape(query_count, H * BS, 1)
-    )
     mass_rows = target_mass[0].reshape(query_count, BS, slot_count)
-    qg_rows, wg_rows, slot_grad_t, div_rows = score_blocks(
-        head_rows, head_cols, slot_keys, key_cols, weight_col, mass_rows, slot_limit, query_pos
+    grad_query_rows, weight_grads, slot_grad_t, div_rows = score_blocks(
+        queries[0].reshape(query_count, BS, H * DH), slot_keys, key_cols,
+        head_weights[0].reshape(query_count, BS, H), mass_rows, slot_limit, query_pos
     )
     divergence_total = jnp.sum(div_rows)
-    query_grads = qg_rows.reshape(query_count, H, BS, DH).transpose(0, 2, 1, 3).reshape(QD, H, DH)
-    weight_grads = wg_rows.reshape(query_count, H, BS).transpose(0, 2, 1).reshape(QD, H)
     grad_slots = slot_grad_t.transpose(0, 2, 1)
-
-    grad_query_rows = (
-        query_grads - query_hat * jnp.mean(query_grads * query_hat, -1, keepdims=True)
-    ) * query_scale
     slot_flat = grad_slots.reshape(request_count, BS * DH)
     outbound = jnp.dot(placement.T.astype(jnp.float32), slot_flat, precision=lax.Precision.HIGHEST)
     returned = lax.all_to_all(

time: 185 us -> 158 us (0.85)
  local copies, waits for them, and re-layouts: 48.3 us -> 13.8 us
  waiting for transfers between devices: 22.8 us -> 49.1 us
  other arithmetic: 30.7 us -> 11 us
  Pallas kernels: 51.9 us -> 61.3 us
  starting transfers between devices: 20.9 us -> 17 us
  matrix products: 6.23 us -> 2.65 us
    all_to_all x1, waiting for transfers between devices: 0.82 us -> 12.9 us  [per_device(): lax.all_to_all(sent_keys, 'ctx', split_axis=0, concat_axis=0, tiled=True)]
    pallas_call x1, Pallas kernels: 51.9 us -> 61.3 us  [score_blocks(): pl.pallas_call(score_kernel, grid=(nblk,), in_specs=[blk(BS, H * DH), blk...]
    mul x4 -> x0, local copies, waits for them, and re-layouts: 9.34 us -> none  [the longest x2 4.71 us: query_norm(): query_hat = query_float * query_scale]
    reshape x7 -> x0, local copies, waits for them, and re-layouts: 8.61 us -> none  [the longest x3 3.5 us: per_device(): weight_col = head_weights[0].astype(jnp.float32).reshape(query_count, BS,...]
    ppermute x5, waiting for transfers between devices: 2.67 us -> 11.2 us  [butterfly_sum(): value = value + lax.ppermute(value, axes, pairs)]
    reduce_sum x2 -> x0, other arithmetic: 5.87 us -> none  [the longest x1 3.66 us: per_device(): jnp.mean(query_grads * query_hat, -1, keepdims=True)]
    mul x1 -> x0, other arithmetic: 4.75 us -> none  [per_device(): (query_grads - query_hat * jnp.mean(query_grads * query_hat, -1, keepdims...]
    all_to_all x1, waiting for transfers between devices: 19.3 us -> 23.8 us  [per_device(): lax.all_to_all(outbound.reshape(ctx_count, capacity, BS * DH), 'ctx', spl...]
  transfers between devices with their start and end apart: 8 -> 8, of which waited for: 4 -> 8; matrix products, arithmetic and copies ran while one was open for 30% -> 7% of each run, Pallas kernels for 0% -> 0%
where the time goes in v7:
time: 158 us
  Pallas kernels  61.3 us (39%)
  waiting for transfers between devices  49.1 us (31%)
  starting transfers between devices  17 us (11%)
  local copies, waits for them, and re-layouts  13.8 us (9%)
  other arithmetic  11 us (7%)
  between operations  2.68 us (2%)
  matrix products  2.65 us (2%)
    pallas_call x1, Pallas kernels, score_blocks(): pl.pallas_call(score_kernel, grid=(nblk,), in_specs=[blk(BS, H * DH), blk...  61.3 us
    all_to_all x1, waiting for transfers between devices, per_device(): lax.all_to_all(outbound.reshape(ctx_count, capacity, BS * DH), 'ctx', spl...  23.8 us
    all_to_all x1, waiting for transfers between devices, per_device(): lax.all_to_all(sent_keys, 'ctx', split_axis=0, concat_axis=0, tiled=True)  12.9 us
    ppermute x5, waiting for transfers between devices, butterfly_sum(): value = value + lax.ppermute(value, axes, pairs)  11.2 us
    all_to_all x1, starting transfers between devices, per_device(): lax.all_to_all(request_table, 'ctx', split_axis=0, concat_axis=0, tiled=T...  6.33 us
    all_to_all x1, starting transfers between devices, per_device(): lax.all_to_all(sent_keys, 'ctx', split_axis=0, concat_axis=0, tiled=True)  3.8 us
    all_to_all x1, starting transfers between devices, per_device(): lax.all_to_all(outbound.reshape(ctx_count, capacity, BS * DH), 'ctx', spl...  3.74 us
  transfers between devices with their start and end apart: 8, of which 8 were waited for; matrix products, arithmetic and copies ran while one was open for 7% of the time, Pallas kernels for 0%

profile of v7, /device:TPU:0, one launch (start us, length us, event | category | flops | bytes accessed | tf_op | source)
XLA Modules:
  0.0 157.6 jit_solution(14754263607103785064)
XLA Ops:
  0.6 0.7 compare_and_fusion.1
  1.3 0.7 multiply_bitcast_fusion
  2.9 0.7 sub.60
  3.5 6.3 %all-to-all-start = ((s32[8,1,4]{2,1,0:T(1,128)}), s32[8,1,4]{2,1,0:T(1,128)S(1)}, u32[]{:S(2)}, u32[]{:S(2)}) async-start(s32[8,1,4]{2,1,0:T(1,128)} %bitcast), calls=%async_computation | async-start | bytes 8192 | tf_op jit(solution)/shard_map/all_to_all | solution.py:215
  10.0 1.1 convert_reduce_fusion
  11.1 1.3 multiply_reduce_fusion.2
  12.7 1.3 add_convert_fusion
  14.0 1.3 all-to-all-done
  15.6 1.4 gather_fusion
  17.0 3.8 %all-to-all-start.1 = ((bf16[8,4,64,128]{3,2,1,0:T(8,128)(2,1)}), bf16[8,4,64,128]{3,2,1,0:T(8,128)(2,1)S(1)}, u32[]{:S(2)}, u32[]{:S(2)}) async-start(bf16[8,4,64,128]{3,2,1,0:T(8,128)(2,1)} %bitcast.5), calls=%async_computation.1 | async-start | bytes 1048576 | tf_op jit(solution)/shard_map/all_to_all | solution.py:217
  21.3 0.7 copy.48
  22.7 0.6 add_select_fusion.spos_ref
  23.3 12.9 %all-to-all-done.1 = bf16[8,4,64,128]{3,2,1,0:T(8,128)(2,1)S(1)} async-done(((bf16[8,4,64,128]{3,2,1,0:T(8,128)(2,1)}), bf16[8,4,64,128]{3,2,1,0:T(8,128)(2,1)S(1)}, u32[]{:S(2)}, u32[]{:S(2)}) %all-to-all-start.1) | async-done | bytes 524320 | tf_op jit(solution)/shard_map/all_to_all | solution.py:217
  36.2 0.7 gather_fusion.1
  37.0 1.3 copy.47
  38.3 61.3 %shard_map.118 = (f32[2,64,4096]{2,1,0:T(8,128)}, f32[2,64,32]{2,1,0:T(8,128)}, f32[2,128,2048]{2,1,0:T(8,128)}, f32[2,64,1]{2,1,0:T(8,128)}) custom-call(bf16[2,64,4096]{2,1,0:T(8,128)(2,1)} %bitcast.47, bf16[2,2048,128]{2,1,0:T(8,128)(2,1)} %bitcast.41, bf16[2,128,2048]{2,1,0:T(8,128)(2,1)} %bitcast.43, bf16[2,64,32]{2,1,0:T(8,128)(2,1)} %bitcast.45, ...), custom_call_target="tpu_custom_call" | custom-call | flops 8589934592 | bytes 7340032 | tf_op jit(solution)/shard_map/pallas_call | solution.py:146
  99.6 2.9 %copy.50 = f32[2,2048,128]{2,1,0:T(8,128)} copy(f32[2,2048,128]{1,2,0:T(8,128)} %bitcast.42) | data formatting | bytes 4194304 | tf_op jit(solution)/shard_map/transpose | solution.py:236
  102.5 1.7 %reshape.469 = f32[64,8192,1]{1,0,2:T(8,128)S(1)} reshape(f32[2,2048,128]{2,1,0:T(8,128)} %copy.50) | data formatting | bytes 4194304 | tf_op jit(solution)/shard_map/reshape | solution.py:237
  104.2 2.2 %fusion.4 = f32[8,4,8192]{2,1,0:T(4,128)} fusion(f32[64,8192,1]{1,0,2:T(8,128)S(1)} %reshape.469, pred[8,4,64]{2,0,1:T(8,128)(4,1)S(1)} %compare_and_fusion), kind=kOutput, calls=%fused_computation.20 | convolution fusion | flops 201326592 | bytes 3147776 | tf_op jit(solution)/shard_map/dot_general | solution.py:238
  106.4 3.7 %all-to-all-start.2 = ((f32[8,4,8192]{2,1,0:T(4,128)}), f32[8,4,8192]{2,1,0:T(4,128)S(1)}, u32[]{:S(2)}, u32[]{:S(2)}) async-start(f32[8,4,8192]{2,1,0:T(4,128)} %fusion.4), calls=%async_computation.2 | async-start | bytes 2097152 | tf_op jit(solution)/shard_map/all_to_all | solution.py:239
  110.7 0.7 reduce.4
  112.1 0.6 compare_select_fusion.2
  112.7 23.8 %all-to-all-done.2 = f32[8,4,8192]{2,1,0:T(4,128)S(1)} async-done(((f32[8,4,8192]{2,1,0:T(4,128)}), f32[8,4,8192]{2,1,0:T(4,128)S(1)}, u32[]{:S(2)}, u32[]{:S(2)}) %all-to-all-start.2) | async-done | bytes 1048608 | tf_op jit(solution)/shard_map/all_to_all | solution.py:239
  138.2 1.1 collective-permute-done
  139.4 3.6 %collective-permute-done.1 = f32[260]{0:T(512)S(1)} collective-permute-done((f32[260]{0:T(512)S(1)}, f32[260]{0:T(512)S(1)}, u32[]{:S(2)}, u32[]{:S(2)}) %collective-permute-start.1) | collective-permute-done | bytes 1072 | tf_op jit(solution)/shard_map/ppermute | solution.py:182
  143.0 0.7 copy.52
  143.7 3.8 %collective-permute-done.2 = f32[260]{0:T(512)S(1)} collective-permute-done((f32[260]{0:T(512)S(1)}, f32[260]{0:T(512)S(1)}, u32[]{:S(2)}, u32[]{:S(2)}) %collective-permute-start.2) | collective-permute-done | bytes 1072 | tf_op jit(solution)/shard_map/ppermute | solution.py:182
  147.5 1.5 collective-permute-start.3
  149.1 2.0 %collective-permute-done.3 = f32[260]{0:T(512)S(1)} collective-permute-done((f32[260]{0:T(512)S(1)}, f32[260]{0:T(512)S(1)}, u32[]{:S(2)}, u32[]{:S(2)}) %collective-permute-start.3) | collective-permute-done | bytes 1072 | tf_op jit(solution)/shard_map/ppermute | solution.py:182
  151.1 1.5 collective-permute-start.4
  152.6 1.4 subtract_multiply_fusion
  154.0 0.7 collective-permute-done.4
  (66 shorter events, 6.8 us)
Async XLA Ops:
  0.6 20.6 %copy-start.4 = (bf16[1,128,32]{1,2,0:T(8,128)(2,1)S(1)}, bf16[1,128,32]{1,2,0:T(8,128)(2,1)}, u32[]{:S(2)}) copy-start(bf16[1,128,32]{1,2,0:T(8,128)(2,1)} %param.9) | copy-start | bytes 24580
  3.5 11.8 %all-to-all-start = ((s32[8,1,4]{2,1,0:T(1,128)}), s32[8,1,4]{2,1,0:T(1,128)S(1)}, u32[]{:S(2)}, u32[]{:S(2)}) async-start(s32[8,1,4]{2,1,0:T(1,128)} %bitcast), calls=%async_computation | async-start | bytes 8192 | tf_op jit(solution)/shard_map/all_to_all | solution.py:215
  17.0 19.2 %all-to-all-start.1 = ((bf16[8,4,64,128]{3,2,1,0:T(8,128)(2,1)}), bf16[8,4,64,128]{3,2,1,0:T(8,128)(2,1)S(1)}, u32[]{:S(2)}, u32[]{:S(2)}) async-start(bf16[8,4,64,128]{3,2,1,0:T(8,128)(2,1)} %bitcast.5), calls=%async_computation.1 | async-start | bytes 1048576 | tf_op jit(solution)/shard_map/all_to_all | solution.py:217
  36.9 1.3 copy-start.1
  104.2 7.2 %copy-start.3 = (f32[2,64,1]{2,1,0:T(8,128)S(1)}, f32[2,64,1]{2,1,0:T(8,128)}, u32[]{:S(2)}) copy-start(f32[2,64,1]{2,1,0:T(8,128)} %get-tuple-element.11) | copy-start | bytes 1540
  106.4 30.1 %all-to-all-start.2 = ((f32[8,4,8192]{2,1,0:T(4,128)}), f32[8,4,8192]{2,1,0:T(4,128)S(1)}, u32[]{:S(2)}, u32[]{:S(2)}) async-start(f32[8,4,8192]{2,1,0:T(4,128)} %fusion.4), calls=%async_computation.2 | async-start | bytes 2097152 | tf_op jit(solution)/shard_map/all_to_all | solution.py:239
  112.7 24.7 %copy-start = (bf16[1,1024,128]{2,1,0:T(8,128)(2,1)S(1)}, bf16[1,1024,128]{2,1,0:T(8,128)(2,1)}, u32[]{:S(2)}) copy-start(bf16[1,1024,128]{2,1,0:T(8,128)(2,1)} %param.8) | copy-start | bytes 786436
  112.7 24.7 %copy-start.5 = (f32[128]{0:T(128)S(1)}, f32[128]{0:T(128)}, u32[]{:S(2)}) copy-start(f32[128]{0:T(128)} %param.12) | copy-start | bytes 1540
  136.9 6.2 %copy-start.2 = (f32[2,64,32]{2,1,0:T(8,128)S(1)}, f32[2,64,32]{2,1,0:T(8,128)}, u32[]{:S(2)}) copy-start(f32[2,64,32]{2,1,0:T(8,128)} %get-tuple-element.13) | copy-start | bytes 49156
  138.1 1.2 collective-permute-start
  139.4 3.6 %collective-permute-start.1 = (f32[260]{0:T(512)S(1)}, f32[260]{0:T(512)S(1)}, u32[]{:S(2)}, u32[]{:S(2)}) collective-permute-start(f32[260]{0:T(512)S(1)} %fusion.12), channel_id=1, source_target_pairs={{0,2},{1,3},{2,0},{3,1},{4,6},{5,7},{6,4},{7,5},{8,10},{9,11},{10,... | collective-permute-start | bytes 3128 | tf_op jit(solution)/shard_map/ppermute | solution.py:182
  143.0 4.5 %collective-permute-start.2 = (f32[260]{0:T(512)S(1)}, f32[260]{0:T(512)S(1)}, u32[]{:S(2)}, u32[]{:S(2)}) collective-permute-start(f32[260]{0:T(512)S(1)} %add.203), channel_id=1, source_target_pairs={{0,4},{1,5},{2,6},{3,7},{4,0},{5,1},{6,2},{7,3},{8,12},{9,13},{10,... | collective-permute-start | bytes 3128 | tf_op jit(solution)/shard_map/ppermute | solution.py:182
  147.5 3.6 %collective-permute-start.3 = (f32[260]{0:T(512)S(1)}, f32[260]{0:T(512)S(1)}, u32[]{:S(2)}, u32[]{:S(2)}) collective-permute-start(f32[260]{0:T(512)S(1)} %add.204), channel_id=1, source_target_pairs={{0,8},{1,9},{2,10},{3,11},{4,12},{5,13},{6,14},{7,15},{8,0},{9,1},... | collective-permute-start | bytes 3128 | tf_op jit(solution)/shard_map/ppermute | solution.py:182
  151.1 3.6 %collective-permute-start.4 = (f32[260]{0:T(512)S(1)}, f32[260]{0:T(512)S(1)}, u32[]{:S(2)}, u32[]{:S(2)}) collective-permute-start(f32[260]{0:T(512)S(1)} %add.205), channel_id=1, source_target_pairs={{0,16},{1,17},{2,18},{3,19},{4,20},{5,21},{6,22},{7,23},{8,24},{9,... | collective-permute-start | bytes 3128 | tf_op jit(solution)/shard_map/ppermute | solution.py:182

commit v8 on v7

--- a/solution.py
+++ b/solution.py
@@ -64,6 +64,7 @@
         return jnp.concatenate([w4[:, hh:hh + 1] for hh in range(HEAD_GROUP)], 0)
 
     mix_ref[...] = jnp.zeros_like(mix_ref)
+    neg_log2_root = -inv_root * 1.4426950408889634
 
     def first_pass(g, carry):
         r0 = pl.multiple_of(g * rows, rows)
@@ -71,8 +72,9 @@
         wcol = group_weights(g)
         for c in range(chunks):
             cs = slice(c * CHUNK, (c + 1) * CHUNK)
-            s = jnp.dot(q, kt_ref[:, cs], preferred_element_type=f32) * inv_root
-            sp = jnp.maximum(s, 0.0) + jnp.log1p(jnp.exp(-jnp.abs(s)))
+            raw = jnp.dot(q, kt_ref[:, cs], preferred_element_type=f32)
+            tail = jnp.exp2(jnp.abs(raw) * neg_log2_root)
+            sp = jnp.maximum(raw * inv_root, 0.0) + jnp.log(1.0 + tail)
             sp_ref[pl.ds(r0, rows), cs] = sp
             ws = (wcol * sp).reshape(HEAD_GROUP, BS, CHUNK)
             mix_ref[:, cs] += jnp.sum(ws, 0)

time: 158 us -> 150 us (0.949)
  Pallas kernels: 61.3 us -> 53.3 us
    pallas_call x1, Pallas kernels: 61.3 us -> 53.3 us  [score_blocks(): pl.pallas_call(score_kernel, grid=(nblk,), in_specs=[blk(BS, H * DH), blk...]
  transfers between devices with their start and end apart: 8 -> 8, of which waited for: 8 -> 8; matrix products, arithmetic and copies ran while one was open for 7% -> 8% of each run, Pallas kernels for 0% -> 0%
where the time goes in v8:
time: 150 us
  Pallas kernels  53.3 us (36%)
  waiting for transfers between devices  49.3 us (33%)
  starting transfers between devices  16.8 us (11%)
  local copies, waits for them, and re-layouts  13.8 us (9%)
  other arithmetic  11 us (7%)
  between operations  2.68 us (2%)
  matrix products  2.65 us (2%)
    pallas_call x1, Pallas kernels, score_blocks(): pl.pallas_call(score_kernel, grid=(nblk,), in_specs=[blk(BS, H * DH), blk...  53.3 us
    all_to_all x1, waiting for transfers between devices, per_device(): lax.all_to_all(outbound.reshape(ctx_count, capacity, BS * DH), 'ctx', spl...  23.9 us
    all_to_all x1, waiting for transfers between devices, per_device(): lax.all_to_all(sent_keys, 'ctx', split_axis=0, concat_axis=0, tiled=True)  12.9 us
    ppermute x5, waiting for transfers between devices, butterfly_sum(): value = value + lax.ppermute(value, axes, pairs)  11.2 us
    all_to_all x1, starting transfers between devices, per_device(): lax.all_to_all(request_table, 'ctx', split_axis=0, concat_axis=0, tiled=T...  6.33 us
    all_to_all x1, starting transfers between devices, per_device(): lax.all_to_all(sent_keys, 'ctx', split_axis=0, concat_axis=0, tiled=True)  3.8 us
    all_to_all x1, starting transfers between devices, per_device(): lax.all_to_all(outbound.reshape(ctx_count, capacity, BS * DH), 'ctx', spl...  3.56 us
    ppermute x5, starting transfers between devices, butterfly_sum(): value = value + lax.ppermute(value, axes, pairs)  3.16 us
  transfers between devices with their start and end apart: 8, of which 8 were waited for; matrix products, arithmetic and copies ran while one was open for 8% of the time, Pallas kernels for 0%

profile of v8, /device:TPU:0, one launch (start us, length us, event | category | flops | bytes accessed | tf_op | source)
XLA Modules:
  0.0 149.5 jit_solution(14513509678066641842)
XLA Ops:
  0.6 0.7 compare_and_fusion.1
  1.3 0.7 multiply_bitcast_fusion
  2.9 0.7 sub.60
  3.5 6.3 %all-to-all-start = ((s32[8,1,4]{2,1,0:T(1,128)}), s32[8,1,4]{2,1,0:T(1,128)S(1)}, u32[]{:S(2)}, u32[]{:S(2)}) async-start(s32[8,1,4]{2,1,0:T(1,128)} %bitcast), calls=%async_computation | async-start | bytes 8192 | tf_op jit(solution)/shard_map/all_to_all | solution.py:217
  10.0 1.1 convert_reduce_fusion
  11.1 1.3 multiply_reduce_fusion.2
  12.7 1.3 add_convert_fusion
  14.0 1.3 all-to-all-done
  15.6 1.4 gather_fusion
  17.0 3.8 %all-to-all-start.1 = ((bf16[8,4,64,128]{3,2,1,0:T(8,128)(2,1)}), bf16[8,4,64,128]{3,2,1,0:T(8,128)(2,1)S(1)}, u32[]{:S(2)}, u32[]{:S(2)}) async-start(bf16[8,4,64,128]{3,2,1,0:T(8,128)(2,1)} %bitcast.5), calls=%async_computation.1 | async-start | bytes 1048576 | tf_op jit(solution)/shard_map/all_to_all | solution.py:219
  21.3 0.7 copy.48
  23.3 12.9 %all-to-all-done.1 = bf16[8,4,64,128]{3,2,1,0:T(8,128)(2,1)S(1)} async-done(((bf16[8,4,64,128]{3,2,1,0:T(8,128)(2,1)}), bf16[8,4,64,128]{3,2,1,0:T(8,128)(2,1)S(1)}, u32[]{:S(2)}, u32[]{:S(2)}) %all-to-all-start.1) | async-done | bytes 524320 | tf_op jit(solution)/shard_map/all_to_all | solution.py:219
  36.2 0.7 gather_fusion.1
  37.0 1.3 copy.47
  38.3 53.3 %shard_map.118 = (f32[2,64,4096]{2,1,0:T(8,128)}, f32[2,64,32]{2,1,0:T(8,128)}, f32[2,128,2048]{2,1,0:T(8,128)}, f32[2,64,1]{2,1,0:T(8,128)}) custom-call(bf16[2,64,4096]{2,1,0:T(8,128)(2,1)} %bitcast.47, bf16[2,2048,128]{2,1,0:T(8,128)(2,1)} %bitcast.41, bf16[2,128,2048]{2,1,0:T(8,128)(2,1)} %bitcast.43, bf16[2,64,32]{2,1,0:T(8,128)(2,1)} %bitcast.45, ...), custom_call_target="tpu_custom_call" | custom-call | flops 8589934592 | bytes 7340032 | tf_op jit(solution)/shard_map/pallas_call | solution.py:148
  91.6 2.9 %copy.50 = f32[2,2048,128]{2,1,0:T(8,128)} copy(f32[2,2048,128]{1,2,0:T(8,128)} %bitcast.42) | data formatting | bytes 4194304 | tf_op jit(solution)/shard_map/transpose | solution.py:238
  94.4 1.7 %reshape.469 = f32[64,8192,1]{1,0,2:T(8,128)S(1)} reshape(f32[2,2048,128]{2,1,0:T(8,128)} %copy.50) | data formatting | bytes 4194304 | tf_op jit(solution)/shard_map/reshape | solution.py:239
  96.2 2.2 %fusion.4 = f32[8,4,8192]{2,1,0:T(4,128)} fusion(f32[64,8192,1]{1,0,2:T(8,128)S(1)} %reshape.469, pred[8,4,64]{2,0,1:T(8,128)(4,1)S(1)} %compare_and_fusion), kind=kOutput, calls=%fused_computation.20 | convolution fusion | flops 201326592 | bytes 3147776 | tf_op jit(solution)/shard_map/dot_general | solution.py:240
  98.4 3.6 %all-to-all-start.2 = ((f32[8,4,8192]{2,1,0:T(4,128)}), f32[8,4,8192]{2,1,0:T(4,128)S(1)}, u32[]{:S(2)}, u32[]{:S(2)}) async-start(f32[8,4,8192]{2,1,0:T(4,128)} %fusion.4), calls=%async_computation.2 | async-start | bytes 2097152 | tf_op jit(solution)/shard_map/all_to_all | solution.py:241
  102.5 0.7 reduce.4
  103.8 0.6 compare_select_fusion.2
  104.5 23.9 %all-to-all-done.2 = f32[8,4,8192]{2,1,0:T(4,128)S(1)} async-done(((f32[8,4,8192]{2,1,0:T(4,128)}), f32[8,4,8192]{2,1,0:T(4,128)S(1)}, u32[]{:S(2)}, u32[]{:S(2)}) %all-to-all-start.2) | async-done | bytes 1048608 | tf_op jit(solution)/shard_map/all_to_all | solution.py:241
  129.4 0.6 multiply_reduce_fusion
  130.2 1.1 collective-permute-done
  131.4 3.6 %collective-permute-done.1 = f32[260]{0:T(512)S(1)} collective-permute-done((f32[260]{0:T(512)S(1)}, f32[260]{0:T(512)S(1)}, u32[]{:S(2)}, u32[]{:S(2)}) %collective-permute-start.1) | collective-permute-done | bytes 1072 | tf_op jit(solution)/shard_map/ppermute | solution.py:184
  135.0 0.7 copy.52
  135.7 3.8 %collective-permute-done.2 = f32[260]{0:T(512)S(1)} collective-permute-done((f32[260]{0:T(512)S(1)}, f32[260]{0:T(512)S(1)}, u32[]{:S(2)}, u32[]{:S(2)}) %collective-permute-start.2) | collective-permute-done | bytes 1072 | tf_op jit(solution)/shard_map/ppermute | solution.py:184
  139.5 1.5 %collective-permute-start.3 = (f32[260]{0:T(512)S(1)}, f32[260]{0:T(512)S(1)}, u32[]{:S(2)}, u32[]{:S(2)}) collective-permute-start(f32[260]{0:T(512)S(1)} %add.204), channel_id=1, source_target_pairs={{0,8},{1,9},{2,10},{3,11},{4,12},{5,13},{6,14},{7,15},{8,0},{9,1},... | collective-permute-start | bytes 3128 | tf_op jit(solution)/shard_map/ppermute | solution.py:184
  141.0 2.0 %collective-permute-done.3 = f32[260]{0:T(512)S(1)} collective-permute-done((f32[260]{0:T(512)S(1)}, f32[260]{0:T(512)S(1)}, u32[]{:S(2)}, u32[]{:S(2)}) %collective-permute-start.3) | collective-permute-done | bytes 1072 | tf_op jit(solution)/shard_map/ppermute | solution.py:184
  143.0 1.5 %collective-permute-start.4 = (f32[260]{0:T(512)S(1)}, f32[260]{0:T(512)S(1)}, u32[]{:S(2)}, u32[]{:S(2)}) collective-permute-start(f32[260]{0:T(512)S(1)} %add.205), channel_id=1, source_target_pairs={{0,16},{1,17},{2,18},{3,19},{4,20},{5,21},{6,22},{7,23},{8,24},{9,... | collective-permute-start | bytes 3128 | tf_op jit(solution)/shard_map/ppermute | solution.py:184
  144.6 1.4 subtract_multiply_fusion
  146.0 0.7 collective-permute-done.4
  (66 shorter events, 6.8 us)
Async XLA Ops:
  0.6 20.6 %copy-start.4 = (bf16[1,128,32]{1,2,0:T(8,128)(2,1)S(1)}, bf16[1,128,32]{1,2,0:T(8,128)(2,1)}, u32[]{:S(2)}) copy-start(bf16[1,128,32]{1,2,0:T(8,128)(2,1)} %param.9) | copy-start | bytes 24580
  3.5 11.8 %all-to-all-start = ((s32[8,1,4]{2,1,0:T(1,128)}), s32[8,1,4]{2,1,0:T(1,128)S(1)}, u32[]{:S(2)}, u32[]{:S(2)}) async-start(s32[8,1,4]{2,1,0:T(1,128)} %bitcast), calls=%async_computation | async-start | bytes 8192 | tf_op jit(solution)/shard_map/all_to_all | solution.py:217
  17.0 19.2 %all-to-all-start.1 = ((bf16[8,4,64,128]{3,2,1,0:T(8,128)(2,1)}), bf16[8,4,64,128]{3,2,1,0:T(8,128)(2,1)S(1)}, u32[]{:S(2)}, u32[]{:S(2)}) async-start(bf16[8,4,64,128]{3,2,1,0:T(8,128)(2,1)} %bitcast.5), calls=%async_computation.1 | async-start | bytes 1048576 | tf_op jit(solution)/shard_map/all_to_all | solution.py:219
  36.9 1.3 copy-start.1
  96.2 7.0 %copy-start.3 = (f32[2,64,1]{2,1,0:T(8,128)S(1)}, f32[2,64,1]{2,1,0:T(8,128)}, u32[]{:S(2)}) copy-start(f32[2,64,1]{2,1,0:T(8,128)} %get-tuple-element.11) | copy-start | bytes 1540
  98.4 30.1 %all-to-all-start.2 = ((f32[8,4,8192]{2,1,0:T(4,128)}), f32[8,4,8192]{2,1,0:T(4,128)S(1)}, u32[]{:S(2)}, u32[]{:S(2)}) async-start(f32[8,4,8192]{2,1,0:T(4,128)} %fusion.4), calls=%async_computation.2 | async-start | bytes 2097152 | tf_op jit(solution)/shard_map/all_to_all | solution.py:241
  104.5 24.9 %copy-start = (bf16[1,1024,128]{2,1,0:T(8,128)(2,1)S(1)}, bf16[1,1024,128]{2,1,0:T(8,128)(2,1)}, u32[]{:S(2)}) copy-start(bf16[1,1024,128]{2,1,0:T(8,128)(2,1)} %param.8) | copy-start | bytes 786436
  104.5 24.9 %copy-start.5 = (f32[128]{0:T(128)S(1)}, f32[128]{0:T(128)}, u32[]{:S(2)}) copy-start(f32[128]{0:T(128)} %param.12) | copy-start | bytes 1540
  128.8 6.2 %copy-start.2 = (f32[2,64,32]{2,1,0:T(8,128)S(1)}, f32[2,64,32]{2,1,0:T(8,128)}, u32[]{:S(2)}) copy-start(f32[2,64,32]{2,1,0:T(8,128)} %get-tuple-element.13) | copy-start | bytes 49156
  130.1 1.2 collective-permute-start
  131.3 3.6 %collective-permute-start.1 = (f32[260]{0:T(512)S(1)}, f32[260]{0:T(512)S(1)}, u32[]{:S(2)}, u32[]{:S(2)}) collective-permute-start(f32[260]{0:T(512)S(1)} %fusion.12), channel_id=1, source_target_pairs={{0,2},{1,3},{2,0},{3,1},{4,6},{5,7},{6,4},{7,5},{8,10},{9,11},{10,... | collective-permute-start | bytes 3128 | tf_op jit(solution)/shard_map/ppermute | solution.py:184
  135.0 4.5 %collective-permute-start.2 = (f32[260]{0:T(512)S(1)}, f32[260]{0:T(512)S(1)}, u32[]{:S(2)}, u32[]{:S(2)}) collective-permute-start(f32[260]{0:T(512)S(1)} %add.203), channel_id=1, source_target_pairs={{0,4},{1,5},{2,6},{3,7},{4,0},{5,1},{6,2},{7,3},{8,12},{9,13},{10,... | collective-permute-start | bytes 3128 | tf_op jit(solution)/shard_map/ppermute | solution.py:184
  139.5 3.6 %collective-permute-start.3 = (f32[260]{0:T(512)S(1)}, f32[260]{0:T(512)S(1)}, u32[]{:S(2)}, u32[]{:S(2)}) collective-permute-start(f32[260]{0:T(512)S(1)} %add.204), channel_id=1, source_target_pairs={{0,8},{1,9},{2,10},{3,11},{4,12},{5,13},{6,14},{7,15},{8,0},{9,1},... | collective-permute-start | bytes 3128 | tf_op jit(solution)/shard_map/ppermute | solution.py:184
  143.0 3.6 %collective-permute-start.4 = (f32[260]{0:T(512)S(1)}, f32[260]{0:T(512)S(1)}, u32[]{:S(2)}, u32[]{:S(2)}) collective-permute-start(f32[260]{0:T(512)S(1)} %add.205), channel_id=1, source_target_pairs={{0,16},{1,17},{2,18},{3,19},{4,20},{5,21},{6,22},{7,23},{8,24},{9,... | collective-permute-start | bytes 3128 | tf_op jit(solution)/shard_map/ppermute | solution.py:184

commit v9 on v8

--- a/solution.py
+++ b/solution.py
@@ -16,8 +16,8 @@
 epsilon = 1e-06
 soft_cap = 20.0
 
-HEAD_GROUP = 4
-CHUNK = 512
+HEAD_GROUP = 32
+CHUNK = 256
 
 
 def key_norm(key_rows, key_gain, key_bias):

time: 150 us -> 129 us (0.86)
  Pallas kernels: 53.3 us -> 32.6 us
    pallas_call x1, Pallas kernels: 53.3 us -> 32.6 us  [score_blocks(): pl.pallas_call(score_kernel, grid=(nblk,), in_specs=[blk(BS, H * DH), blk...]
  transfers between devices with their start and end apart: 8 -> 8, of which waited for: 8 -> 8; matrix products, arithmetic and copies ran while one was open for 8% -> 9% of each run, Pallas kernels for 0% -> 0%
where the time goes in v9:
time: 129 us
  waiting for transfers between devices  49.3 us (38%)
  Pallas kernels  32.6 us (25%)
  starting transfers between devices  16.8 us (13%)
  local copies, waits for them, and re-layouts  13.8 us (11%)
  other arithmetic  11 us (9%)
  between operations  2.69 us (2%)
  matrix products  2.65 us (2%)
    pallas_call x1, Pallas kernels, score_blocks(): pl.pallas_call(score_kernel, grid=(nblk,), in_specs=[blk(BS, H * DH), blk...  32.6 us
    all_to_all x1, waiting for transfers between devices, per_device(): lax.all_to_all(outbound.reshape(ctx_count, capacity, BS * DH), 'ctx', spl...  23.9 us
    all_to_all x1, waiting for transfers between devices, per_device(): lax.all_to_all(sent_keys, 'ctx', split_axis=0, concat_axis=0, tiled=True)  12.9 us
    ppermute x5, waiting for transfers between devices, butterfly_sum(): value = value + lax.ppermute(value, axes, pairs)  11.2 us
    all_to_all x1, starting transfers between devices, per_device(): lax.all_to_all(request_table, 'ctx', split_axis=0, concat_axis=0, tiled=T...  6.33 us
    all_to_all x1, starting transfers between devices, per_device(): lax.all_to_all(sent_keys, 'ctx', split_axis=0, concat_axis=0, tiled=True)  3.8 us
    all_to_all x1, starting transfers between devices, per_device(): lax.all_to_all(outbound.reshape(ctx_count, capacity, BS * DH), 'ctx', spl...  3.56 us
    ppermute x5, starting transfers between devices, butterfly_sum(): value = value + lax.ppermute(value, axes, pairs)  3.16 us
  transfers between devices with their start and end apart: 8, of which 8 were waited for; matrix products, arithmetic and copies ran while one was open for 9% of the time, Pallas kernels for 0%

profile of v9, /device:TPU:0, one launch (start us, length us, event | category | flops | bytes accessed | tf_op | source)
XLA Modules:
  0.0 128.9 jit_solution(10168320081310980044)
XLA Ops:
  0.6 0.7 compare_and_fusion.1
  1.3 0.7 multiply_bitcast_fusion
  2.9 0.7 sub.60
  3.5 6.3 %all-to-all-start = ((s32[8,1,4]{2,1,0:T(1,128)}), s32[8,1,4]{2,1,0:T(1,128)S(1)}, u32[]{:S(2)}, u32[]{:S(2)}) async-start(s32[8,1,4]{2,1,0:T(1,128)} %bitcast), calls=%async_computation | async-start | bytes 8192 | tf_op jit(solution)/shard_map/all_to_all | solution.py:217
  10.0 1.1 convert_reduce_fusion
  11.1 1.3 %multiply_reduce_fusion.2 = f32[1024]{0:T(1024)S(1)} fusion(bf16[1,1024,128]{2,1,0:T(8,128)(2,1)} %param.8, f32[1024]{0:T(1024)S(1)} %broadcast_multiply_fusion.2), kind=kLoop, calls=%fused_computation.7 | loop fusion | flops 523264 | bytes 270336 | tf_op jit(solution)/shard_map/reduce_sum | solution.py:27
  12.7 1.3 %add_convert_fusion = bf16[16,64,128]{2,1,0:T(8,128)(2,1)S(1)} fusion(f32[128]{0:T(128)} %param.13, f32[128]{0:T(128)} %param.12, f32[16,64]{1,0:T(8,128)S(1)} %rsqrt.13, f32[16,64]{1,0:T(8,128)S(1)} %div.38, bf16[16,64,128]{2,1,0:T(8,128)(2,1)} %bitcast.38), kind=kLoop, calls=%fused_computation.6 | loop fusion | flops 786432 | bytes 533504 | tf_op jit(solution)/shard_map/convert_element_type | solution.py:30
  14.0 1.3 %all-to-all-done = s32[8,1,4]{2,1,0:T(1,128)S(1)} async-done(((s32[8,1,4]{2,1,0:T(1,128)}), s32[8,1,4]{2,1,0:T(1,128)S(1)}, u32[]{:S(2)}, u32[]{:S(2)}) %all-to-all-start) | async-done | bytes 160 | tf_op jit(solution)/shard_map/all_to_all | solution.py:217
  15.6 1.4 %gather_fusion = bf16[32,64,128]{2,1,0:T(8,128)(2,1)} fusion(bf16[16,64,128]{2,1,0:T(8,128)(2,1)S(1)} %add_convert_fusion, s32[1024]{0:T(1024)S(1)} %pad_clamp_fusion.1), kind=kCustom, calls=%fused_computation | custom fusion | bytes 1048704 | tf_op jit(solution)/shard_map/gather | solution.py:218
  17.0 3.8 %all-to-all-start.1 = ((bf16[8,4,64,128]{3,2,1,0:T(8,128)(2,1)}), bf16[8,4,64,128]{3,2,1,0:T(8,128)(2,1)S(1)}, u32[]{:S(2)}, u32[]{:S(2)}) async-start(bf16[8,4,64,128]{3,2,1,0:T(8,128)(2,1)} %bitcast.5), calls=%async_computation.1 | async-start | bytes 1048576 | tf_op jit(solution)/shard_map/all_to_all | solution.py:219
  21.3 0.7 copy.48
  23.3 12.9 %all-to-all-done.1 = bf16[8,4,64,128]{3,2,1,0:T(8,128)(2,1)S(1)} async-done(((bf16[8,4,64,128]{3,2,1,0:T(8,128)(2,1)}), bf16[8,4,64,128]{3,2,1,0:T(8,128)(2,1)S(1)}, u32[]{:S(2)}, u32[]{:S(2)}) %all-to-all-start.1) | async-done | bytes 524320 | tf_op jit(solution)/shard_map/all_to_all | solution.py:219
  36.2 0.7 gather_fusion.1
  37.0 1.3 %copy.47 = bf16[2,2048,128]{1,2,0:T(8,128)(2,1)} copy(bf16[2,2048,128]{2,1,0:T(8,128)(2,1)S(1)} %bitcast.40) | data formatting | bytes 2097152 | tf_op jit(solution)/shard_map/reshape | solution.py:221
  38.3 32.6 %shard_map.118 = (f32[2,64,4096]{2,1,0:T(8,128)}, f32[2,64,32]{2,1,0:T(8,128)}, f32[2,128,2048]{2,1,0:T(8,128)}, f32[2,64,1]{2,1,0:T(8,128)}) custom-call(bf16[2,64,4096]{2,1,0:T(8,128)(2,1)} %bitcast.47, bf16[2,2048,128]{2,1,0:T(8,128)(2,1)} %bitcast.41, bf16[2,128,2048]{2,1,0:T(8,128)(2,1)} %bitcast.43, bf16[2,64,32]{2,1,0:T(8,128)(2,1)} %bitcast.45, ...), custom_call_target="tpu_custom_call" | custom-call | flops 8589934592 | bytes 7340032 | tf_op jit(solution)/shard_map/pallas_call | solution.py:148
  70.9 2.9 %copy.50 = f32[2,2048,128]{2,1,0:T(8,128)} copy(f32[2,2048,128]{1,2,0:T(8,128)} %bitcast.42) | data formatting | bytes 4194304 | tf_op jit(solution)/shard_map/transpose | solution.py:238
  73.8 1.7 %reshape.469 = f32[64,8192,1]{1,0,2:T(8,128)S(1)} reshape(f32[2,2048,128]{2,1,0:T(8,128)} %copy.50) | data formatting | bytes 4194304 | tf_op jit(solution)/shard_map/reshape | solution.py:239
  75.6 2.2 %fusion.4 = f32[8,4,8192]{2,1,0:T(4,128)} fusion(f32[64,8192,1]{1,0,2:T(8,128)S(1)} %reshape.469, pred[8,4,64]{2,0,1:T(8,128)(4,1)S(1)} %compare_and_fusion), kind=kOutput, calls=%fused_computation.20 | convolution fusion | flops 201326592 | bytes 3147776 | tf_op jit(solution)/shard_map/dot_general | solution.py:240
  77.7 3.6 %all-to-all-start.2 = ((f32[8,4,8192]{2,1,0:T(4,128)}), f32[8,4,8192]{2,1,0:T(4,128)S(1)}, u32[]{:S(2)}, u32[]{:S(2)}) async-start(f32[8,4,8192]{2,1,0:T(4,128)} %fusion.4), calls=%async_computation.2 | async-start | bytes 2097152 | tf_op jit(solution)/shard_map/all_to_all | solution.py:241
  81.8 0.7 reduce.4
  83.2 0.6 compare_select_fusion.2
  83.9 23.9 %all-to-all-done.2 = f32[8,4,8192]{2,1,0:T(4,128)S(1)} async-done(((f32[8,4,8192]{2,1,0:T(4,128)}), f32[8,4,8192]{2,1,0:T(4,128)S(1)}, u32[]{:S(2)}, u32[]{:S(2)}) %all-to-all-start.2) | async-done | bytes 1048608 | tf_op jit(solution)/shard_map/all_to_all | solution.py:241
  108.8 0.6 multiply_reduce_fusion
  109.5 1.1 collective-permute-done
  110.8 3.6 %collective-permute-done.1 = f32[260]{0:T(512)S(1)} collective-permute-done((f32[260]{0:T(512)S(1)}, f32[260]{0:T(512)S(1)}, u32[]{:S(2)}, u32[]{:S(2)}) %collective-permute-start.1) | collective-permute-done | bytes 1072 | tf_op jit(solution)/shard_map/ppermute | solution.py:184
  114.3 0.7 copy.52
  115.0 3.8 %collective-permute-done.2 = f32[260]{0:T(512)S(1)} collective-permute-done((f32[260]{0:T(512)S(1)}, f32[260]{0:T(512)S(1)}, u32[]{:S(2)}, u32[]{:S(2)}) %collective-permute-start.2) | collective-permute-done | bytes 1072 | tf_op jit(solution)/shard_map/ppermute | solution.py:184
  118.8 1.5 %collective-permute-start.3 = (f32[260]{0:T(512)S(1)}, f32[260]{0:T(512)S(1)}, u32[]{:S(2)}, u32[]{:S(2)}) collective-permute-start(f32[260]{0:T(512)S(1)} %add.204), channel_id=1, source_target_pairs={{0,8},{1,9},{2,10},{3,11},{4,12},{5,13},{6,14},{7,15},{8,0},{9,1},... | collective-permute-start | bytes 3128 | tf_op jit(solution)/shard_map/ppermute | solution.py:184
  120.4 2.0 %collective-permute-done.3 = f32[260]{0:T(512)S(1)} collective-permute-done((f32[260]{0:T(512)S(1)}, f32[260]{0:T(512)S(1)}, u32[]{:S(2)}, u32[]{:S(2)}) %collective-permute-start.3) | collective-permute-done | bytes 1072 | tf_op jit(solution)/shard_map/ppermute | solution.py:184
  122.4 1.5 %collective-permute-start.4 = (f32[260]{0:T(512)S(1)}, f32[260]{0:T(512)S(1)}, u32[]{:S(2)}, u32[]{:S(2)}) collective-permute-start(f32[260]{0:T(512)S(1)} %add.205), channel_id=1, source_target_pairs={{0,16},{1,17},{2,18},{3,19},{4,20},{5,21},{6,22},{7,23},{8,24},{9,... | collective-permute-start | bytes 3128 | tf_op jit(solution)/shard_map/ppermute | solution.py:184
  123.9 1.4 %subtract_multiply_fusion = f32[1,1024,128]{2,1,0:T(8,128)} fusion(f32[1,1024,128]{2,1,0:T(8,128)S(1)} %reshape.450, bf16[1,1024,128]{2,1,0:T(8,128)(2,1)S(1)} %copy-done, f32[1024]{0:T(1024)S(1)} %get-tuple-element.58, f32[1024]{0:T(1024)S(1)} %add_rsqrt_fusion, f32[1024]{0:T(1024)S(1)} %broadcast_multiply_fusion.2, f32[1024]{0:T(1024)S(1)} %get-tuple-element.59, ...), kind=kLoop, calls=%fused_computation.3 | loop fusion | flops 1048576 | bytes 1327616 | tf_op jit(solution)/shard_map/mul | solution.py:254
  125.3 0.7 collective-permute-done.4
  (66 shorter events, 6.8 us)
Async XLA Ops:
  0.6 20.6 %copy-start.4 = (bf16[1,128,32]{1,2,0:T(8,128)(2,1)S(1)}, bf16[1,128,32]{1,2,0:T(8,128)(2,1)}, u32[]{:S(2)}) copy-start(bf16[1,128,32]{1,2,0:T(8,128)(2,1)} %param.9) | copy-start | bytes 24580
  3.5 11.8 %all-to-all-start = ((s32[8,1,4]{2,1,0:T(1,128)}), s32[8,1,4]{2,1,0:T(1,128)S(1)}, u32[]{:S(2)}, u32[]{:S(2)}) async-start(s32[8,1,4]{2,1,0:T(1,128)} %bitcast), calls=%async_computation | async-start | bytes 8192 | tf_op jit(solution)/shard_map/all_to_all | solution.py:217
  17.0 19.2 %all-to-all-start.1 = ((bf16[8,4,64,128]{3,2,1,0:T(8,128)(2,1)}), bf16[8,4,64,128]{3,2,1,0:T(8,128)(2,1)S(1)}, u32[]{:S(2)}, u32[]{:S(2)}) async-start(bf16[8,4,64,128]{3,2,1,0:T(8,128)(2,1)} %bitcast.5), calls=%async_computation.1 | async-start | bytes 1048576 | tf_op jit(solution)/shard_map/all_to_all | solution.py:219
  36.9 1.3 %copy-start.1 = (bf16[64,64,128]{2,1,0:T(8,128)(2,1)}, bf16[64,64,128]{2,1,0:T(8,128)(2,1)S(1)}, u32[]{:S(2)}) copy-start(bf16[64,64,128]{2,1,0:T(8,128)(2,1)S(1)} %gather_fusion.1) | copy-start | bytes 3145732
  75.6 7.0 %copy-start.3 = (f32[2,64,1]{2,1,0:T(8,128)S(1)}, f32[2,64,1]{2,1,0:T(8,128)}, u32[]{:S(2)}) copy-start(f32[2,64,1]{2,1,0:T(8,128)} %get-tuple-element.11) | copy-start | bytes 1540
  77.7 30.1 %all-to-all-start.2 = ((f32[8,4,8192]{2,1,0:T(4,128)}), f32[8,4,8192]{2,1,0:T(4,128)S(1)}, u32[]{:S(2)}, u32[]{:S(2)}) async-start(f32[8,4,8192]{2,1,0:T(4,128)} %fusion.4), calls=%async_computation.2 | async-start | bytes 2097152 | tf_op jit(solution)/shard_map/all_to_all | solution.py:241
  83.8 24.9 %copy-start = (bf16[1,1024,128]{2,1,0:T(8,128)(2,1)S(1)}, bf16[1,1024,128]{2,1,0:T(8,128)(2,1)}, u32[]{:S(2)}) copy-start(bf16[1,1024,128]{2,1,0:T(8,128)(2,1)} %param.8) | copy-start | bytes 786436
  83.9 24.9 %copy-start.5 = (f32[128]{0:T(128)S(1)}, f32[128]{0:T(128)}, u32[]{:S(2)}) copy-start(f32[128]{0:T(128)} %param.12) | copy-start | bytes 1540
  108.2 6.2 %copy-start.2 = (f32[2,64,32]{2,1,0:T(8,128)S(1)}, f32[2,64,32]{2,1,0:T(8,128)}, u32[]{:S(2)}) copy-start(f32[2,64,32]{2,1,0:T(8,128)} %get-tuple-element.13) | copy-start | bytes 49156
  109.5 1.2 collective-permute-start
  110.7 3.6 %collective-permute-start.1 = (f32[260]{0:T(512)S(1)}, f32[260]{0:T(512)S(1)}, u32[]{:S(2)}, u32[]{:S(2)}) collective-permute-start(f32[260]{0:T(512)S(1)} %fusion.12), channel_id=1, source_target_pairs={{0,2},{1,3},{2,0},{3,1},{4,6},{5,7},{6,4},{7,5},{8,10},{9,11},{10,... | collective-permute-start | bytes 3128 | tf_op jit(solution)/shard_map/ppermute | solution.py:184
  114.3 4.5 %collective-permute-start.2 = (f32[260]{0:T(512)S(1)}, f32[260]{0:T(512)S(1)}, u32[]{:S(2)}, u32[]{:S(2)}) collective-permute-start(f32[260]{0:T(512)S(1)} %add.203), channel_id=1, source_target_pairs={{0,4},{1,5},{2,6},{3,7},{4,0},{5,1},{6,2},{7,3},{8,12},{9,13},{10,... | collective-permute-start | bytes 3128 | tf_op jit(solution)/shard_map/ppermute | solution.py:184
  118.8 3.6 %collective-permute-start.3 = (f32[260]{0:T(512)S(1)}, f32[260]{0:T(512)S(1)}, u32[]{:S(2)}, u32[]{:S(2)}) collective-permute-start(f32[260]{0:T(512)S(1)} %add.204), channel_id=1, source_target_pairs={{0,8},{1,9},{2,10},{3,11},{4,12},{5,13},{6,14},{7,15},{8,0},{9,1},... | collective-permute-start | bytes 3128 | tf_op jit(solution)/shard_map/ppermute | solution.py:184
  122.4 3.6 %collective-permute-start.4 = (f32[260]{0:T(512)S(1)}, f32[260]{0:T(512)S(1)}, u32[]{:S(2)}, u32[]{:S(2)}) collective-permute-start(f32[260]{0:T(512)S(1)} %add.205), channel_id=1, source_target_pairs={{0,16},{1,17},{2,18},{3,19},{4,20},{5,21},{6,22},{7,23},{8,24},{9,... | collective-permute-start | bytes 3128 | tf_op jit(solution)/shard_map/ppermute | solution.py:184

commit v10 on v9

--- a/solution.py
+++ b/solution.py
@@ -38,21 +38,47 @@
     return (query_hat, query_scale, query_hat.astype(jnp.bfloat16))
 
 
-def score_kernel(q_ref, k_ref, kt_ref, w_ref, mass_ref, spos_ref, qpos_ref,
-                 gq_ref, wg_ref, sgt_ref, div_ref, qr_ref, qt_ref, mix_ref, mg_ref, sp_ref):
+def query_kernel(q_ref, qr_ref, qt_ref):
+    f32 = jnp.float32
+    for h in range(H):
+        x = q_ref[:, h * DH:(h + 1) * DH].astype(f32)
+        scale = lax.rsqrt(jnp.mean(x * x, -1, keepdims=True) + epsilon)
+        nq = (x * scale).astype(jnp.bfloat16)
+        qr_ref[h * BS:(h + 1) * BS, :] = nq
+        qt_ref[:, h * BS:(h + 1) * BS] = nq.astype(f32).T.astype(jnp.bfloat16)
+
+
+def normed_query_rows(q):
+    nblk = q.shape[0]
+    nrows = H * BS
+
+    def blk(*shape):
+        return pl.BlockSpec((None,) + shape, lambda b: (b,) + (0,) * len(shape))
+
+    return pl.pallas_call(
+        query_kernel,
+        grid=(nblk,),
+        in_specs=[blk(BS, H * DH)],
+        out_specs=[blk(nrows, DH), blk(DH, nrows)],
+        out_shape=[
+            jax.ShapeDtypeStruct((nblk, nrows, DH), jnp.bfloat16),
+            jax.ShapeDtypeStruct((nblk, DH, nrows), jnp.bfloat16),
+        ],
+        compiler_params=pltpu.CompilerParams(dimension_semantics=("arbitrary",)),
+        cost_estimate=pl.CostEstimate(
+            flops=nblk * nrows * DH * 4, transcendentals=nblk * nrows,
+            bytes_accessed=nblk * nrows * DH * 6),
+    )(q)
+
+
+def score_kernel(q_ref, qr_ref, qt_ref, k_ref, kt_ref, w_ref, mass_ref, spos_ref, qpos_ref,
+                 gq_ref, wg_ref, sgt_ref, div_ref, mix_ref, mg_ref, sp_ref):
     f32 = jnp.float32
     inv_root = DH ** (-0.5)
     rows = HEAD_GROUP * BS
     groups = H // HEAD_GROUP
     slots = kt_ref.shape[1]
     chunks = slots // CHUNK
-
-    for h in range(H):
-        x = q_ref[:, h * DH:(h + 1) * DH].astype(f32)
-        scale = lax.rsqrt(jnp.mean(x * x, -1, keepdims=True) + epsilon)
-        nq = (x * scale).astype(jnp.bfloat16)
-        qr_ref[h * BS:(h + 1) * BS, :] = nq
-        qt_ref[:, h * BS:(h + 1) * BS] = nq.astype(f32).T.astype(jnp.bfloat16)
 
     head_ids = lax.broadcasted_iota(jnp.int32, (H, HEAD_GROUP), 0)
     pick_ids = lax.broadcasted_iota(jnp.int32, (H, HEAD_GROUP), 1)
@@ -135,7 +161,7 @@
     sgt_ref[...] = sgt_ref[...] * inv_root
 
 
-def score_blocks(q, k, kt, w, mass, spos, qpos):
+def score_blocks(q, qr, qt, k, kt, w, mass, spos, qpos):
     nblk = q.shape[0]
     slots = k.shape[1]
     nrows = H * BS
@@ -149,7 +175,7 @@
         score_kernel,
         grid=(nblk,),
         in_specs=[
-            blk(BS, H * DH), blk(slots, DH), blk(DH, slots),
+            blk(BS, H * DH), blk(nrows, DH), blk(DH, nrows), blk(slots, DH), blk(DH, slots),
             blk(BS, H), blk(BS, slots), blk(1, slots), blk(BS, 1),
         ],
         out_specs=[blk(BS, H * DH), blk(BS, H), blk(DH, slots), blk(BS, 1)],
@@ -160,7 +186,6 @@
             jax.ShapeDtypeStruct((nblk, BS, 1), f32),
         ],
         scratch_shapes=[
-            pltpu.VMEM((nrows, DH), jnp.bfloat16), pltpu.VMEM((DH, nrows), jnp.bfloat16),
             pltpu.VMEM((BS, slots), f32), pltpu.VMEM((BS, slots), f32), pltpu.VMEM((nrows, slots), f32)
         ],
         compiler_params=pltpu.CompilerParams(
@@ -169,7 +194,7 @@
         cost_estimate=pl.CostEstimate(
             flops=flops, transcendentals=nblk * nrows * slots * 3,
             bytes_accessed=nblk * (BS * H * DH * 6 + slots * DH * 4 + DH * slots * 4)),
-    )(q, k, kt, w, mass, spos, qpos)
+    )(q, qr, qt, k, kt, w, mass, spos, qpos)
 
 
 def butterfly_sum(value, axes):
@@ -230,8 +255,10 @@
 
     key_cols = slot_keys.transpose(0, 2, 1)
     mass_rows = target_mass[0].reshape(query_count, BS, slot_count)
+    query_blocks = queries[0].reshape(query_count, BS, H * DH)
+    head_rows, head_cols = normed_query_rows(query_blocks)
     grad_query_rows, weight_grads, slot_grad_t, div_rows = score_blocks(
-        queries[0].reshape(query_count, BS, H * DH), slot_keys, key_cols,
+        query_blocks, head_rows, head_cols, slot_keys, key_cols,
         head_weights[0].reshape(query_count, BS, H), mass_rows, slot_limit, query_pos
     )
     divergence_total = jnp.sum(div_rows)

time: 129 us -> 129 us (level)
  waiting for transfers between devices: 49.3 us -> 39.7 us
  Pallas kernels: 32.6 us -> 41.3 us
    all_to_all x1, waiting for transfers between devices: 12.9 us -> 3.3 us  [per_device(): lax.all_to_all(sent_keys, 'ctx', split_axis=0, concat_axis=0, tiled=True)]
    pallas_call x0 -> x1, Pallas kernels: none -> 9.55 us  [normed_query_rows(): pl.pallas_call(query_kernel, grid=(nblk,), in_specs=[blk(BS, H * DH)], ou...]
  transfers between devices with their start and end apart: 8 -> 8, of which waited for: 8 -> 8; matrix products, arithmetic and copies ran while one was open for 9% -> 9% of each run, Pallas kernels for 0% -> 7%
where the time goes in v10:
time: 129 us; the launch traced here: 128 us
  Pallas kernels  41.3 us (32%)
  waiting for transfers between devices  39.7 us (31%)
  starting transfers between devices  16.8 us (13%)
  local copies, waits for them, and re-layouts  13.8 us (11%)
  other arithmetic  11 us (9%)
  between operations  2.69 us (2%)
  matrix products  2.65 us (2%)
    pallas_call x1, Pallas kernels, score_blocks(): pl.pallas_call(score_kernel, grid=(nblk,), in_specs=[blk(BS, H * DH), blk...  31.8 us
    all_to_all x1, waiting for transfers between devices, per_device(): lax.all_to_all(outbound.reshape(ctx_count, capacity, BS * DH), 'ctx', spl...  23.9 us
    ppermute x5, waiting for transfers between devices, butterfly_sum(): value = value + lax.ppermute(value, axes, pairs)  11.2 us
    pallas_call x1, Pallas kernels, normed_query_rows(): pl.pallas_call(query_kernel, grid=(nblk,), in_specs=[blk(BS, H * DH)], ou...  9.55 us
    all_to_all x1, starting transfers between devices, per_device(): lax.all_to_all(request_table, 'ctx', split_axis=0, concat_axis=0, tiled=T...  6.33 us
    all_to_all x1, starting transfers between devices, per_device(): lax.all_to_all(sent_keys, 'ctx', split_axis=0, concat_axis=0, tiled=True)  3.8 us
    all_to_all x1, starting transfers between devices, per_device(): lax.all_to_all(outbound.reshape(ctx_count, capacity, BS * DH), 'ctx', spl...  3.56 us
    all_to_all x1, waiting for transfers between devices, per_device(): lax.all_to_all(sent_keys, 'ctx', split_axis=0, concat_axis=0, tiled=True)  3.3 us
  transfers between devices with their start and end apart: 8, of which 8 were waited for; matrix products, arithmetic and copies ran while one was open for 9% of the time, Pallas kernels for 7%

profile of v10, /device:TPU:0, one launch (start us, length us, event | category | flops | bytes accessed | tf_op | source)
XLA Modules:
  0.0 128.1 jit_solution(7575560023082345895)
XLA Ops:
  0.6 0.7 compare_and_fusion.1
  1.3 0.7 multiply_bitcast_fusion
  2.9 0.7 sub.60
  3.5 6.3 %all-to-all-start = ((s32[8,1,4]{2,1,0:T(1,128)}), s32[8,1,4]{2,1,0:T(1,128)S(1)}, u32[]{:S(2)}, u32[]{:S(2)}) async-start(s32[8,1,4]{2,1,0:T(1,128)} %bitcast), calls=%async_computation | async-start | bytes 8192 | tf_op jit(solution)/shard_map/all_to_all | solution.py:242
  10.0 1.1 convert_reduce_fusion
  11.1 1.3 %multiply_reduce_fusion.2 = f32[1024]{0:T(1024)S(1)} fusion(bf16[1,1024,128]{2,1,0:T(8,128)(2,1)} %param.8, f32[1024]{0:T(1024)S(1)} %broadcast_multiply_fusion.2), kind=kLoop, calls=%fused_computation.7 | loop fusion | flops 523264 | bytes 270336 | tf_op jit(solution)/shard_map/reduce_sum | solution.py:27
  12.7 1.3 %add_convert_fusion = bf16[16,64,128]{2,1,0:T(8,128)(2,1)S(1)} fusion(f32[128]{0:T(128)} %param.13, f32[128]{0:T(128)} %param.12, f32[16,64]{1,0:T(8,128)S(1)} %rsqrt.13, f32[16,64]{1,0:T(8,128)S(1)} %div.38, bf16[16,64,128]{2,1,0:T(8,128)(2,1)} %bitcast.38), kind=kLoop, calls=%fused_computation.6 | loop fusion | flops 786432 | bytes 533504 | tf_op jit(solution)/shard_map/convert_element_type | solution.py:30
  14.0 1.3 %all-to-all-done = s32[8,1,4]{2,1,0:T(1,128)S(1)} async-done(((s32[8,1,4]{2,1,0:T(1,128)}), s32[8,1,4]{2,1,0:T(1,128)S(1)}, u32[]{:S(2)}, u32[]{:S(2)}) %all-to-all-start) | async-done | bytes 160 | tf_op jit(solution)/shard_map/all_to_all | solution.py:242
  15.6 1.4 %gather_fusion = bf16[32,64,128]{2,1,0:T(8,128)(2,1)} fusion(bf16[16,64,128]{2,1,0:T(8,128)(2,1)S(1)} %add_convert_fusion, s32[1024]{0:T(1024)S(1)} %pad_clamp_fusion.1), kind=kCustom, calls=%fused_computation | custom fusion | bytes 1048704 | tf_op jit(solution)/shard_map/gather | solution.py:243
  17.0 3.8 %all-to-all-start.1 = ((bf16[8,4,64,128]{3,2,1,0:T(8,128)(2,1)}), bf16[8,4,64,128]{3,2,1,0:T(8,128)(2,1)S(1)}, u32[]{:S(2)}, u32[]{:S(2)}) async-start(bf16[8,4,64,128]{3,2,1,0:T(8,128)(2,1)} %bitcast.5), calls=%async_computation.1 | async-start | bytes 1048576 | tf_op jit(solution)/shard_map/all_to_all | solution.py:244
  21.3 0.7 copy.48
  22.0 9.6 %shard_map.118 = (bf16[2,2048,128]{2,1,0:T(8,128)(2,1)}, bf16[2,128,2048]{2,1,0:T(8,128)(2,1)}) custom-call(bf16[2,64,4096]{2,1,0:T(8,128)(2,1)} %bitcast.43), custom_call_target="tpu_custom_call" | custom-call | flops 2097152 | bytes 3145728 | tf_op jit(solution)/shard_map/pallas_call | solution.py:58
  32.9 3.3 %all-to-all-done.1 = bf16[8,4,64,128]{3,2,1,0:T(8,128)(2,1)S(1)} async-done(((bf16[8,4,64,128]{3,2,1,0:T(8,128)(2,1)}), bf16[8,4,64,128]{3,2,1,0:T(8,128)(2,1)S(1)}, u32[]{:S(2)}, u32[]{:S(2)}) %all-to-all-start.1) | async-done | bytes 524320 | tf_op jit(solution)/shard_map/all_to_all | solution.py:244
  36.2 0.7 gather_fusion.1
  37.0 1.3 %copy.47 = bf16[2,2048,128]{1,2,0:T(8,128)(2,1)} copy(bf16[2,2048,128]{2,1,0:T(8,128)(2,1)S(1)} %bitcast.40) | data formatting | bytes 2097152 | tf_op jit(solution)/shard_map/reshape | solution.py:246
  38.3 31.8 %shard_map.119 = (f32[2,64,4096]{2,1,0:T(8,128)}, f32[2,64,32]{2,1,0:T(8,128)}, f32[2,128,2048]{2,1,0:T(8,128)}, f32[2,64,1]{2,1,0:T(8,128)}) custom-call(bf16[2,64,4096]{2,1,0:T(8,128)(2,1)} %bitcast.44, bf16[2,2048,128]{2,1,0:T(8,128)(2,1)} %get-tuple-element.12.qr_ref, bf16[2,128,2048]{2,1,0:T(8,128)(2,1)} %get-tuple-element.13.qt_ref, ...), custom_call_target="tpu_custom_call" | custom-call | flops 8589934592 | bytes 7340032 | tf_op jit(solution)/shard_map/pallas_call | solution.py:174
  70.1 2.9 %copy.50 = f32[2,2048,128]{2,1,0:T(8,128)} copy(f32[2,2048,128]{1,2,0:T(8,128)} %bitcast.42) | data formatting | bytes 4194304 | tf_op jit(solution)/shard_map/transpose | solution.py:265
  73.0 1.7 %reshape.469 = f32[64,8192,1]{1,0,2:T(8,128)S(1)} reshape(f32[2,2048,128]{2,1,0:T(8,128)} %copy.50) | data formatting | bytes 4194304 | tf_op jit(solution)/shard_map/reshape | solution.py:266
  74.7 2.2 %fusion.4 = f32[8,4,8192]{2,1,0:T(4,128)} fusion(f32[64,8192,1]{1,0,2:T(8,128)S(1)} %reshape.469, pred[8,4,64]{2,0,1:T(8,128)(4,1)S(1)} %compare_and_fusion), kind=kOutput, calls=%fused_computation.20 | convolution fusion | flops 201326592 | bytes 3147776 | tf_op jit(solution)/shard_map/dot_general | solution.py:267
  76.9 3.6 %all-to-all-start.2 = ((f32[8,4,8192]{2,1,0:T(4,128)}), f32[8,4,8192]{2,1,0:T(4,128)S(1)}, u32[]{:S(2)}, u32[]{:S(2)}) async-start(f32[8,4,8192]{2,1,0:T(4,128)} %fusion.4), calls=%async_computation.2 | async-start | bytes 2097152 | tf_op jit(solution)/shard_map/all_to_all | solution.py:268
  81.0 0.7 reduce.4
  82.4 0.6 compare_select_fusion.2
  83.0 23.9 %all-to-all-done.2 = f32[8,4,8192]{2,1,0:T(4,128)S(1)} async-done(((f32[8,4,8192]{2,1,0:T(4,128)}), f32[8,4,8192]{2,1,0:T(4,128)S(1)}, u32[]{:S(2)}, u32[]{:S(2)}) %all-to-all-start.2) | async-done | bytes 1048608 | tf_op jit(solution)/shard_map/all_to_all | solution.py:268
  108.7 1.1 collective-permute-done
  109.9 3.6 %collective-permute-done.1 = f32[260]{0:T(512)S(1)} collective-permute-done((f32[260]{0:T(512)S(1)}, f32[260]{0:T(512)S(1)}, u32[]{:S(2)}, u32[]{:S(2)}) %collective-permute-start.1) | collective-permute-done | bytes 1072 | tf_op jit(solution)/shard_map/ppermute | solution.py:209
  113.5 0.7 copy.52
  114.2 3.8 %collective-permute-done.2 = f32[260]{0:T(512)S(1)} collective-permute-done((f32[260]{0:T(512)S(1)}, f32[260]{0:T(512)S(1)}, u32[]{:S(2)}, u32[]{:S(2)}) %collective-permute-start.2) | collective-permute-done | bytes 1072 | tf_op jit(solution)/shard_map/ppermute | solution.py:209
  118.0 1.5 %collective-permute-start.3 = (f32[260]{0:T(512)S(1)}, f32[260]{0:T(512)S(1)}, u32[]{:S(2)}, u32[]{:S(2)}) collective-permute-start(f32[260]{0:T(512)S(1)} %add.204), channel_id=1, source_target_pairs={{0,8},{1,9},{2,10},{3,11},{4,12},{5,13},{6,14},{7,15},{8,0},{9,1},... | collective-permute-start | bytes 3128 | tf_op jit(solution)/shard_map/ppermute | solution.py:209
  119.6 2.0 %collective-permute-done.3 = f32[260]{0:T(512)S(1)} collective-permute-done((f32[260]{0:T(512)S(1)}, f32[260]{0:T(512)S(1)}, u32[]{:S(2)}, u32[]{:S(2)}) %collective-permute-start.3) | collective-permute-done | bytes 1072 | tf_op jit(solution)/shard_map/ppermute | solution.py:209
  121.6 1.5 %collective-permute-start.4 = (f32[260]{0:T(512)S(1)}, f32[260]{0:T(512)S(1)}, u32[]{:S(2)}, u32[]{:S(2)}) collective-permute-start(f32[260]{0:T(512)S(1)} %add.205), channel_id=1, source_target_pairs={{0,16},{1,17},{2,18},{3,19},{4,20},{5,21},{6,22},{7,23},{8,24},{9,... | collective-permute-start | bytes 3128 | tf_op jit(solution)/shard_map/ppermute | solution.py:209
  123.1 1.4 %subtract_multiply_fusion = f32[1,1024,128]{2,1,0:T(8,128)} fusion(f32[1,1024,128]{2,1,0:T(8,128)S(1)} %reshape.450, bf16[1,1024,128]{2,1,0:T(8,128)(2,1)S(1)} %copy-done, f32[1024]{0:T(1024)S(1)} %get-tuple-element.62, f32[1024]{0:T(1024)S(1)} %add_rsqrt_fusion, f32[1024]{0:T(1024)S(1)} %broadcast_multiply_fusion.2, f32[1024]{0:T(1024)S(1)} %get-tuple-element.63, ...), kind=kLoop, calls=%fused_computation.3 | loop fusion | flops 1048576 | bytes 1327616 | tf_op jit(solution)/shard_map/mul | solution.py:281
  124.5 0.7 collective-permute-done.4
  (67 shorter events, 7.4 us)
Async XLA Ops:
  0.6 20.6 %copy-start.4 = (bf16[1,128,32]{1,2,0:T(8,128)(2,1)S(1)}, bf16[1,128,32]{1,2,0:T(8,128)(2,1)}, u32[]{:S(2)}) copy-start(bf16[1,128,32]{1,2,0:T(8,128)(2,1)} %param.9) | copy-start | bytes 24580
  3.5 11.8 %all-to-all-start = ((s32[8,1,4]{2,1,0:T(1,128)}), s32[8,1,4]{2,1,0:T(1,128)S(1)}, u32[]{:S(2)}, u32[]{:S(2)}) async-start(s32[8,1,4]{2,1,0:T(1,128)} %bitcast), calls=%async_computation | async-start | bytes 8192 | tf_op jit(solution)/shard_map/all_to_all | solution.py:242
  17.0 19.2 %all-to-all-start.1 = ((bf16[8,4,64,128]{3,2,1,0:T(8,128)(2,1)}), bf16[8,4,64,128]{3,2,1,0:T(8,128)(2,1)S(1)}, u32[]{:S(2)}, u32[]{:S(2)}) async-start(bf16[8,4,64,128]{3,2,1,0:T(8,128)(2,1)} %bitcast.5), calls=%async_computation.1 | async-start | bytes 1048576 | tf_op jit(solution)/shard_map/all_to_all | solution.py:244
  36.9 1.3 %copy-start.1 = (bf16[64,64,128]{2,1,0:T(8,128)(2,1)}, bf16[64,64,128]{2,1,0:T(8,128)(2,1)S(1)}, u32[]{:S(2)}) copy-start(bf16[64,64,128]{2,1,0:T(8,128)(2,1)S(1)} %gather_fusion.1) | copy-start | bytes 3145732
  74.7 7.0 %copy-start.3 = (f32[2,64,1]{2,1,0:T(8,128)S(1)}, f32[2,64,1]{2,1,0:T(8,128)}, u32[]{:S(2)}) copy-start(f32[2,64,1]{2,1,0:T(8,128)} %get-tuple-element.15) | copy-start | bytes 1540
  76.9 30.1 %all-to-all-start.2 = ((f32[8,4,8192]{2,1,0:T(4,128)}), f32[8,4,8192]{2,1,0:T(4,128)S(1)}, u32[]{:S(2)}, u32[]{:S(2)}) async-start(f32[8,4,8192]{2,1,0:T(4,128)} %fusion.4), calls=%async_computation.2 | async-start | bytes 2097152 | tf_op jit(solution)/shard_map/all_to_all | solution.py:268
  83.0 24.9 %copy-start = (bf16[1,1024,128]{2,1,0:T(8,128)(2,1)S(1)}, bf16[1,1024,128]{2,1,0:T(8,128)(2,1)}, u32[]{:S(2)}) copy-start(bf16[1,1024,128]{2,1,0:T(8,128)(2,1)} %param.8) | copy-start | bytes 786436
  83.0 24.9 %copy-start.5 = (f32[128]{0:T(128)S(1)}, f32[128]{0:T(128)}, u32[]{:S(2)}) copy-start(f32[128]{0:T(128)} %param.12) | copy-start | bytes 1540
  107.4 6.2 %copy-start.2 = (f32[2,64,32]{2,1,0:T(8,128)S(1)}, f32[2,64,32]{2,1,0:T(8,128)}, u32[]{:S(2)}) copy-start(f32[2,64,32]{2,1,0:T(8,128)} %get-tuple-element.17) | copy-start | bytes 49156
  108.6 1.2 collective-permute-start
  109.9 3.6 %collective-permute-start.1 = (f32[260]{0:T(512)S(1)}, f32[260]{0:T(512)S(1)}, u32[]{:S(2)}, u32[]{:S(2)}) collective-permute-start(f32[260]{0:T(512)S(1)} %fusion.12), channel_id=1, source_target_pairs={{0,2},{1,3},{2,0},{3,1},{4,6},{5,7},{6,4},{7,5},{8,10},{9,11},{10,... | collective-permute-start | bytes 3128 | tf_op jit(solution)/shard_map/ppermute | solution.py:209
  113.5 4.5 %collective-permute-start.2 = (f32[260]{0:T(512)S(1)}, f32[260]{0:T(512)S(1)}, u32[]{:S(2)}, u32[]{:S(2)}) collective-permute-start(f32[260]{0:T(512)S(1)} %add.203), channel_id=1, source_target_pairs={{0,4},{1,5},{2,6},{3,7},{4,0},{5,1},{6,2},{7,3},{8,12},{9,13},{10,... | collective-permute-start | bytes 3128 | tf_op jit(solution)/shard_map/ppermute | solution.py:209
  118.0 3.6 %collective-permute-start.3 = (f32[260]{0:T(512)S(1)}, f32[260]{0:T(512)S(1)}, u32[]{:S(2)}, u32[]{:S(2)}) collective-permute-start(f32[260]{0:T(512)S(1)} %add.204), channel_id=1, source_target_pairs={{0,8},{1,9},{2,10},{3,11},{4,12},{5,13},{6,14},{7,15},{8,0},{9,1},... | collective-permute-start | bytes 3128 | tf_op jit(solution)/shard_map/ppermute | solution.py:209
  121.6 3.6 %collective-permute-start.4 = (f32[260]{0:T(512)S(1)}, f32[260]{0:T(512)S(1)}, u32[]{:S(2)}, u32[]{:S(2)}) collective-permute-start(f32[260]{0:T(512)S(1)} %add.205), channel_id=1, source_target_pairs={{0,16},{1,17},{2,18},{3,19},{4,20},{5,21},{6,22},{7,23},{8,24},{9,... | collective-permute-start | bytes 3128 | tf_op jit(solution)/shard_map/ppermute | solution.py:209

commit v11 on v10

--- a/solution.py
+++ b/solution.py
@@ -240,10 +240,11 @@
     request_table = jnp.sum(jnp.where(placement, local_block[:, None] + 1, 0), 0) - 1
     request_table = request_table.reshape(ctx_count, capacity)
     asked_back = lax.all_to_all(request_table, "ctx", split_axis=0, concat_axis=0, tiled=True)
-    sent_keys = normed_keys.reshape(key_count, BS, DH)[jnp.clip(asked_back, 0, key_count - 1)]
-    arrived_keys = lax.all_to_all(sent_keys, "ctx", split_axis=0, concat_axis=0, tiled=True)
-    picked = arrived_keys.reshape(ctx_count * capacity, BS, DH)[target_slot]
-    slot_keys = picked.reshape(query_count, slot_count, DH)
+    sent_hats = key_hat.reshape(key_count, BS, DH)[jnp.clip(asked_back, 0, key_count - 1)]
+    arrived_hats = lax.all_to_all(sent_hats, "ctx", split_axis=0, concat_axis=0, tiled=True)
+    slot_hats = arrived_hats.reshape(ctx_count * capacity, BS, DH)[target_slot]
+    slot_keys = (slot_hats * key_gain + key_bias).astype(jnp.bfloat16)
+    slot_keys = slot_keys.reshape(query_count, slot_count, DH)
     slot_positions = (block_safe[:, None] * BS + jnp.arange(BS, dtype=jnp.int32)[None, :]).reshape(
         query_count, slot_count
     )
@@ -263,6 +264,9 @@
     )
     divergence_total = jnp.sum(div_rows)
     grad_slots = slot_grad_t.transpose(0, 2, 1)
+    live_slots = jnp.where(is_listed[:, None, None], grad_slots.reshape(request_count, BS, DH), 0.0)
+    gain_part = jnp.sum(live_slots * slot_hats, (0, 1))
+    bias_part = jnp.sum(live_slots, (0, 1))
     slot_flat = grad_slots.reshape(request_count, BS * DH)
     outbound = jnp.dot(placement.T.astype(jnp.float32), slot_flat, precision=lax.Precision.HIGHEST)
     returned = lax.all_to_all(
@@ -275,8 +279,6 @@
     key_grad = jnp.dot(
         own_rows, returned.reshape(ctx_count * capacity, BS * DH), precision=lax.Precision.HIGHEST
     ).reshape(KD, DH)
-    gain_part = jnp.sum(key_grad * key_hat, 0)
-    bias_part = jnp.sum(key_grad, 0)
     scaled_grad = key_grad * key_gain
     grad_key_rows = (
         scaled_grad

time: 129 us -> 140 us (1.085)
  starting transfers between devices: 16.8 us -> 23.3 us
  waiting for transfers between devices: 39.7 us -> 34.4 us
  local copies, waits for them, and re-layouts: 13.8 us -> 18.6 us
  other arithmetic: 11 us -> 14.7 us
  matrix products: 2.65 us -> 4.22 us
    all_to_all x1, waiting for transfers between devices: 23.9 us -> 0.01 us  [per_device(): lax.all_to_all(outbound.reshape(ctx_count, capacity, BS * DH), 'ctx', spl...]
    all_to_all x1, waiting for transfers between devices: 3.3 us -> 14.2 us  [per_device(): lax.all_to_all(sent_hats, 'ctx', split_axis=0, concat_axis=0, tiled=True)]
    ppermute x5, waiting for transfers between devices: 11.2 us -> 18.6 us  [butterfly_sum(): value = value + lax.ppermute(value, axes, pairs)]
    ppermute x5, starting transfers between devices: 3.16 us -> 9.82 us  [butterfly_sum(): value = value + lax.ppermute(value, axes, pairs)]
    gather x2 -> x3, local copies, waits for them, and re-layouts: 2.16 us -> 5.53 us  [the longest x2 3.95 us: per_device(): slot_hats = arrived_hats.reshape(ctx_count * capacity, BS, DH)[target_slot]]
    reduce_sum x1 -> x2, other arithmetic: 0.64 us -> 2.69 us  [the longest x1 2.03 us: per_device(): gain_part = jnp.sum(live_slots * slot_hats, (0, 1))]
    dot_general x1, matrix products: 2.18 us -> 3.74 us  [per_device(): jnp.dot(placement.T.astype(jnp.float32), slot_flat, precision=lax.Precisi...]
  transfers between devices with their start and end apart: 8 -> 8, of which waited for: 8 -> 7; matrix products, arithmetic and copies ran while one was open for 9% -> 9% of each run, Pallas kernels for 7% -> 7%
where the time goes in v11:
time: 140 us; the launch traced here: 139 us
  Pallas kernels  41.3 us (30%)
  waiting for transfers between devices  34.4 us (25%)
  starting transfers between devices  23.3 us (17%)
  local copies, waits for them, and re-layouts  18.6 us (13%)
  other arithmetic  14.7 us (10%)
  matrix products  4.22 us (3%)
  between operations  2.67 us (2%)
    pallas_call x1, Pallas kernels, score_blocks(): pl.pallas_call(score_kernel, grid=(nblk,), in_specs=[blk(BS, H * DH), blk...  31.8 us
    ppermute x5, waiting for transfers between devices, butterfly_sum(): value = value + lax.ppermute(value, axes, pairs)  18.6 us
    all_to_all x1, waiting for transfers between devices, per_device(): lax.all_to_all(sent_hats, 'ctx', split_axis=0, concat_axis=0, tiled=True)  14.2 us
    ppermute x5, starting transfers between devices, butterfly_sum(): value = value + lax.ppermute(value, axes, pairs)  9.82 us
    pallas_call x1, Pallas kernels, normed_query_rows(): pl.pallas_call(query_kernel, grid=(nblk,), in_specs=[blk(BS, H * DH)], ou...  9.55 us
    all_to_all x1, starting transfers between devices, per_device(): lax.all_to_all(request_table, 'ctx', split_axis=0, concat_axis=0, tiled=T...  6.33 us
    gather x2, local copies, waits for them, and re-layouts, per_device(): slot_hats = arrived_hats.reshape(ctx_count * capacity, BS, DH)[target_slot]  3.95 us
    dot_general x1, matrix products, per_device(): jnp.dot(placement.T.astype(jnp.float32), slot_flat, precision=lax.Precisi...  3.74 us
  transfers between devices with their start and end apart: 8, of which 7 were waited for; matrix products, arithmetic and copies ran while one was open for 9% of the time, Pallas kernels for 7%

profile of v11, /device:TPU:0, one launch (start us, length us, event | category | flops | bytes accessed | tf_op | source)
XLA Modules:
  0.0 139.1 jit_solution(7488768837420729699)
XLA Ops:
  0.6 0.7 compare_and_fusion.1
  1.3 0.7 multiply_bitcast_fusion
  3.5 6.3 %all-to-all-start = ((s32[8,1,4]{2,1,0:T(1,128)}), s32[8,1,4]{2,1,0:T(1,128)S(1)}, u32[]{:S(2)}, u32[]{:S(2)}) async-start(s32[8,1,4]{2,1,0:T(1,128)} %bitcast.4), calls=%async_computation | async-start | bytes 8192 | tf_op jit(solution)/shard_map/all_to_all | solution.py:242
  9.9 1.1 convert_reduce_fusion
  11.0 1.3 multiply_reduce_fusion.2
  12.4 1.3 subtract_multiply_fusion.1
  13.7 1.6 %all-to-all-done = s32[8,1,4]{2,1,0:T(1,128)S(1)} async-done(((s32[8,1,4]{2,1,0:T(1,128)}), s32[8,1,4]{2,1,0:T(1,128)S(1)}, u32[]{:S(2)}, u32[]{:S(2)}) %all-to-all-start) | async-done | bytes 160 | tf_op jit(solution)/shard_map/all_to_all | solution.py:242
  15.6 1.6 %gather_fusion = f32[32,64,128]{2,1,0:T(8,128)} fusion(f32[16,64,128]{2,1,0:T(8,128)S(1)} %subtract_multiply_fusion.1, s32[1024]{0:T(1024)S(1)} %pad_clamp_fusion.1), kind=kCustom, calls=%fused_computation | custom fusion | bytes 2097280 | tf_op jit(solution)/shard_map/gather | solution.py:243
  17.2 3.6 %all-to-all-start.1 = ((f32[8,4,64,128]{3,2,1,0:T(8,128)}), f32[8,4,64,128]{3,2,1,0:T(8,128)S(1)}, u32[]{:S(2)}, u32[]{:S(2)}) async-start(f32[8,4,64,128]{3,2,1,0:T(8,128)} %bitcast.6), calls=%async_computation.1 | async-start | bytes 2097152 | tf_op jit(solution)/shard_map/all_to_all | solution.py:244
  21.5 0.7 copy.54
  22.2 9.6 %shard_map.118 = (bf16[2,2048,128]{2,1,0:T(8,128)(2,1)}, bf16[2,128,2048]{2,1,0:T(8,128)(2,1)}) custom-call(bf16[2,64,4096]{2,1,0:T(8,128)(2,1)} %bitcast.41), custom_call_target="tpu_custom_call" | custom-call | flops 2097152 | bytes 3145728 | tf_op jit(solution)/shard_map/pallas_call | solution.py:58
  33.1 14.2 %all-to-all-done.1 = f32[8,4,64,128]{3,2,1,0:T(8,128)S(1)} async-done(((f32[8,4,64,128]{3,2,1,0:T(8,128)}), f32[8,4,64,128]{3,2,1,0:T(8,128)S(1)}, u32[]{:S(2)}, u32[]{:S(2)}) %all-to-all-start.1) | async-done | bytes 1048608 | tf_op jit(solution)/shard_map/all_to_all | solution.py:244
  47.3 2.0 %gather_fusion.1 = f32[64,64,128]{2,1,0:T(8,128)} fusion(f32[32,64,128]{2,1,0:T(8,128)S(1)} %bitcast.37, s32[1024]{0:T(1024)S(1)} %pad_clamp_fusion), kind=kCustom, calls=%fused_computation.1 | custom fusion | bytes 4194560 | tf_op jit(solution)/shard_map/gather | solution.py:245
  49.3 1.9 %copy.53 = f32[2,2048,128]{1,2,0:T(8,128)S(1)} copy(f32[2,2048,128]{2,1,0:T(8,128)} %bitcast.39) | data formatting | bytes 4194304 | tf_op jit(solution)/shard_map/gather | solution.py:245
  51.3 1.3 fusion.15.kt_ref
  52.9 1.3 copy.56.k_ref
  54.3 31.8 %shard_map.119 = (f32[2,64,4096]{2,1,0:T(8,128)}, f32[2,64,32]{2,1,0:T(8,128)}, f32[2,128,2048]{2,1,0:T(8,128)}, f32[2,64,1]{2,1,0:T(8,128)}) custom-call(bf16[2,64,4096]{2,1,0:T(8,128)(2,1)} %bitcast.42, bf16[2,2048,128]{2,1,0:T(8,128)(2,1)} %get-tuple-element.12.qr_ref, bf16[2,128,2048]{2,1,0:T(8,128)(2,1)} %get-tuple-element.13.qt_ref, ...), custom_call_target="tpu_custom_call" | custom-call | flops 8589934592 | bytes 7340032 | tf_op jit(solution)/shard_map/pallas_call | solution.py:174
  86.1 2.9 %copy.58 = f32[2,2048,128]{2,1,0:T(8,128)} copy(f32[2,2048,128]{1,2,0:T(8,128)} %bitcast.38) | data formatting | bytes 4194304 | tf_op jit(solution)/shard_map/transpose | solution.py:266
  89.0 2.7 %reshape.474 = f32[64,8192,1]{1,0,2:T(8,128)} reshape(f32[2,2048,128]{2,1,0:T(8,128)} %copy.58) | data formatting | bytes 4194304 | tf_op jit(solution)/shard_map/reshape | solution.py:270
  91.7 3.7 %fusion.3 = f32[8,4,8192]{2,1,0:T(4,128)} fusion(f32[64,8192,1]{1,0,2:T(8,128)} %reshape.474, pred[8,4,64]{2,0,1:T(8,128)(4,1)S(1)} %compare_and_fusion), kind=kOutput, calls=%fused_computation.21 | convolution fusion | flops 201326592 | bytes 3147776 | tf_op jit(solution)/shard_map/dot_general | solution.py:271
  95.5 3.6 %all-to-all-start.2 = ((f32[8,4,8192]{2,1,0:T(4,128)}), f32[8,4,8192]{2,1,0:T(4,128)S(1)}, u32[]{:S(2)}, u32[]{:S(2)}) async-start(f32[8,4,8192]{2,1,0:T(4,128)} %fusion.3), calls=%async_computation.2 | async-start | bytes 2097152 | tf_op jit(solution)/shard_map/all_to_all | solution.py:272
  100.4 2.0 %multiply_reduce_fusion = (f32[128]{0:T(128)S(1)}, f32[128]{0:T(128)S(1)}) fusion(f32[2,2048,128]{1,2,0:T(8,128)S(1)} %copy.53, pred[2,2048]{1,0:T(4,128)(4,1)S(1)} %broadcast_in_dim.66, f32[2,128,2048]{2,1,0:T(8,128)} %get-tuple-element.14), kind=kLoop, calls=%fused_computation.2 | loop fusion | flops 2096896 | bytes 4199424 | tf_op jit(solution)/shard_map/reduce_sum | solution.py:268
  102.9 0.8 collective-permute-done
  103.8 1.9 %collective-permute-start.1 = (f32[260]{0:T(512)S(1)}, f32[260]{0:T(512)S(1)}, u32[]{:S(2)}, u32[]{:S(2)}) collective-permute-start(f32[260]{0:T(512)S(1)} %fusion.11), channel_id=1, source_target_pairs={{0,2},{1,3},{2,0},{3,1},{4,6},{5,7},{6,4},{7,5},{8,10},{9,11},{10,... | collective-permute-start | bytes 3128 | tf_op jit(solution)/shard_map/ppermute | solution.py:209
  105.7 11.4 %collective-permute-done.1 = f32[260]{0:T(512)S(1)} collective-permute-done((f32[260]{0:T(512)S(1)}, f32[260]{0:T(512)S(1)}, u32[]{:S(2)}, u32[]{:S(2)}) %collective-permute-start.1) | collective-permute-done | bytes 1072 | tf_op jit(solution)/shard_map/ppermute | solution.py:209
  117.1 4.4 %collective-permute-start.2 = (f32[260]{0:T(512)S(1)}, f32[260]{0:T(512)S(1)}, u32[]{:S(2)}, u32[]{:S(2)}) collective-permute-start(f32[260]{0:T(512)S(1)} %add.203), channel_id=1, source_target_pairs={{0,4},{1,5},{2,6},{3,7},{4,0},{5,1},{6,2},{7,3},{8,12},{9,13},{10,... | collective-permute-start | bytes 3128 | tf_op jit(solution)/shard_map/ppermute | solution.py:209
  121.5 4.1 %collective-permute-done.2 = f32[260]{0:T(512)S(1)} collective-permute-done((f32[260]{0:T(512)S(1)}, f32[260]{0:T(512)S(1)}, u32[]{:S(2)}, u32[]{:S(2)}) %collective-permute-start.2) | collective-permute-done | bytes 1072 | tf_op jit(solution)/shard_map/ppermute | solution.py:209
  125.6 1.5 %collective-permute-start.3 = (f32[260]{0:T(512)S(1)}, f32[260]{0:T(512)S(1)}, u32[]{:S(2)}, u32[]{:S(2)}) collective-permute-start(f32[260]{0:T(512)S(1)} %add.204), channel_id=1, source_target_pairs={{0,8},{1,9},{2,10},{3,11},{4,12},{5,13},{6,14},{7,15},{8,0},{9,1},... | collective-permute-start | bytes 3128 | tf_op jit(solution)/shard_map/ppermute | solution.py:209
  127.1 2.1 %collective-permute-done.3 = f32[260]{0:T(512)S(1)} collective-permute-done((f32[260]{0:T(512)S(1)}, f32[260]{0:T(512)S(1)}, u32[]{:S(2)}, u32[]{:S(2)}) %collective-permute-start.3) | collective-permute-done | bytes 1072 | tf_op jit(solution)/shard_map/ppermute | solution.py:209
  129.2 1.5 %collective-permute-start.4 = (f32[260]{0:T(512)S(1)}, f32[260]{0:T(512)S(1)}, u32[]{:S(2)}, u32[]{:S(2)}) collective-permute-start(f32[260]{0:T(512)S(1)} %add.205), channel_id=1, source_target_pairs={{0,16},{1,17},{2,18},{3,19},{4,20},{5,21},{6,22},{7,23},{8,24},{9,... | collective-permute-start | bytes 3128 | tf_op jit(solution)/shard_map/ppermute | solution.py:209
  132.0 0.7 copy.60
  136.6 1.4 %subtract_multiply_fusion = f32[1,1024,128]{2,1,0:T(8,128)} fusion(f32[1,1024,128]{2,1,0:T(8,128)S(1)} %reshape.454, bf16[1,1024,128]{2,1,0:T(8,128)(2,1)S(1)} %copy-done, f32[1024]{0:T(1024)S(1)} %get-tuple-element.62, f32[1024]{0:T(1024)S(1)} %add_rsqrt_fusion, f32[1024]{0:T(1024)S(1)} %broadcast_multiply_fusion.2, f32[1024]{0:T(1024)S(1)} %get-tuple-element.63, ...), kind=kLoop, calls=%fused_computation.6 | loop fusion | flops 1048576 | bytes 1327616 | tf_op jit(solution)/shard_map/mul | solution.py:283
  (72 shorter events, 10.6 us)
Async XLA Ops:
  3.5 11.8 %all-to-all-start = ((s32[8,1,4]{2,1,0:T(1,128)}), s32[8,1,4]{2,1,0:T(1,128)S(1)}, u32[]{:S(2)}, u32[]{:S(2)}) async-start(s32[8,1,4]{2,1,0:T(1,128)} %bitcast.4), calls=%async_computation | async-start | bytes 8192 | tf_op jit(solution)/shard_map/all_to_all | solution.py:242
  15.6 5.8 %copy-start.4 = (bf16[1,128,32]{1,2,0:T(8,128)(2,1)S(1)}, bf16[1,128,32]{1,2,0:T(8,128)(2,1)}, u32[]{:S(2)}) copy-start(bf16[1,128,32]{1,2,0:T(8,128)(2,1)} %param.9) | copy-start | bytes 24580
  17.2 30.1 %all-to-all-start.1 = ((f32[8,4,64,128]{3,2,1,0:T(8,128)}), f32[8,4,64,128]{3,2,1,0:T(8,128)S(1)}, u32[]{:S(2)}, u32[]{:S(2)}) async-start(f32[8,4,64,128]{3,2,1,0:T(8,128)} %bitcast.6), calls=%async_computation.1 | async-start | bytes 2097152 | tf_op jit(solution)/shard_map/all_to_all | solution.py:244
  49.3 2.0 %copy-start.3 = (f32[128]{0:T(128)S(1)}, f32[128]{0:T(128)}, u32[]{:S(2)}) copy-start(f32[128]{0:T(128)} %param.12) | copy-start | bytes 1540
  49.3 2.0 %copy-start.5 = (f32[128]{0:T(128)S(1)}, f32[128]{0:T(128)}, u32[]{:S(2)}) copy-start(f32[128]{0:T(128)} %param.13) | copy-start | bytes 1540
  91.7 7.4 %copy-start.2 = (f32[2,64,1]{2,1,0:T(8,128)S(1)}, f32[2,64,1]{2,1,0:T(8,128)}, u32[]{:S(2)}) copy-start(f32[2,64,1]{2,1,0:T(8,128)} %get-tuple-element.15) | copy-start | bytes 1540
  95.5 39.1 %all-to-all-start.2 = ((f32[8,4,8192]{2,1,0:T(4,128)}), f32[8,4,8192]{2,1,0:T(4,128)S(1)}, u32[]{:S(2)}, u32[]{:S(2)}) async-start(f32[8,4,8192]{2,1,0:T(4,128)} %fusion.3), calls=%async_computation.2 | async-start | bytes 2097152 | tf_op jit(solution)/shard_map/all_to_all | solution.py:272
  100.4 31.6 %copy-start.1 = (f32[2,64,32]{2,1,0:T(8,128)S(1)}, f32[2,64,32]{2,1,0:T(8,128)}, u32[]{:S(2)}) copy-start(f32[2,64,32]{2,1,0:T(8,128)} %get-tuple-element.17) | copy-start | bytes 49156
  102.5 1.3 collective-permute-start
  103.8 13.3 %collective-permute-start.1 = (f32[260]{0:T(512)S(1)}, f32[260]{0:T(512)S(1)}, u32[]{:S(2)}, u32[]{:S(2)}) collective-permute-start(f32[260]{0:T(512)S(1)} %fusion.11), channel_id=1, source_target_pairs={{0,2},{1,3},{2,0},{3,1},{4,6},{5,7},{6,4},{7,5},{8,10},{9,11},{10,... | collective-permute-start | bytes 3128 | tf_op jit(solution)/shard_map/ppermute | solution.py:209
  117.1 8.5 %collective-permute-start.2 = (f32[260]{0:T(512)S(1)}, f32[260]{0:T(512)S(1)}, u32[]{:S(2)}, u32[]{:S(2)}) collective-permute-start(f32[260]{0:T(512)S(1)} %add.203), channel_id=1, source_target_pairs={{0,4},{1,5},{2,6},{3,7},{4,0},{5,1},{6,2},{7,3},{8,12},{9,13},{10,... | collective-permute-start | bytes 3128 | tf_op jit(solution)/shard_map/ppermute | solution.py:209
  125.6 3.6 %collective-permute-start.3 = (f32[260]{0:T(512)S(1)}, f32[260]{0:T(512)S(1)}, u32[]{:S(2)}, u32[]{:S(2)}) collective-permute-start(f32[260]{0:T(512)S(1)} %add.204), channel_id=1, source_target_pairs={{0,8},{1,9},{2,10},{3,11},{4,12},{5,13},{6,14},{7,15},{8,0},{9,1},... | collective-permute-start | bytes 3128 | tf_op jit(solution)/shard_map/ppermute | solution.py:209
  129.2 3.6 %collective-permute-start.4 = (f32[260]{0:T(512)S(1)}, f32[260]{0:T(512)S(1)}, u32[]{:S(2)}, u32[]{:S(2)}) collective-permute-start(f32[260]{0:T(512)S(1)} %add.205), channel_id=1, source_target_pairs={{0,16},{1,17},{2,18},{3,19},{4,20},{5,21},{6,22},{7,23},{8,24},{9,... | collective-permute-start | bytes 3128 | tf_op jit(solution)/shard_map/ppermute | solution.py:209
  134.9 1.0 copy-start

commit v12 on v10

--- a/solution.py
+++ b/solution.py
@@ -71,13 +71,13 @@
     )(q)
 
 
-def score_kernel(q_ref, qr_ref, qt_ref, k_ref, kt_ref, w_ref, mass_ref, spos_ref, qpos_ref,
+def score_kernel(q_ref, qr_ref, qt_ref, k_ref, w_ref, mass_ref, spos_ref, qpos_ref,
                  gq_ref, wg_ref, sgt_ref, div_ref, mix_ref, mg_ref, sp_ref):
     f32 = jnp.float32
     inv_root = DH ** (-0.5)
     rows = HEAD_GROUP * BS
     groups = H // HEAD_GROUP
-    slots = kt_ref.shape[1]
+    slots = k_ref.shape[0]
     chunks = slots // CHUNK
 
     head_ids = lax.broadcasted_iota(jnp.int32, (H, HEAD_GROUP), 0)
@@ -98,7 +98,7 @@
         wcol = group_weights(g)
         for c in range(chunks):
             cs = slice(c * CHUNK, (c + 1) * CHUNK)
-            raw = jnp.dot(q, kt_ref[:, cs], preferred_element_type=f32)
+            raw = lax.dot_general(q, k_ref[cs, :], (((1,), (1,)), ((), ())), preferred_element_type=f32)
             tail = jnp.exp2(jnp.abs(raw) * neg_log2_root)
             sp = jnp.maximum(raw * inv_root, 0.0) + jnp.log(1.0 + tail)
             sp_ref[pl.ds(r0, rows), cs] = sp
@@ -134,7 +134,7 @@
         wg_acc = jnp.zeros((rows, 1), f32)
         for c in range(chunks):
             cs = slice(c * CHUNK, (c + 1) * CHUNK)
-            s = jnp.dot(q, kt_ref[:, cs], preferred_element_type=f32) * inv_root
+            s = lax.dot_general(q, k_ref[cs, :], (((1,), (1,)), ((), ())), preferred_element_type=f32) * inv_root
             sp = sp_ref[pl.ds(r0, rows), cs]
             sig = jnp.exp(s - sp)
             mgc = mg_ref[:, cs]
@@ -161,7 +161,7 @@
     sgt_ref[...] = sgt_ref[...] * inv_root
 
 
-def score_blocks(q, qr, qt, k, kt, w, mass, spos, qpos):
+def score_blocks(q, qr, qt, k, w, mass, spos, qpos):
     nblk = q.shape[0]
     slots = k.shape[1]
     nrows = H * BS
@@ -175,7 +175,7 @@
         score_kernel,
         grid=(nblk,),
         in_specs=[
-            blk(BS, H * DH), blk(nrows, DH), blk(DH, nrows), blk(slots, DH), blk(DH, slots),
+            blk(BS, H * DH), blk(nrows, DH), blk(DH, nrows), blk(slots, DH),
             blk(BS, H), blk(BS, slots), blk(1, slots), blk(BS, 1),
         ],
         out_specs=[blk(BS, H * DH), blk(BS, H), blk(DH, slots), blk(BS, 1)],
@@ -193,8 +193,8 @@
         ),
         cost_estimate=pl.CostEstimate(
             flops=flops, transcendentals=nblk * nrows * slots * 3,
-            bytes_accessed=nblk * (BS * H * DH * 6 + slots * DH * 4 + DH * slots * 4)),
-    )(q, qr, qt, k, kt, w, mass, spos, qpos)
+            bytes_accessed=nblk * (BS * H * DH * 10 + slots * DH * 6)),
+    )(q, qr, qt, k, w, mass, spos, qpos)
 
 
 def butterfly_sum(value, axes):
@@ -253,18 +253,20 @@
     first_pos = ctx_index * KD + KD - QD
     query_pos = (first_pos + jnp.arange(QD, dtype=jnp.int32)).reshape(query_count, BS, 1)
 
-    key_cols = slot_keys.transpose(0, 2, 1)
     mass_rows = target_mass[0].reshape(query_count, BS, slot_count)
     query_blocks = queries[0].reshape(query_count, BS, H * DH)
     head_rows, head_cols = normed_query_rows(query_blocks)
     grad_query_rows, weight_grads, slot_grad_t, div_rows = score_blocks(
-        query_blocks, head_rows, head_cols, slot_keys, key_cols,
+        query_blocks, head_rows, head_cols, slot_keys,
         head_weights[0].reshape(query_count, BS, H), mass_rows, slot_limit, query_pos
     )
     divergence_total = jnp.sum(div_rows)
     grad_slots = slot_grad_t.transpose(0, 2, 1)
     slot_flat = grad_slots.reshape(request_count, BS * DH)
-    outbound = jnp.dot(placement.T.astype(jnp.float32), slot_flat, precision=lax.Precision.HIGHEST)
+    request_iota = jnp.arange(request_count, dtype=jnp.int32)[:, None]
+    source_request = jnp.sum(jnp.where(placement, request_iota, 0), 0)
+    slot_used = jnp.any(placement, 0)
+    outbound = jnp.where(slot_used[:, None], slot_flat[source_request], 0.0)
     returned = lax.all_to_all(
         outbound.reshape(ctx_count, capacity, BS * DH), "ctx", split_axis=0, concat_axis=0, tiled=True
     )

time: 129 us -> 128 us (level)
  matrix products: 2.65 us -> 0.47 us
  other arithmetic: 11 us -> 12.3 us
    dot_general x1 -> x0, matrix products: 2.18 us -> none  [per_device(): jnp.dot(placement.T.astype(jnp.float32), slot_flat, precision=lax.Precisi...]
    reshape x1 -> x0, local copies, waits for them, and re-layouts: 1.33 us -> none  [per_device(): slot_keys = picked.reshape(query_count, slot_count, DH)]
where the time goes in v12:
time: 128 us
  Pallas kernels  41.2 us (32%)
  waiting for transfers between devices  39.6 us (31%)
  starting transfers between devices  16.9 us (13%)
  local copies, waits for them, and re-layouts  14.7 us (11%)
  other arithmetic  12.3 us (10%)
  between operations  2.67 us (2%)
    pallas_call x1, Pallas kernels, score_blocks(): pl.pallas_call(score_kernel, grid=(nblk,), in_specs=[blk(BS, H * DH), blk...  31.7 us
    all_to_all x1, waiting for transfers between devices, per_device(): lax.all_to_all(outbound.reshape(ctx_count, capacity, BS * DH), 'ctx', spl...  23.9 us
    ppermute x5, waiting for transfers between devices, butterfly_sum(): value = value + lax.ppermute(value, axes, pairs)  11.2 us
    pallas_call x1, Pallas kernels, normed_query_rows(): pl.pallas_call(query_kernel, grid=(nblk,), in_specs=[blk(BS, H * DH)], ou...  9.56 us
    all_to_all x1, starting transfers between devices, per_device(): lax.all_to_all(request_table, 'ctx', split_axis=0, concat_axis=0, tiled=T...  6.33 us
    all_to_all x1, starting transfers between devices, per_device(): lax.all_to_all(sent_keys, 'ctx', split_axis=0, concat_axis=0, tiled=True)  3.91 us
    all_to_all x1, starting transfers between devices, per_device(): lax.all_to_all(outbound.reshape(ctx_count, capacity, BS * DH), 'ctx', spl...  3.56 us
    all_to_all x1, waiting for transfers between devices, per_device(): lax.all_to_all(sent_keys, 'ctx', split_axis=0, concat_axis=0, tiled=True)  3.29 us
  transfers between devices with their start and end apart: 8, of which 8 were waited for; matrix products, arithmetic and copies ran while one was open for 9% of the time, Pallas kernels for 7%

profile of v12, /device:TPU:0, one launch (start us, length us, event | category | flops | bytes accessed | tf_op | source)
XLA Modules:
  0.0 127.9 jit_solution(2592628411154846856)
XLA Ops:
  0.6 0.7 multiply_bitcast_fusion
  1.3 0.7 compare_and_fusion
  2.9 0.7 sub.60
  3.5 6.3 %all-to-all-start = ((s32[8,1,4]{2,1,0:T(1,128)}), s32[8,1,4]{2,1,0:T(1,128)S(1)}, u32[]{:S(2)}, u32[]{:S(2)}) async-start(s32[8,1,4]{2,1,0:T(1,128)} %bitcast), calls=%async_computation | async-start | bytes 8192 | tf_op jit(solution)/shard_map/all_to_all | solution.py:242
  9.9 1.1 convert_reduce_fusion
  11.0 1.3 %multiply_reduce_fusion.2 = f32[1024]{0:T(1024)S(1)} fusion(bf16[1,1024,128]{2,1,0:T(8,128)(2,1)} %param.8, f32[1024]{0:T(1024)S(1)} %broadcast_multiply_fusion.2), kind=kLoop, calls=%fused_computation.9 | loop fusion | flops 523264 | bytes 270336 | tf_op jit(solution)/shard_map/reduce_sum | solution.py:27
  12.7 1.3 %add_convert_fusion = bf16[16,64,128]{2,1,0:T(8,128)(2,1)S(1)} fusion(f32[128]{0:T(128)} %param.13, f32[128]{0:T(128)} %param.12, f32[16,64]{1,0:T(8,128)S(1)} %rsqrt.13, f32[16,64]{1,0:T(8,128)S(1)} %div.38, bf16[16,64,128]{2,1,0:T(8,128)(2,1)} %bitcast.40), kind=kLoop, calls=%fused_computation.8 | loop fusion | flops 786432 | bytes 533504 | tf_op jit(solution)/shard_map/convert_element_type | solution.py:30
  14.2 1.2 all-to-all-done
  15.6 1.4 %gather_fusion = bf16[32,64,128]{2,1,0:T(8,128)(2,1)} fusion(bf16[16,64,128]{2,1,0:T(8,128)(2,1)S(1)} %add_convert_fusion, s32[1024]{0:T(1024)S(1)} %pad_clamp_fusion.2), kind=kCustom, calls=%fused_computation | custom fusion | bytes 1048704 | tf_op jit(solution)/shard_map/gather | solution.py:243
  17.0 3.9 %all-to-all-start.1 = ((bf16[8,4,64,128]{3,2,1,0:T(8,128)(2,1)}), bf16[8,4,64,128]{3,2,1,0:T(8,128)(2,1)S(1)}, u32[]{:S(2)}, u32[]{:S(2)}) async-start(bf16[8,4,64,128]{3,2,1,0:T(8,128)(2,1)} %bitcast.5), calls=%async_computation.1 | async-start | bytes 1048576 | tf_op jit(solution)/shard_map/all_to_all | solution.py:244
  21.4 0.7 copy.40
  22.2 9.6 %shard_map.118 = (bf16[2,2048,128]{2,1,0:T(8,128)(2,1)}, bf16[2,128,2048]{2,1,0:T(8,128)(2,1)}) custom-call(bf16[2,64,4096]{2,1,0:T(8,128)(2,1)} %bitcast.44), custom_call_target="tpu_custom_call" | custom-call | flops 2097152 | bytes 3145728 | tf_op jit(solution)/shard_map/pallas_call | solution.py:58
  33.0 3.3 %all-to-all-done.1 = bf16[8,4,64,128]{3,2,1,0:T(8,128)(2,1)S(1)} async-done(((bf16[8,4,64,128]{3,2,1,0:T(8,128)(2,1)}), bf16[8,4,64,128]{3,2,1,0:T(8,128)(2,1)S(1)}, u32[]{:S(2)}, u32[]{:S(2)}) %all-to-all-start.1) | async-done | bytes 524320 | tf_op jit(solution)/shard_map/all_to_all | solution.py:244
  36.3 1.7 %gather_fusion.1 = bf16[64,64,128]{2,1,0:T(8,128)(2,1)} fusion(bf16[32,64,128]{2,1,0:T(8,128)(2,1)S(1)} %bitcast.41, s32[1024]{0:T(1024)S(1)} %pad_clamp_fusion.1), kind=kCustom, calls=%fused_computation.1 | custom fusion | bytes 2097408 | tf_op jit(solution)/shard_map/gather | solution.py:245
  38.0 31.7 %shard_map.119 = (f32[2,64,4096]{2,1,0:T(8,128)}, f32[2,64,32]{2,1,0:T(8,128)}, f32[2,128,2048]{2,1,0:T(8,128)}, f32[2,64,1]{2,1,0:T(8,128)}) custom-call(bf16[2,64,4096]{2,1,0:T(8,128)(2,1)} %bitcast.45, bf16[2,2048,128]{2,1,0:T(8,128)(2,1)} %get-tuple-element.12.qr_ref, bf16[2,128,2048]{2,1,0:T(8,128)(2,1)} %get-tuple-element.13.qt_ref, ...), custom_call_target="tpu_custom_call" | custom-call | flops 8589934592 | bytes 8388608 | tf_op jit(solution)/shard_map/pallas_call | solution.py:174
  69.6 2.9 %copy.42 = f32[2,2048,128]{2,1,0:T(8,128)} copy(f32[2,2048,128]{1,2,0:T(8,128)} %bitcast.42) | data formatting | bytes 4194304 | tf_op jit(solution)/shard_map/transpose | solution.py:264
  72.5 1.7 %reshape.443 = f32[64,8192]{1,0:T(8,128)S(1)} reshape(f32[2,2048,128]{2,1,0:T(8,128)} %copy.42) | data formatting | bytes 4194304 | tf_op jit(solution)/shard_map/reshape | solution.py:265
  74.3 0.9 gather_fusion.2
  75.5 1.3 %broadcast_select_fusion = f32[8,4,8192]{2,1,0:T(4,128)} fusion(f32[8,4,8192]{2,1,0:T(4,128)S(1)} %gather.14, pred[8,4]{1,0:T(8,128)(4,1)S(1)} %broadcast_in_dim.75), kind=kLoop, calls=%fused_computation.7 | loop fusion | flops 262144 | bytes 2097184 | tf_op jit(solution)/shard_map/jit(_where)/select_n | solution.py:269
  76.8 3.6 %all-to-all-start.2 = ((f32[8,4,8192]{2,1,0:T(4,128)}), f32[8,4,8192]{2,1,0:T(4,128)S(1)}, u32[]{:S(2)}, u32[]{:S(2)}) async-start(f32[8,4,8192]{2,1,0:T(4,128)} %broadcast_select_fusion), calls=%async_computation.2 | async-start | bytes 2097152 | tf_op jit(solution)/shard_map/all_to_all | solution.py:270
  80.9 0.7 reduce.4
  82.2 0.6 compare_select_fusion.3
  82.9 23.9 %all-to-all-done.2 = f32[8,4,8192]{2,1,0:T(4,128)S(1)} async-done(((f32[8,4,8192]{2,1,0:T(4,128)}), f32[8,4,8192]{2,1,0:T(4,128)S(1)}, u32[]{:S(2)}, u32[]{:S(2)}) %all-to-all-start.2) | async-done | bytes 1048608 | tf_op jit(solution)/shard_map/all_to_all | solution.py:270
  108.6 1.1 collective-permute-done
  109.8 3.6 %collective-permute-done.1 = f32[260]{0:T(512)S(1)} collective-permute-done((f32[260]{0:T(512)S(1)}, f32[260]{0:T(512)S(1)}, u32[]{:S(2)}, u32[]{:S(2)}) %collective-permute-start.1) | collective-permute-done | bytes 1072 | tf_op jit(solution)/shard_map/ppermute | solution.py:209
  113.4 0.7 copy.43
  114.1 3.8 %collective-permute-done.2 = f32[260]{0:T(512)S(1)} collective-permute-done((f32[260]{0:T(512)S(1)}, f32[260]{0:T(512)S(1)}, u32[]{:S(2)}, u32[]{:S(2)}) %collective-permute-start.2) | collective-permute-done | bytes 1072 | tf_op jit(solution)/shard_map/ppermute | solution.py:209
  117.8 1.5 %collective-permute-start.3 = (f32[260]{0:T(512)S(1)}, f32[260]{0:T(512)S(1)}, u32[]{:S(2)}, u32[]{:S(2)}) collective-permute-start(f32[260]{0:T(512)S(1)} %add.215), channel_id=1, source_target_pairs={{0,8},{1,9},{2,10},{3,11},{4,12},{5,13},{6,14},{7,15},{8,0},{9,1},... | collective-permute-start | bytes 3128 | tf_op jit(solution)/shard_map/ppermute | solution.py:209
  119.4 2.0 %collective-permute-done.3 = f32[260]{0:T(512)S(1)} collective-permute-done((f32[260]{0:T(512)S(1)}, f32[260]{0:T(512)S(1)}, u32[]{:S(2)}, u32[]{:S(2)}) %collective-permute-start.3) | collective-permute-done | bytes 1072 | tf_op jit(solution)/shard_map/ppermute | solution.py:209
  121.4 1.5 %collective-permute-start.4 = (f32[260]{0:T(512)S(1)}, f32[260]{0:T(512)S(1)}, u32[]{:S(2)}, u32[]{:S(2)}) collective-permute-start(f32[260]{0:T(512)S(1)} %add.216), channel_id=1, source_target_pairs={{0,16},{1,17},{2,18},{3,19},{4,20},{5,21},{6,22},{7,23},{8,24},{9,... | collective-permute-start | bytes 3128 | tf_op jit(solution)/shard_map/ppermute | solution.py:209
  122.9 1.4 %subtract_multiply_fusion = f32[1,1024,128]{2,1,0:T(8,128)} fusion(f32[1,1024,128]{2,1,0:T(8,128)S(1)} %reshape.448, bf16[1,1024,128]{2,1,0:T(8,128)(2,1)S(1)} %copy-done, f32[1024]{0:T(1024)S(1)} %get-tuple-element.64, f32[1024]{0:T(1024)S(1)} %add_rsqrt_fusion, f32[1024]{0:T(1024)S(1)} %broadcast_multiply_fusion.2, f32[1024]{0:T(1024)S(1)} %get-tuple-element.65, ...), kind=kLoop, calls=%fused_computation.4 | loop fusion | flops 1048576 | bytes 1327616 | tf_op jit(solution)/shard_map/mul | solution.py:283
  124.3 0.7 collective-permute-done.4
  (68 shorter events, 7.8 us)
Async XLA Ops:
  0.6 20.7 %copy-start.3 = (bf16[1,128,32]{1,2,0:T(8,128)(2,1)S(1)}, bf16[1,128,32]{1,2,0:T(8,128)(2,1)}, u32[]{:S(2)}) copy-start(bf16[1,128,32]{1,2,0:T(8,128)(2,1)} %param.9) | copy-start | bytes 24580
  3.5 11.8 %all-to-all-start = ((s32[8,1,4]{2,1,0:T(1,128)}), s32[8,1,4]{2,1,0:T(1,128)S(1)}, u32[]{:S(2)}, u32[]{:S(2)}) async-start(s32[8,1,4]{2,1,0:T(1,128)} %bitcast), calls=%async_computation | async-start | bytes 8192 | tf_op jit(solution)/shard_map/all_to_all | solution.py:242
  17.0 19.3 %all-to-all-start.1 = ((bf16[8,4,64,128]{3,2,1,0:T(8,128)(2,1)}), bf16[8,4,64,128]{3,2,1,0:T(8,128)(2,1)S(1)}, u32[]{:S(2)}, u32[]{:S(2)}) async-start(bf16[8,4,64,128]{3,2,1,0:T(8,128)(2,1)} %bitcast.5), calls=%async_computation.1 | async-start | bytes 1048576 | tf_op jit(solution)/shard_map/all_to_all | solution.py:244
  75.5 6.1 %copy-start.2 = (f32[2,64,1]{2,1,0:T(8,128)S(1)}, f32[2,64,1]{2,1,0:T(8,128)}, u32[]{:S(2)}) copy-start(f32[2,64,1]{2,1,0:T(8,128)} %get-tuple-element.15) | copy-start | bytes 1540
  76.8 30.1 %all-to-all-start.2 = ((f32[8,4,8192]{2,1,0:T(4,128)}), f32[8,4,8192]{2,1,0:T(4,128)S(1)}, u32[]{:S(2)}, u32[]{:S(2)}) async-start(f32[8,4,8192]{2,1,0:T(4,128)} %broadcast_select_fusion), calls=%async_computation.2 | async-start | bytes 2097152 | tf_op jit(solution)/shard_map/all_to_all | solution.py:270
  82.9 24.9 %copy-start = (bf16[1,1024,128]{2,1,0:T(8,128)(2,1)S(1)}, bf16[1,1024,128]{2,1,0:T(8,128)(2,1)}, u32[]{:S(2)}) copy-start(bf16[1,1024,128]{2,1,0:T(8,128)(2,1)} %param.8) | copy-start | bytes 786436
  82.9 24.9 %copy-start.4 = (f32[128]{0:T(128)S(1)}, f32[128]{0:T(128)}, u32[]{:S(2)}) copy-start(f32[128]{0:T(128)} %param.12) | copy-start | bytes 1540
  107.2 6.2 %copy-start.1 = (f32[2,64,32]{2,1,0:T(8,128)S(1)}, f32[2,64,32]{2,1,0:T(8,128)}, u32[]{:S(2)}) copy-start(f32[2,64,32]{2,1,0:T(8,128)} %get-tuple-element.17) | copy-start | bytes 49156
  108.5 1.2 collective-permute-start
  109.7 3.6 %collective-permute-start.1 = (f32[260]{0:T(512)S(1)}, f32[260]{0:T(512)S(1)}, u32[]{:S(2)}, u32[]{:S(2)}) collective-permute-start(f32[260]{0:T(512)S(1)} %fusion.12), channel_id=1, source_target_pairs={{0,2},{1,3},{2,0},{3,1},{4,6},{5,7},{6,4},{7,5},{8,10},{9,11},{10,... | collective-permute-start | bytes 3128 | tf_op jit(solution)/shard_map/ppermute | solution.py:209
  113.4 4.5 %collective-permute-start.2 = (f32[260]{0:T(512)S(1)}, f32[260]{0:T(512)S(1)}, u32[]{:S(2)}, u32[]{:S(2)}) collective-permute-start(f32[260]{0:T(512)S(1)} %add.214), channel_id=1, source_target_pairs={{0,4},{1,5},{2,6},{3,7},{4,0},{5,1},{6,2},{7,3},{8,12},{9,13},{10,... | collective-permute-start | bytes 3128 | tf_op jit(solution)/shard_map/ppermute | solution.py:209
  117.8 3.6 %collective-permute-start.3 = (f32[260]{0:T(512)S(1)}, f32[260]{0:T(512)S(1)}, u32[]{:S(2)}, u32[]{:S(2)}) collective-permute-start(f32[260]{0:T(512)S(1)} %add.215), channel_id=1, source_target_pairs={{0,8},{1,9},{2,10},{3,11},{4,12},{5,13},{6,14},{7,15},{8,0},{9,1},... | collective-permute-start | bytes 3128 | tf_op jit(solution)/shard_map/ppermute | solution.py:209
  121.4 3.6 %collective-permute-start.4 = (f32[260]{0:T(512)S(1)}, f32[260]{0:T(512)S(1)}, u32[]{:S(2)}, u32[]{:S(2)}) collective-permute-start(f32[260]{0:T(512)S(1)} %add.216), channel_id=1, source_target_pairs={{0,16},{1,17},{2,18},{3,19},{4,20},{5,21},{6,22},{7,23},{8,24},{9,... | collective-permute-start | bytes 3128 | tf_op jit(solution)/shard_map/ppermute | solution.py:209

commit v13 on v12

--- a/solution.py
+++ b/solution.py
@@ -265,8 +265,7 @@
     slot_flat = grad_slots.reshape(request_count, BS * DH)
     request_iota = jnp.arange(request_count, dtype=jnp.int32)[:, None]
     source_request = jnp.sum(jnp.where(placement, request_iota, 0), 0)
-    slot_used = jnp.any(placement, 0)
-    outbound = jnp.where(slot_used[:, None], slot_flat[source_request], 0.0)
+    outbound = slot_flat[source_request]
     returned = lax.all_to_all(
         outbound.reshape(ctx_count, capacity, BS * DH), "ctx", split_axis=0, concat_axis=0, tiled=True
     )

time: 128 us -> 128 us (level)
  other arithmetic: 12.3 us -> 10.9 us
    reshape x0 -> x1, local copies, waits for them, and re-layouts: none -> 1.29 us  [per_device(): outbound.reshape(ctx_count, capacity, BS * DH)]
where the time goes in v13:
time: 128 us
  Pallas kernels  41.2 us (32%)
  waiting for transfers between devices  39.9 us (31%)
  starting transfers between devices  16.8 us (13%)
  local copies, waits for them, and re-layouts  15.6 us (12%)
  other arithmetic  10.9 us (9%)
  between operations  2.67 us (2%)
    pallas_call x1, Pallas kernels, score_blocks(): pl.pallas_call(score_kernel, grid=(nblk,), in_specs=[blk(BS, H * DH), blk...  31.7 us
    all_to_all x1, waiting for transfers between devices, per_device(): lax.all_to_all(outbound.reshape(ctx_count, capacity, BS * DH), 'ctx', spl...  23.9 us
    ppermute x5, waiting for transfers between devices, butterfly_sum(): value = value + lax.ppermute(value, axes, pairs)  11.2 us
    pallas_call x1, Pallas kernels, normed_query_rows(): pl.pallas_call(query_kernel, grid=(nblk,), in_specs=[blk(BS, H * DH)], ou...  9.55 us
    all_to_all x1, starting transfers between devices, per_device(): lax.all_to_all(request_table, 'ctx', split_axis=0, concat_axis=0, tiled=T...  6.33 us
    all_to_all x1, starting transfers between devices, per_device(): lax.all_to_all(sent_keys, 'ctx', split_axis=0, concat_axis=0, tiled=True)  3.8 us
    all_to_all x1, starting transfers between devices, per_device(): lax.all_to_all(outbound.reshape(ctx_count, capacity, BS * DH), 'ctx', spl...  3.56 us
    all_to_all x1, waiting for transfers between devices, per_device(): lax.all_to_all(sent_keys, 'ctx', split_axis=0, concat_axis=0, tiled=True)  3.38 us
  transfers between devices with their start and end apart: 8, of which 8 were waited for; matrix products, arithmetic and copies ran while one was open for 9% of the time, Pallas kernels for 7%

profile of v13, /device:TPU:0, one launch (start us, length us, event | category | flops | bytes accessed | tf_op | source)
XLA Modules:
  0.0 127.5 jit_solution(14655996051347203606)
XLA Ops:
  0.6 0.7 multiply_bitcast_fusion
  1.3 0.7 compare_and_fusion
  2.9 0.7 sub.60
  3.5 6.3 %all-to-all-start = ((s32[8,1,4]{2,1,0:T(1,128)}), s32[8,1,4]{2,1,0:T(1,128)S(1)}, u32[]{:S(2)}, u32[]{:S(2)}) async-start(s32[8,1,4]{2,1,0:T(1,128)} %bitcast), calls=%async_computation | async-start | bytes 8192 | tf_op jit(solution)/shard_map/all_to_all | solution.py:242
  9.9 1.1 convert_reduce_fusion
  11.0 1.3 %multiply_reduce_fusion.2 = f32[1024]{0:T(1024)S(1)} fusion(bf16[1,1024,128]{2,1,0:T(8,128)(2,1)} %param.8, f32[1024]{0:T(1024)S(1)} %broadcast_multiply_fusion.2), kind=kLoop, calls=%fused_computation.8 | loop fusion | flops 523264 | bytes 270336 | tf_op jit(solution)/shard_map/reduce_sum | solution.py:27
  12.7 1.3 %add_convert_fusion = bf16[16,64,128]{2,1,0:T(8,128)(2,1)S(1)} fusion(f32[128]{0:T(128)} %param.13, f32[128]{0:T(128)} %param.12, f32[16,64]{1,0:T(8,128)S(1)} %rsqrt.13, f32[16,64]{1,0:T(8,128)S(1)} %div.38, bf16[16,64,128]{2,1,0:T(8,128)(2,1)} %bitcast.40), kind=kLoop, calls=%fused_computation.7 | loop fusion | flops 786432 | bytes 533504 | tf_op jit(solution)/shard_map/convert_element_type | solution.py:30
  14.0 1.3 %all-to-all-done = s32[8,1,4]{2,1,0:T(1,128)S(1)} async-done(((s32[8,1,4]{2,1,0:T(1,128)}), s32[8,1,4]{2,1,0:T(1,128)S(1)}, u32[]{:S(2)}, u32[]{:S(2)}) %all-to-all-start) | async-done | bytes 160 | tf_op jit(solution)/shard_map/all_to_all | solution.py:242
  15.6 1.4 %gather_fusion = bf16[32,64,128]{2,1,0:T(8,128)(2,1)} fusion(bf16[16,64,128]{2,1,0:T(8,128)(2,1)S(1)} %add_convert_fusion, s32[1024]{0:T(1024)S(1)} %pad_clamp_fusion.2), kind=kCustom, calls=%fused_computation | custom fusion | bytes 1048704 | tf_op jit(solution)/shard_map/gather | solution.py:243
  17.0 3.8 %all-to-all-start.1 = ((bf16[8,4,64,128]{3,2,1,0:T(8,128)(2,1)}), bf16[8,4,64,128]{3,2,1,0:T(8,128)(2,1)S(1)}, u32[]{:S(2)}, u32[]{:S(2)}) async-start(bf16[8,4,64,128]{3,2,1,0:T(8,128)(2,1)} %bitcast.5), calls=%async_computation.1 | async-start | bytes 1048576 | tf_op jit(solution)/shard_map/all_to_all | solution.py:244
  21.3 0.7 copy.40
  22.0 9.6 %shard_map.118 = (bf16[2,2048,128]{2,1,0:T(8,128)(2,1)}, bf16[2,128,2048]{2,1,0:T(8,128)(2,1)}) custom-call(bf16[2,64,4096]{2,1,0:T(8,128)(2,1)} %bitcast.44), custom_call_target="tpu_custom_call" | custom-call | flops 2097152 | bytes 3145728 | tf_op jit(solution)/shard_map/pallas_call | solution.py:58
  32.8 3.4 %all-to-all-done.1 = bf16[8,4,64,128]{3,2,1,0:T(8,128)(2,1)S(1)} async-done(((bf16[8,4,64,128]{3,2,1,0:T(8,128)(2,1)}), bf16[8,4,64,128]{3,2,1,0:T(8,128)(2,1)S(1)}, u32[]{:S(2)}, u32[]{:S(2)}) %all-to-all-start.1) | async-done | bytes 524320 | tf_op jit(solution)/shard_map/all_to_all | solution.py:244
  36.2 1.7 %gather_fusion.1 = bf16[64,64,128]{2,1,0:T(8,128)(2,1)} fusion(bf16[32,64,128]{2,1,0:T(8,128)(2,1)S(1)} %bitcast.41, s32[1024]{0:T(1024)S(1)} %pad_clamp_fusion.1), kind=kCustom, calls=%fused_computation.1 | custom fusion | bytes 2097408 | tf_op jit(solution)/shard_map/gather | solution.py:245
  37.8 31.7 %shard_map.119 = (f32[2,64,4096]{2,1,0:T(8,128)}, f32[2,64,32]{2,1,0:T(8,128)}, f32[2,128,2048]{2,1,0:T(8,128)}, f32[2,64,1]{2,1,0:T(8,128)}) custom-call(bf16[2,64,4096]{2,1,0:T(8,128)(2,1)} %bitcast.45, bf16[2,2048,128]{2,1,0:T(8,128)(2,1)} %get-tuple-element.12.qr_ref, bf16[2,128,2048]{2,1,0:T(8,128)(2,1)} %get-tuple-element.13.qt_ref, ...), custom_call_target="tpu_custom_call" | custom-call | flops 8589934592 | bytes 8388608 | tf_op jit(solution)/shard_map/pallas_call | solution.py:174
  69.5 2.9 %copy.42 = f32[2,2048,128]{2,1,0:T(8,128)} copy(f32[2,2048,128]{1,2,0:T(8,128)} %bitcast.42) | data formatting | bytes 4194304 | tf_op jit(solution)/shard_map/transpose | solution.py:264
  72.4 1.7 %reshape.438 = f32[64,8192]{1,0:T(8,128)S(1)} reshape(f32[2,2048,128]{2,1,0:T(8,128)} %copy.42) | data formatting | bytes 4194304 | tf_op jit(solution)/shard_map/reshape | solution.py:265
  74.2 0.9 gather_fusion.2
  75.1 1.3 %reshape.439 = f32[8,4,8192]{2,1,0:T(4,128)} reshape(f32[32,8192]{1,0:T(8,128)S(1)} %gather_fusion.2) | data formatting | bytes 2097152 | tf_op jit(solution)/shard_map/reshape | solution.py:270
  76.4 3.6 %all-to-all-start.2 = ((f32[8,4,8192]{2,1,0:T(4,128)}), f32[8,4,8192]{2,1,0:T(4,128)S(1)}, u32[]{:S(2)}, u32[]{:S(2)}) async-start(f32[8,4,8192]{2,1,0:T(4,128)} %reshape.439), calls=%async_computation.2 | async-start | bytes 2097152 | tf_op jit(solution)/shard_map/all_to_all | solution.py:269
  80.4 0.7 reduce.4
  81.8 0.6 compare_select_fusion.3
  82.5 23.9 %all-to-all-done.2 = f32[8,4,8192]{2,1,0:T(4,128)S(1)} async-done(((f32[8,4,8192]{2,1,0:T(4,128)}), f32[8,4,8192]{2,1,0:T(4,128)S(1)}, u32[]{:S(2)}, u32[]{:S(2)}) %all-to-all-start.2) | async-done | bytes 1048608 | tf_op jit(solution)/shard_map/all_to_all | solution.py:269
  108.2 1.1 collective-permute-done
  109.4 3.6 %collective-permute-done.1 = f32[260]{0:T(512)S(1)} collective-permute-done((f32[260]{0:T(512)S(1)}, f32[260]{0:T(512)S(1)}, u32[]{:S(2)}, u32[]{:S(2)}) %collective-permute-start.1) | collective-permute-done | bytes 1072 | tf_op jit(solution)/shard_map/ppermute | solution.py:209
  113.0 0.7 copy.43
  113.6 3.8 %collective-permute-done.2 = f32[260]{0:T(512)S(1)} collective-permute-done((f32[260]{0:T(512)S(1)}, f32[260]{0:T(512)S(1)}, u32[]{:S(2)}, u32[]{:S(2)}) %collective-permute-start.2) | collective-permute-done | bytes 1072 | tf_op jit(solution)/shard_map/ppermute | solution.py:209
  117.4 1.5 %collective-permute-start.3 = (f32[260]{0:T(512)S(1)}, f32[260]{0:T(512)S(1)}, u32[]{:S(2)}, u32[]{:S(2)}) collective-permute-start(f32[260]{0:T(512)S(1)} %add.215), channel_id=1, source_target_pairs={{0,8},{1,9},{2,10},{3,11},{4,12},{5,13},{6,14},{7,15},{8,0},{9,1},... | collective-permute-start | bytes 3128 | tf_op jit(solution)/shard_map/ppermute | solution.py:209
  119.0 2.0 %collective-permute-done.3 = f32[260]{0:T(512)S(1)} collective-permute-done((f32[260]{0:T(512)S(1)}, f32[260]{0:T(512)S(1)}, u32[]{:S(2)}, u32[]{:S(2)}) %collective-permute-start.3) | collective-permute-done | bytes 1072 | tf_op jit(solution)/shard_map/ppermute | solution.py:209
  121.0 1.5 %collective-permute-start.4 = (f32[260]{0:T(512)S(1)}, f32[260]{0:T(512)S(1)}, u32[]{:S(2)}, u32[]{:S(2)}) collective-permute-start(f32[260]{0:T(512)S(1)} %add.216), channel_id=1, source_target_pairs={{0,16},{1,17},{2,18},{3,19},{4,20},{5,21},{6,22},{7,23},{8,24},{9,... | collective-permute-start | bytes 3128 | tf_op jit(solution)/shard_map/ppermute | solution.py:209
  122.5 1.4 %subtract_multiply_fusion = f32[1,1024,128]{2,1,0:T(8,128)} fusion(f32[1,1024,128]{2,1,0:T(8,128)S(1)} %reshape.444, bf16[1,1024,128]{2,1,0:T(8,128)(2,1)S(1)} %copy-done, f32[1024]{0:T(1024)S(1)} %get-tuple-element.64, f32[1024]{0:T(1024)S(1)} %add_rsqrt_fusion, f32[1024]{0:T(1024)S(1)} %broadcast_multiply_fusion.2, f32[1024]{0:T(1024)S(1)} %get-tuple-element.65, ...), kind=kLoop, calls=%fused_computation.4 | loop fusion | flops 1048576 | bytes 1327616 | tf_op jit(solution)/shard_map/mul | solution.py:282
  123.9 0.7 collective-permute-done.4
  (65 shorter events, 7.3 us)
Async XLA Ops:
  0.6 20.6 %copy-start.3 = (bf16[1,128,32]{1,2,0:T(8,128)(2,1)S(1)}, bf16[1,128,32]{1,2,0:T(8,128)(2,1)}, u32[]{:S(2)}) copy-start(bf16[1,128,32]{1,2,0:T(8,128)(2,1)} %param.9) | copy-start | bytes 24580
  3.5 11.8 %all-to-all-start = ((s32[8,1,4]{2,1,0:T(1,128)}), s32[8,1,4]{2,1,0:T(1,128)S(1)}, u32[]{:S(2)}, u32[]{:S(2)}) async-start(s32[8,1,4]{2,1,0:T(1,128)} %bitcast), calls=%async_computation | async-start | bytes 8192 | tf_op jit(solution)/shard_map/all_to_all | solution.py:242
  17.0 19.2 %all-to-all-start.1 = ((bf16[8,4,64,128]{3,2,1,0:T(8,128)(2,1)}), bf16[8,4,64,128]{3,2,1,0:T(8,128)(2,1)S(1)}, u32[]{:S(2)}, u32[]{:S(2)}) async-start(bf16[8,4,64,128]{3,2,1,0:T(8,128)(2,1)} %bitcast.5), calls=%async_computation.1 | async-start | bytes 1048576 | tf_op jit(solution)/shard_map/all_to_all | solution.py:244
  75.1 6.1 %copy-start.2 = (f32[2,64,1]{2,1,0:T(8,128)S(1)}, f32[2,64,1]{2,1,0:T(8,128)}, u32[]{:S(2)}) copy-start(f32[2,64,1]{2,1,0:T(8,128)} %get-tuple-element.15) | copy-start | bytes 1540
  76.4 30.1 %all-to-all-start.2 = ((f32[8,4,8192]{2,1,0:T(4,128)}), f32[8,4,8192]{2,1,0:T(4,128)S(1)}, u32[]{:S(2)}, u32[]{:S(2)}) async-start(f32[8,4,8192]{2,1,0:T(4,128)} %reshape.439), calls=%async_computation.2 | async-start | bytes 2097152 | tf_op jit(solution)/shard_map/all_to_all | solution.py:269
  82.5 24.9 %copy-start = (bf16[1,1024,128]{2,1,0:T(8,128)(2,1)S(1)}, bf16[1,1024,128]{2,1,0:T(8,128)(2,1)}, u32[]{:S(2)}) copy-start(bf16[1,1024,128]{2,1,0:T(8,128)(2,1)} %param.8) | copy-start | bytes 786436
  82.5 24.9 %copy-start.4 = (f32[128]{0:T(128)S(1)}, f32[128]{0:T(128)}, u32[]{:S(2)}) copy-start(f32[128]{0:T(128)} %param.12) | copy-start | bytes 1540
  106.8 6.2 %copy-start.1 = (f32[2,64,32]{2,1,0:T(8,128)S(1)}, f32[2,64,32]{2,1,0:T(8,128)}, u32[]{:S(2)}) copy-start(f32[2,64,32]{2,1,0:T(8,128)} %get-tuple-element.17) | copy-start | bytes 49156
  108.1 1.2 collective-permute-start
  109.3 3.6 %collective-permute-start.1 = (f32[260]{0:T(512)S(1)}, f32[260]{0:T(512)S(1)}, u32[]{:S(2)}, u32[]{:S(2)}) collective-permute-start(f32[260]{0:T(512)S(1)} %fusion.11), channel_id=1, source_target_pairs={{0,2},{1,3},{2,0},{3,1},{4,6},{5,7},{6,4},{7,5},{8,10},{9,11},{10,... | collective-permute-start | bytes 3128 | tf_op jit(solution)/shard_map/ppermute | solution.py:209
  113.0 4.5 %collective-permute-start.2 = (f32[260]{0:T(512)S(1)}, f32[260]{0:T(512)S(1)}, u32[]{:S(2)}, u32[]{:S(2)}) collective-permute-start(f32[260]{0:T(512)S(1)} %add.214), channel_id=1, source_target_pairs={{0,4},{1,5},{2,6},{3,7},{4,0},{5,1},{6,2},{7,3},{8,12},{9,13},{10,... | collective-permute-start | bytes 3128 | tf_op jit(solution)/shard_map/ppermute | solution.py:209
  117.4 3.6 %collective-permute-start.3 = (f32[260]{0:T(512)S(1)}, f32[260]{0:T(512)S(1)}, u32[]{:S(2)}, u32[]{:S(2)}) collective-permute-start(f32[260]{0:T(512)S(1)} %add.215), channel_id=1, source_target_pairs={{0,8},{1,9},{2,10},{3,11},{4,12},{5,13},{6,14},{7,15},{8,0},{9,1},... | collective-permute-start | bytes 3128 | tf_op jit(solution)/shard_map/ppermute | solution.py:209
  121.0 3.6 %collective-permute-start.4 = (f32[260]{0:T(512)S(1)}, f32[260]{0:T(512)S(1)}, u32[]{:S(2)}, u32[]{:S(2)}) collective-permute-start(f32[260]{0:T(512)S(1)} %add.216), channel_id=1, source_target_pairs={{0,16},{1,17},{2,18},{3,19},{4,20},{5,21},{6,22},{7,23},{8,24},{9,... | collective-permute-start | bytes 3128 | tf_op jit(solution)/shard_map/ppermute | solution.py:209

commit v14 on v13

--- a/solution.py
+++ b/solution.py
@@ -72,7 +72,7 @@
 
 
 def score_kernel(q_ref, qr_ref, qt_ref, k_ref, w_ref, mass_ref, spos_ref, qpos_ref,
-                 gq_ref, wg_ref, sgt_ref, div_ref, mix_ref, mg_ref, sp_ref):
+                 gq_ref, wg_ref, sgo_ref, div_ref, mix_ref, mg_ref, sp_ref, sgt_ref):
     f32 = jnp.float32
     inv_root = DH ** (-0.5)
     rows = HEAD_GROUP * BS
@@ -158,7 +158,7 @@
         return carry
 
     lax.fori_loop(0, groups, second_pass, 0)
-    sgt_ref[...] = sgt_ref[...] * inv_root
+    sgo_ref[...] = (sgt_ref[...] * inv_root).T
 
 
 def score_blocks(q, qr, qt, k, w, mass, spos, qpos):
@@ -178,15 +178,16 @@
             blk(BS, H * DH), blk(nrows, DH), blk(DH, nrows), blk(slots, DH),
             blk(BS, H), blk(BS, slots), blk(1, slots), blk(BS, 1),
         ],
-        out_specs=[blk(BS, H * DH), blk(BS, H), blk(DH, slots), blk(BS, 1)],
+        out_specs=[blk(BS, H * DH), blk(BS, H), blk(slots, DH), blk(BS, 1)],
         out_shape=[
             jax.ShapeDtypeStruct((nblk, BS, H * DH), f32),
             jax.ShapeDtypeStruct((nblk, BS, H), f32),
-            jax.ShapeDtypeStruct((nblk, DH, slots), f32),
+            jax.ShapeDtypeStruct((nblk, slots, DH), f32),
             jax.ShapeDtypeStruct((nblk, BS, 1), f32),
         ],
         scratch_shapes=[
-            pltpu.VMEM((BS, slots), f32), pltpu.VMEM((BS, slots), f32), pltpu.VMEM((nrows, slots), f32)
+            pltpu.VMEM((BS, slots), f32), pltpu.VMEM((BS, slots), f32), pltpu.VMEM((nrows, slots), f32),
+            pltpu.VMEM((DH, slots), f32),
         ],
         compiler_params=pltpu.CompilerParams(
             dimension_semantics=("arbitrary",), vmem_limit_bytes=60 * 1024 * 1024
@@ -261,7 +262,7 @@
         head_weights[0].reshape(query_count, BS, H), mass_rows, slot_limit, query_pos
     )
     divergence_total = jnp.sum(div_rows)
-    grad_slots = slot_grad_t.transpose(0, 2, 1)
+    grad_slots = slot_grad_t
     slot_flat = grad_slots.reshape(request_count, BS * DH)
     request_iota = jnp.arange(request_count, dtype=jnp.int32)[:, None]
     source_request = jnp.sum(jnp.where(placement, request_iota, 0), 0)

time: 128 us -> 125 us (0.977)
  local copies, waits for them, and re-layouts: 15.6 us -> 12.7 us
    transpose x1 -> x0, local copies, waits for them, and re-layouts: 2.89 us -> none  [per_device(): grad_slots = slot_grad_t.transpose(0, 2, 1)]
  transfers between devices with their start and end apart: 8 -> 8, of which waited for: 8 -> 8; matrix products, arithmetic and copies ran while one was open for 9% -> 9% of each run, Pallas kernels for 7% -> 8%
where the time goes in v14:
time: 125 us
  Pallas kernels  41.4 us (33%)
  waiting for transfers between devices  39.8 us (32%)
  starting transfers between devices  16.8 us (13%)
  local copies, waits for them, and re-layouts  12.7 us (10%)
  other arithmetic  10.9 us (9%)
  between operations  2.67 us (2%)
    pallas_call x1, Pallas kernels, score_blocks(): pl.pallas_call(score_kernel, grid=(nblk,), in_specs=[blk(BS, H * DH), blk...  31.9 us
    all_to_all x1, waiting for transfers between devices, per_device(): lax.all_to_all(outbound.reshape(ctx_count, capacity, BS * DH), 'ctx', spl...  23.9 us
    ppermute x5, waiting for transfers between devices, butterfly_sum(): value = value + lax.ppermute(value, axes, pairs)  11.2 us
    pallas_call x1, Pallas kernels, normed_query_rows(): pl.pallas_call(query_kernel, grid=(nblk,), in_specs=[blk(BS, H * DH)], ou...  9.55 us
    all_to_all x1, starting transfers between devices, per_device(): lax.all_to_all(request_table, 'ctx', split_axis=0, concat_axis=0, tiled=T...  6.33 us
    all_to_all x1, starting transfers between devices, per_device(): lax.all_to_all(sent_keys, 'ctx', split_axis=0, concat_axis=0, tiled=True)  3.8 us
    all_to_all x1, starting transfers between devices, per_device(): lax.all_to_all(outbound.reshape(ctx_count, capacity, BS * DH), 'ctx', spl...  3.56 us
    all_to_all x1, waiting for transfers between devices, per_device(): lax.all_to_all(sent_keys, 'ctx', split_axis=0, concat_axis=0, tiled=True)  3.38 us
  transfers between devices with their start and end apart: 8, of which 8 were waited for; matrix products, arithmetic and copies ran while one was open for 9% of the time, Pallas kernels for 8%

profile of v14, /device:TPU:0, one launch (start us, length us, event | category | flops | bytes accessed | tf_op | source)
XLA Modules:
  0.0 124.8 jit_solution(15027410604670856609)
XLA Ops:
  0.6 0.7 multiply_bitcast_fusion
  1.3 0.7 compare_and_fusion
  2.9 0.7 sub.60
  3.5 6.3 %all-to-all-start = ((s32[8,1,4]{2,1,0:T(1,128)}), s32[8,1,4]{2,1,0:T(1,128)S(1)}, u32[]{:S(2)}, u32[]{:S(2)}) async-start(s32[8,1,4]{2,1,0:T(1,128)} %bitcast), calls=%async_computation | async-start | bytes 8192 | tf_op jit(solution)/shard_map/all_to_all | solution.py:243
  9.9 1.1 convert_reduce_fusion
  11.0 1.3 %multiply_reduce_fusion.2 = f32[1024]{0:T(1024)S(1)} fusion(bf16[1,1024,128]{2,1,0:T(8,128)(2,1)} %param.8, f32[1024]{0:T(1024)S(1)} %broadcast_multiply_fusion.2), kind=kLoop, calls=%fused_computation.8 | loop fusion | flops 523264 | bytes 270336 | tf_op jit(solution)/shard_map/reduce_sum | solution.py:27
  12.7 1.3 %add_convert_fusion = bf16[16,64,128]{2,1,0:T(8,128)(2,1)S(1)} fusion(f32[128]{0:T(128)} %param.13, f32[128]{0:T(128)} %param.12, f32[16,64]{1,0:T(8,128)S(1)} %rsqrt.13, f32[16,64]{1,0:T(8,128)S(1)} %div.38, bf16[16,64,128]{2,1,0:T(8,128)(2,1)} %bitcast.39), kind=kLoop, calls=%fused_computation.7 | loop fusion | flops 786432 | bytes 533504 | tf_op jit(solution)/shard_map/convert_element_type | solution.py:30
  14.0 1.3 %all-to-all-done = s32[8,1,4]{2,1,0:T(1,128)S(1)} async-done(((s32[8,1,4]{2,1,0:T(1,128)}), s32[8,1,4]{2,1,0:T(1,128)S(1)}, u32[]{:S(2)}, u32[]{:S(2)}) %all-to-all-start) | async-done | bytes 160 | tf_op jit(solution)/shard_map/all_to_all | solution.py:243
  15.6 1.4 %gather_fusion = bf16[32,64,128]{2,1,0:T(8,128)(2,1)} fusion(bf16[16,64,128]{2,1,0:T(8,128)(2,1)S(1)} %add_convert_fusion, s32[1024]{0:T(1024)S(1)} %pad_clamp_fusion.2), kind=kCustom, calls=%fused_computation | custom fusion | bytes 1048704 | tf_op jit(solution)/shard_map/gather | solution.py:244
  17.0 3.8 %all-to-all-start.1 = ((bf16[8,4,64,128]{3,2,1,0:T(8,128)(2,1)}), bf16[8,4,64,128]{3,2,1,0:T(8,128)(2,1)S(1)}, u32[]{:S(2)}, u32[]{:S(2)}) async-start(bf16[8,4,64,128]{3,2,1,0:T(8,128)(2,1)} %bitcast.5), calls=%async_computation.1 | async-start | bytes 1048576 | tf_op jit(solution)/shard_map/all_to_all | solution.py:245
  21.3 0.7 copy.37
  22.0 9.6 %shard_map.118 = (bf16[2,2048,128]{2,1,0:T(8,128)(2,1)}, bf16[2,128,2048]{2,1,0:T(8,128)(2,1)}) custom-call(bf16[2,64,4096]{2,1,0:T(8,128)(2,1)} %bitcast.42), custom_call_target="tpu_custom_call" | custom-call | flops 2097152 | bytes 3145728 | tf_op jit(solution)/shard_map/pallas_call | solution.py:58
  32.8 3.4 %all-to-all-done.1 = bf16[8,4,64,128]{3,2,1,0:T(8,128)(2,1)S(1)} async-done(((bf16[8,4,64,128]{3,2,1,0:T(8,128)(2,1)}), bf16[8,4,64,128]{3,2,1,0:T(8,128)(2,1)S(1)}, u32[]{:S(2)}, u32[]{:S(2)}) %all-to-all-start.1) | async-done | bytes 524320 | tf_op jit(solution)/shard_map/all_to_all | solution.py:245
  36.2 1.7 %gather_fusion.1 = bf16[64,64,128]{2,1,0:T(8,128)(2,1)} fusion(bf16[32,64,128]{2,1,0:T(8,128)(2,1)S(1)} %bitcast.40, s32[1024]{0:T(1024)S(1)} %pad_clamp_fusion.1), kind=kCustom, calls=%fused_computation.1 | custom fusion | bytes 2097408 | tf_op jit(solution)/shard_map/gather | solution.py:246
  37.8 31.9 %shard_map.119 = (f32[2,64,4096]{2,1,0:T(8,128)}, f32[2,64,32]{2,1,0:T(8,128)}, f32[2,2048,128]{2,1,0:T(8,128)}, f32[2,64,1]{2,1,0:T(8,128)}) custom-call(bf16[2,64,4096]{2,1,0:T(8,128)(2,1)} %bitcast.43, bf16[2,2048,128]{2,1,0:T(8,128)(2,1)} %get-tuple-element.12.qr_ref, bf16[2,128,2048]{2,1,0:T(8,128)(2,1)} %get-tuple-element.13.qt_ref, ...), custom_call_target="tpu_custom_call" | custom-call | flops 8589934592 | bytes 8388608 | tf_op jit(solution)/shard_map/pallas_call | solution.py:174
  69.7 1.8 %reshape.438 = f32[64,8192]{1,0:T(8,128)S(1)} reshape(f32[2,2048,128]{2,1,0:T(8,128)} %get-tuple-element.14) | data formatting | bytes 4194304 | tf_op jit(solution)/shard_map/reshape | solution.py:266
  71.5 0.9 gather_fusion.2
  72.4 1.3 %reshape.439 = f32[8,4,8192]{2,1,0:T(4,128)} reshape(f32[32,8192]{1,0:T(8,128)S(1)} %gather_fusion.2) | data formatting | bytes 2097152 | tf_op jit(solution)/shard_map/reshape | solution.py:271
  73.7 3.6 %all-to-all-start.2 = ((f32[8,4,8192]{2,1,0:T(4,128)}), f32[8,4,8192]{2,1,0:T(4,128)S(1)}, u32[]{:S(2)}, u32[]{:S(2)}) async-start(f32[8,4,8192]{2,1,0:T(4,128)} %reshape.439), calls=%async_computation.2 | async-start | bytes 2097152 | tf_op jit(solution)/shard_map/all_to_all | solution.py:270
  77.8 0.7 reduce.4
  79.1 0.6 compare_select_fusion.3
  79.8 23.9 %all-to-all-done.2 = f32[8,4,8192]{2,1,0:T(4,128)S(1)} async-done(((f32[8,4,8192]{2,1,0:T(4,128)}), f32[8,4,8192]{2,1,0:T(4,128)S(1)}, u32[]{:S(2)}, u32[]{:S(2)}) %all-to-all-start.2) | async-done | bytes 1048608 | tf_op jit(solution)/shard_map/all_to_all | solution.py:270
  104.7 0.6 multiply_reduce_fusion
  105.5 1.1 collective-permute-done
  106.7 3.6 %collective-permute-done.1 = f32[260]{0:T(512)S(1)} collective-permute-done((f32[260]{0:T(512)S(1)}, f32[260]{0:T(512)S(1)}, u32[]{:S(2)}, u32[]{:S(2)}) %collective-permute-start.1) | collective-permute-done | bytes 1072 | tf_op jit(solution)/shard_map/ppermute | solution.py:210
  110.3 0.7 copy.39
  111.0 3.8 %collective-permute-done.2 = f32[260]{0:T(512)S(1)} collective-permute-done((f32[260]{0:T(512)S(1)}, f32[260]{0:T(512)S(1)}, u32[]{:S(2)}, u32[]{:S(2)}) %collective-permute-start.2) | collective-permute-done | bytes 1072 | tf_op jit(solution)/shard_map/ppermute | solution.py:210
  114.8 1.5 %collective-permute-start.3 = (f32[260]{0:T(512)S(1)}, f32[260]{0:T(512)S(1)}, u32[]{:S(2)}, u32[]{:S(2)}) collective-permute-start(f32[260]{0:T(512)S(1)} %add.215), channel_id=1, source_target_pairs={{0,8},{1,9},{2,10},{3,11},{4,12},{5,13},{6,14},{7,15},{8,0},{9,1},... | collective-permute-start | bytes 3128 | tf_op jit(solution)/shard_map/ppermute | solution.py:210
  116.4 2.0 %collective-permute-done.3 = f32[260]{0:T(512)S(1)} collective-permute-done((f32[260]{0:T(512)S(1)}, f32[260]{0:T(512)S(1)}, u32[]{:S(2)}, u32[]{:S(2)}) %collective-permute-start.3) | collective-permute-done | bytes 1072 | tf_op jit(solution)/shard_map/ppermute | solution.py:210
  118.4 1.5 %collective-permute-start.4 = (f32[260]{0:T(512)S(1)}, f32[260]{0:T(512)S(1)}, u32[]{:S(2)}, u32[]{:S(2)}) collective-permute-start(f32[260]{0:T(512)S(1)} %add.216), channel_id=1, source_target_pairs={{0,16},{1,17},{2,18},{3,19},{4,20},{5,21},{6,22},{7,23},{8,24},{9,... | collective-permute-start | bytes 3128 | tf_op jit(solution)/shard_map/ppermute | solution.py:210
  119.9 1.4 %subtract_multiply_fusion = f32[1,1024,128]{2,1,0:T(8,128)} fusion(f32[1,1024,128]{2,1,0:T(8,128)S(1)} %reshape.444, bf16[1,1024,128]{2,1,0:T(8,128)(2,1)S(1)} %copy-done, f32[1024]{0:T(1024)S(1)} %get-tuple-element.64, f32[1024]{0:T(1024)S(1)} %add_rsqrt_fusion, f32[1024]{0:T(1024)S(1)} %broadcast_multiply_fusion.2, f32[1024]{0:T(1024)S(1)} %get-tuple-element.65, ...), kind=kLoop, calls=%fused_computation.4 | loop fusion | flops 1048576 | bytes 1327616 | tf_op jit(solution)/shard_map/mul | solution.py:283
  121.3 0.7 collective-permute-done.4
  (64 shorter events, 6.7 us)
Async XLA Ops:
  0.6 20.6 %copy-start.3 = (bf16[1,128,32]{1,2,0:T(8,128)(2,1)S(1)}, bf16[1,128,32]{1,2,0:T(8,128)(2,1)}, u32[]{:S(2)}) copy-start(bf16[1,128,32]{1,2,0:T(8,128)(2,1)} %param.9) | copy-start | bytes 24580
  3.5 11.8 %all-to-all-start = ((s32[8,1,4]{2,1,0:T(1,128)}), s32[8,1,4]{2,1,0:T(1,128)S(1)}, u32[]{:S(2)}, u32[]{:S(2)}) async-start(s32[8,1,4]{2,1,0:T(1,128)} %bitcast), calls=%async_computation | async-start | bytes 8192 | tf_op jit(solution)/shard_map/all_to_all | solution.py:243
  17.0 19.2 %all-to-all-start.1 = ((bf16[8,4,64,128]{3,2,1,0:T(8,128)(2,1)}), bf16[8,4,64,128]{3,2,1,0:T(8,128)(2,1)S(1)}, u32[]{:S(2)}, u32[]{:S(2)}) async-start(bf16[8,4,64,128]{3,2,1,0:T(8,128)(2,1)} %bitcast.5), calls=%async_computation.1 | async-start | bytes 1048576 | tf_op jit(solution)/shard_map/all_to_all | solution.py:245
  72.4 6.1 %copy-start.2 = (f32[2,64,1]{2,1,0:T(8,128)S(1)}, f32[2,64,1]{2,1,0:T(8,128)}, u32[]{:S(2)}) copy-start(f32[2,64,1]{2,1,0:T(8,128)} %get-tuple-element.15) | copy-start | bytes 1540
  73.7 30.1 %all-to-all-start.2 = ((f32[8,4,8192]{2,1,0:T(4,128)}), f32[8,4,8192]{2,1,0:T(4,128)S(1)}, u32[]{:S(2)}, u32[]{:S(2)}) async-start(f32[8,4,8192]{2,1,0:T(4,128)} %reshape.439), calls=%async_computation.2 | async-start | bytes 2097152 | tf_op jit(solution)/shard_map/all_to_all | solution.py:270
  79.8 24.9 %copy-start = (bf16[1,1024,128]{2,1,0:T(8,128)(2,1)S(1)}, bf16[1,1024,128]{2,1,0:T(8,128)(2,1)}, u32[]{:S(2)}) copy-start(bf16[1,1024,128]{2,1,0:T(8,128)(2,1)} %param.8) | copy-start | bytes 786436
  79.8 24.9 %copy-start.4 = (f32[128]{0:T(128)S(1)}, f32[128]{0:T(128)}, u32[]{:S(2)}) copy-start(f32[128]{0:T(128)} %param.12) | copy-start | bytes 1540
  104.1 6.2 %copy-start.1 = (f32[2,64,32]{2,1,0:T(8,128)S(1)}, f32[2,64,32]{2,1,0:T(8,128)}, u32[]{:S(2)}) copy-start(f32[2,64,32]{2,1,0:T(8,128)} %get-tuple-element.17) | copy-start | bytes 49156
  105.4 1.2 collective-permute-start
  106.6 3.6 %collective-permute-start.1 = (f32[260]{0:T(512)S(1)}, f32[260]{0:T(512)S(1)}, u32[]{:S(2)}, u32[]{:S(2)}) collective-permute-start(f32[260]{0:T(512)S(1)} %fusion.11), channel_id=1, source_target_pairs={{0,2},{1,3},{2,0},{3,1},{4,6},{5,7},{6,4},{7,5},{8,10},{9,11},{10,... | collective-permute-start | bytes 3128 | tf_op jit(solution)/shard_map/ppermute | solution.py:210
  110.3 4.5 %collective-permute-start.2 = (f32[260]{0:T(512)S(1)}, f32[260]{0:T(512)S(1)}, u32[]{:S(2)}, u32[]{:S(2)}) collective-permute-start(f32[260]{0:T(512)S(1)} %add.214), channel_id=1, source_target_pairs={{0,4},{1,5},{2,6},{3,7},{4,0},{5,1},{6,2},{7,3},{8,12},{9,13},{10,... | collective-permute-start | bytes 3128 | tf_op jit(solution)/shard_map/ppermute | solution.py:210
  114.8 3.6 %collective-permute-start.3 = (f32[260]{0:T(512)S(1)}, f32[260]{0:T(512)S(1)}, u32[]{:S(2)}, u32[]{:S(2)}) collective-permute-start(f32[260]{0:T(512)S(1)} %add.215), channel_id=1, source_target_pairs={{0,8},{1,9},{2,10},{3,11},{4,12},{5,13},{6,14},{7,15},{8,0},{9,1},... | collective-permute-start | bytes 3128 | tf_op jit(solution)/shard_map/ppermute | solution.py:210
  118.4 3.6 %collective-permute-start.4 = (f32[260]{0:T(512)S(1)}, f32[260]{0:T(512)S(1)}, u32[]{:S(2)}, u32[]{:S(2)}) collective-permute-start(f32[260]{0:T(512)S(1)} %add.216), channel_id=1, source_target_pairs={{0,16},{1,17},{2,18},{3,19},{4,20},{5,21},{6,22},{7,23},{8,24},{9,... | collective-permute-start | bytes 3128 | tf_op jit(solution)/shard_map/ppermute | solution.py:210
